TPU v7x, 128 devices: a whole 4x4x4 slice. The times are simulated.
128 devices in a mesh: seq: 32 (over x, z, core), mp: 4 (over y).
Axes of the slice: x: 4, y: 4, z: 4, core: 2. Of those that a mesh axis runs over, the one named last changes fastest.
Arguments:
- hidden: bfloat16 [16384, 4096], P('seq', 'mp'), may hold values from -6 to 6
- w_zx: bfloat16 [4096, 2, 4096], P(None, None, 'mp'), may hold values from -0.09375 to 0.09375
- w_bc: bfloat16 [4096, 2, 512], P(None, None, 'mp'), may hold values from -0.09375 to 0.09375
- w_dt: bfloat16 [4096, 64], P(None, 'mp'), may hold values from -0.09375 to 0.09375
- conv_x: float32 [4, 4096], P(None, 'mp'), may hold values from -3 to 3
- conv_x_bias: float32 [4096], P('mp'), may hold values from -3 to 3
- conv_bc: float32 [4, 2, 512], P(None, None, 'mp'), may hold values from -3 to 3
- conv_bc_bias: float32 [2, 512], P(None, 'mp'), may hold values from -3 to 3
- a_log: float32 [64], P('mp'), may hold values from -9.5 to -0.5
- dt_bias: float32 [64], P('mp'), may hold values from -4 to -1
- d_skip: float32 [64], P('mp'), may hold values from 0.5 to 4
- norm_gain: float32 [4096], P('mp'), may hold values from 0.4 to 1.6
- state_bank: float32 [2, 64, 64, 128], P(None, 'mp'), may hold values from -2 to 2
- conv_bank_x: bfloat16 [2, 3, 4096], P(None, None, 'mp'), may hold values from -5 to 5
- conv_bank_bc: bfloat16 [2, 3, 2, 512], P(None, None, None, 'mp'), may hold values from -5 to 5
- prompt_blocks: int32 [9], replicated, may hold values from 1 to 48, 64 in all
- prompt_order: int32 [9], replicated, may hold values from 0 to 8, each once
- resume_slot: int32 [9], replicated, may hold values from 0 to 2
Outputs:
- mixed: bfloat16 [16384, 4096], P('seq', 'mp')
Inputs may be any that keep to these rules, and one draw needn't show every extreme that they name: `prompt_blocks`: blocks of each prompt; they sum to 64 and the longest is exactly 48. `prompt_order`: A permutation of the prompts. `resume_slot`: 2 means a fresh start from zero state and zero convolution rows.
All inputs are finite; a program needn't handle non-finite values.
Results may differ from a plain program's by a relative error of at most 0.0068.
Values may be sent and summed in bfloat16 or wider, within the bound.
No kernel may reach another device: no remote copies, remote signals or barrier semaphores. Data moves between devices by JAX's collectives and lax.ppermute only.
A program may use at most 192 MiB of HBM per device.

v0:
```python
import jax
import jax.numpy as jnp
from jax import lax
from jax.sharding import PartitionSpec as P

WIDTH = 4096
HEAD_DIM = 64
STATE = 128
BLOCK = 256
KERNEL = 4
BANK = 2


def from_behind(value, axis, steps):
    count = lax.axis_size(axis)
    pairs = [(source, (source + steps) % count) for source in range(count)]
    return lax.ppermute(value, axis, pairs)


def entering(value, axis, join, neutral):
    count, mine = (lax.axis_size(axis), lax.axis_index(axis))
    pieces = jax.tree.map(lambda part: lax.all_gather(part, axis), value)
    total = jax.tree.map(
        lambda part, zero: jnp.full_like(part, 0) + jnp.asarray(zero, part.dtype), value, neutral
    )

    def turn(position, total):
        longer = join(total, jax.tree.map(lambda part: part[position], pieces))
        return jax.tree.map(lambda new, old: jnp.where(position < mine, new, old), longer, total)

    return lax.fori_loop(0, count - 1, turn, total)


def broadcast(block, axis, source):
    block = jnp.where(lax.axis_index(axis) == source, block, jnp.zeros_like(block))
    return lax.psum(block, axis)


def combine(earlier, later):
    return (earlier[0] * later[0], later[0][..., None, None] * earlier[1] + later[1])


def per_device(
    hidden,
    w_zx,
    w_bc,
    w_dt,
    conv_x,
    conv_x_bias,
    conv_bc,
    conv_bc_bias,
    a_log,
    dt_bias,
    d_skip,
    norm_gain,
    state_bank,
    conv_bank_x,
    conv_bank_bc,
    prompt_blocks,
    prompt_order,
    resume_slot,
):
    devices = lax.axis_size("seq")
    place = lax.axis_index("seq")
    rows_dev = hidden.shape[0]
    blocks = rows_dev // BLOCK
    inner_dev = w_zx.shape[2]
    gstate_dev = w_bc.shape[2]
    heads_dev = w_dt.shape[1]
    groups_dev = gstate_dev // STATE
    per_group = heads_dev // groups_dev
    channels = inner_dev + 2 * gstate_dev
    prompts = prompt_blocks.shape[0]
    flat_zx = w_zx.reshape(WIDTH, 2 * inner_dev)
    flat_bc = w_bc.reshape(WIDTH, 2 * gstate_dev)
    piece = lax.all_gather(hidden, "mp", axis=1, tiled=True)
    zx_sum = jnp.dot(piece, flat_zx, preferred_element_type=jnp.float32)
    bc_sum = jnp.dot(piece, flat_bc, preferred_element_type=jnp.float32)
    dt_raw = jnp.dot(piece, w_dt, preferred_element_type=jnp.float32)
    zx = zx_sum.astype(jnp.bfloat16)
    bc = bc_sum.astype(jnp.bfloat16)
    gate = zx[:, :inner_dev]
    mixin = jnp.concatenate([zx[:, inner_dev:], bc], axis=1).reshape(blocks, BLOCK, channels)
    own_tails = mixin[:, BLOCK - (KERNEL - 1) :, :]
    arrived = from_behind(own_tails, "seq", 1)
    wrapped = jnp.concatenate([jnp.zeros_like(arrived[:1]), arrived[:-1]], axis=0)
    before = jnp.where(place > 0, arrived, wrapped)
    prompt_ids = jnp.arange(prompts, dtype=jnp.int32)
    order_hot = (prompt_order[:, None] == prompt_ids[None, :]).astype(jnp.int32)
    lengths = jnp.sum(order_hot * prompt_blocks[None, :], axis=1)
    slots = jnp.sum(order_hot * resume_slot[None, :], axis=1)
    ends = jnp.cumsum(lengths)
    starts = ends - lengths
    stream_ids = jnp.arange(blocks, dtype=jnp.int32) * devices + place
    inside = (
        (stream_ids[:, None] >= starts[None, :]) & (stream_ids[:, None] < ends[None, :])
    ).astype(jnp.int32)
    block_slot = jnp.sum(inside * slots[None, :], axis=1)
    first = jnp.any(stream_ids[:, None] == starts[None, :], axis=1)
    pick = (block_slot[:, None] == jnp.arange(BANK, dtype=jnp.int32)[None, :]).astype(jnp.float32)
    bank_state = jnp.einsum("cr,rhpn->chpn", pick, state_bank, precision=lax.Precision.HIGHEST)
    bank_rows = jnp.concatenate(
        [conv_bank_x, conv_bank_bc.reshape(BANK, KERNEL - 1, 2 * gstate_dev)], axis=2
    )
    bank_tail = jnp.einsum("cr,rkz->ckz", pick, bank_rows.astype(jnp.float32)).astype(jnp.bfloat16)
    tail = jnp.where(first[:, None, None], bank_tail, before)
    kernel = jnp.concatenate([conv_x, conv_bc.reshape(KERNEL, 2 * gstate_dev)], axis=1)
    bias = jnp.concatenate([conv_x_bias, conv_bc_bias.reshape(2 * gstate_dev)], axis=0)
    padded = jnp.concatenate([tail, mixin], axis=1).astype(jnp.float32)
    acc = bias[None, None, :] + padded[:, 0:BLOCK] * kernel[0]
    for k in range(1, KERNEL):
        acc = acc + padded[:, k : k + BLOCK] * kernel[k]
    conv = jax.nn.silu(acc).astype(jnp.bfloat16)
    xs = conv[..., :inner_dev].reshape(blocks, BLOCK, groups_dev, per_group, HEAD_DIM)
    bs = conv[..., inner_dev : inner_dev + gstate_dev].reshape(blocks, BLOCK, groups_dev, STATE)
    cq = conv[..., inner_dev + gstate_dev :].reshape(blocks, BLOCK, groups_dev, STATE)
    dt = jax.nn.softplus(dt_raw.reshape(blocks, BLOCK, heads_dev) + dt_bias[None, None, :])
    cum = jnp.cumsum(dt * (-jnp.exp(a_log))[None, None, :], axis=1)
    scores = jnp.einsum("cqgn,ckgn->cgqk", cq, bs, preferred_element_type=jnp.float32)
    cum_h = cum.transpose(0, 2, 1)
    lower = jnp.arange(BLOCK)[:, None] >= jnp.arange(BLOCK)[None, :]
    damp = jnp.exp(
        jnp.where(lower[None, None], cum_h[:, :, :, None] - cum_h[:, :, None, :], -jnp.inf)
    )
    damp = damp.reshape(blocks, groups_dev, per_group, BLOCK, BLOCK)
    dt_h = dt.transpose(0, 2, 1).reshape(blocks, groups_dev, per_group, 1, BLOCK)
    mix = (scores[:, :, None] * damp * dt_h).astype(jnp.bfloat16)
    y_intra = jnp.einsum("cgjqk,ckgjp->cqgjp", mix, xs, preferred_element_type=jnp.float32)
    last = cum[:, -1, :]
    grow = jnp.exp(last)
    factor = (dt * jnp.exp(last[:, None, :] - cum)).reshape(blocks, BLOCK, groups_dev, per_group, 1)
    weighted = (xs.astype(jnp.float32) * factor).astype(jnp.bfloat16)
    local_state = jnp.einsum(
        "cqgjp,cqgn->cgjpn", weighted, bs, preferred_element_type=jnp.float32
    ).reshape(blocks, heads_dev, HEAD_DIM, STATE)
    step_a = jnp.where(first[:, None], 0.0, grow)
    step_b = local_state + jnp.where(
        first[:, None, None, None], grow[:, :, None, None] * bank_state, 0.0
    )
    carry = jnp.zeros((heads_dev, HEAD_DIM, STATE), jnp.float32)
    found = []
    for row in range(blocks):
        own = (step_a[row], step_b[row])
        unit = (jnp.ones_like(own[0]), jnp.zeros_like(own[1]))
        prior_a, prior_b = entering(own, "seq", combine, unit)
        found.append(prior_a[:, None, None] * carry + prior_b)
        whole_a, whole_b = combine((prior_a, prior_b), own)
        carry = broadcast(whole_a[:, None, None] * carry + whole_b, "seq", devices - 1)
    previous = jnp.stack(found, axis=0)
    state_in = jnp.where(first[:, None, None, None], bank_state, previous)
    read = jnp.einsum(
        "cqgn,cgjpn->cqgjp",
        cq.astype(jnp.float32),
        state_in.reshape(blocks, groups_dev, per_group, HEAD_DIM, STATE),
        precision=lax.Precision.HIGHEST,
    )
    growth = jnp.exp(cum).reshape(blocks, BLOCK, groups_dev, per_group, 1)
    skip = d_skip.reshape(1, 1, groups_dev, per_group, 1)
    y_total = y_intra + growth * read + skip * xs.astype(jnp.float32)
    gated = y_total.reshape(rows_dev, inner_dev) * jax.nn.silu(gate.astype(jnp.float32))
    grouped = gated.reshape(rows_dev, groups_dev, inner_dev // groups_dev)
    scale = lax.rsqrt(jnp.mean(grouped * grouped, axis=2, keepdims=True) + 1e-05)
    result = (grouped * scale).reshape(rows_dev, inner_dev) * norm_gain[None, :]
    return result.astype(jnp.bfloat16)


def solution(mesh):
    placed = (
        P("seq", "mp"),
        P(None, None, "mp"),
        P(None, None, "mp"),
        P(None, "mp"),
        P(None, "mp"),
        P("mp"),
        P(None, None, "mp"),
        P(None, "mp"),
        P("mp"),
        P("mp"),
        P("mp"),
        P("mp"),
        P(None, "mp", None, None),
        P(None, None, "mp"),
        P(None, None, None, "mp"),
        P(),
        P(),
        P(),
    )
    return jax.shard_map(
        per_device, mesh=mesh, in_specs=placed, out_specs=P("seq", "mp"), check_vma=False
    )
```

profile of v0, /device:TPU:0, one launch (start us, length us, event | category | flops | bytes accessed | tf_op | source)
XLA Modules:
  0.0 372.5 jit_solution(10664198602085482660)
XLA Ops:
  7.4 17.2 %copy.108 = bf16[512,8,2,1024]{3,1,2,0:T(8,128)(2,1)} copy(bf16[512,8,2,1024]{3,2,1,0:T(2,128)(2,1)} %bitcast.135) | data formatting | bytes 33554432
  26.1 2.5 fusion.29
  28.6 31.1 %all-gather.6.cloned.1.call-done = bf16[512,4096]{1,0:T(8,128)(2,1)} async-done(((bf16[512,1024]{1,0:T(8,128)(2,1)}), bf16[512,4096]{1,0:T(8,128)(2,1)}) %all-gather.6.cloned.1.call-update) | async-done | bytes 4194320 | tf_op jit(solution)/shard_map/all_gather | solution.py:76
  59.7 15.7 %convolution_convert_fusion = bf16[512,2048]{1,0:T(8,128)(2,1)S(1)} fusion(bf16[512,4096]{1,0:T(8,128)(2,1)} %all-gather.6.cloned.1.call-done, bf16[4096,2048]{1,0:T(8,128)(2,1)} %bitcast.136), kind=kOutput, calls=%fused_computation.18 | convolution fusion | flops 8590983168 | bytes 23068672 | tf_op jit(solution)/shard_map/dot_general | solution.py:77
  75.6 2.2 copy-done.27
  77.9 1.3 fusion.22
  80.1 1.2 fusion.54
  84.3 1.8 collective-permute-done
  86.6 1.7 multiply_convert_fusion.2
  89.4 1.6 slice_convert_fusion
  91.7 1.5 convolution_add_fusion
  95.2 20.0 %all-gather = f32[32,1,16]{2,1,0:T(1,128)S(1)} all-gather(f32[1,1,16]{2,1,0:T(1,128)S(1)} %get-tuple-element.318), channel_id=1, replica_groups=mesh['seq'=32,'mp'=4] {'seq'}, dimensions={0}, use_global_device_ids=true | all-gather | bytes 2112 | tf_op jit(solution)/shard_map/all_gather | solution.py:22
  115.2 20.5 %all-gather.1 = f32[32,1,16]{2,1,0:T(1,128)S(1)} all-gather(f32[1,1,16]{2,1,0:T(1,128)S(1)} %get-tuple-element.317), channel_id=1, replica_groups=mesh['seq'=32,'mp'=4] {'seq'}, dimensions={0}, use_global_device_ids=true | all-gather | bytes 2112 | tf_op jit(solution)/shard_map/all_gather | solution.py:22
  135.7 3.0 copy.95
  138.7 2.0 fusion.36
  140.7 25.7 %all-gather.8.cloned.1.call-done = f32[32,16,64,128]{3,2,1,0:T(8,128)} async-done(((f32[1,16,64,128]{3,2,1,0:T(8,128)}), f32[32,16,64,128]{3,2,1,0:T(8,128)}) %all-gather.8.cloned.1.call-update) | async-done | bytes 16777232 | tf_op jit(solution)/shard_map/all_gather | solution.py:22
  166.4 38.3 %while.32 = (s32[]{:T(128)}, f32[16]{0:T(128)S(1)}, f32[16,64,128]{2,1,0:T(8,128)S(1)}, s32[]{:T(128)}, f32[32,16]{1,0:T(8,128)S(1)}, /*index=5*/f32[32,16,64,128]{3,2,1,0:T(8,128)}, s32[]{:T(128)}, s32[]{:T(128)}) while((s32[]{:T(128)}, f32[16]{0:T(128)S(1)}, f32[16,64,128]{2,1,0:T(8,128)S(1)}, s32[]{:T(128)}, ...), condition=%wide.region_8.9_spmd.clone, body=%wide.region_7.8_spmd.clone.sunk | while | flops 524340 | bytes 1573299 | solution.py:31
  167.7 1.2 fusion.63
  168.9 1.2 fusion.63
  171.3 1.2 fusion.63
  172.5 1.2 fusion.63
  176.2 1.2 fusion.63
  177.4 1.2 fusion.63
  178.7 1.3 fusion.63
  180.0 1.2 fusion.63
  183.7 1.2 fusion.63
  184.9 1.2 fusion.63
  188.6 1.2 fusion.63
  189.8 1.2 fusion.63
  191.1 1.2 fusion.63
  192.3 1.2 fusion.63
  195.9 1.2 fusion.63
  199.6 1.2 fusion.63
  200.8 1.3 fusion.63
  202.2 1.3 fusion.63
  203.5 1.2 fusion.63
  205.9 34.8 %all-gather.10.cloned.1.call-done = f32[32,16,64,128]{3,2,1,0:T(8,128)} async-done(((f32[1,16,64,128]{3,2,1,0:T(8,128)}), f32[32,16,64,128]{3,2,1,0:T(8,128)}) %all-gather.10.cloned.1.call-update) | async-done | bytes 16777232 | tf_op jit(solution)/shard_map/all_gather | solution.py:22
  240.7 37.9 %while.33 = (s32[]{:T(128)}, f32[16]{0:T(128)S(1)}, f32[16,64,128]{2,1,0:T(8,128)S(1)}, s32[]{:T(128)}, f32[32,16]{1,0:T(8,128)S(1)}, /*index=5*/f32[32,16,64,128]{3,2,1,0:T(8,128)}, s32[]{:T(128)}, s32[]{:T(128)}) while((s32[]{:T(128)}, f32[16]{0:T(128)S(1)}, f32[16,64,128]{2,1,0:T(8,128)S(1)}, s32[]{:T(128)}, ...), condition=%wide.region_10.11_spmd.clone, body=%wide.region_9.10_spmd.clone.sunk | while | flops 524340 | bytes 1573299 | solution.py:31
  240.8 1.2 fusion.64
  243.3 1.2 fusion.64
  246.9 1.2 fusion.64
  250.6 1.2 fusion.64
  251.8 1.2 fusion.64
  255.5 1.2 fusion.64
  256.7 1.2 fusion.64
  257.9 1.2 fusion.64
  259.2 1.2 fusion.64
  260.4 1.2 fusion.64
  261.6 1.2 fusion.64
  262.8 1.2 fusion.64
  264.0 1.2 fusion.64
  265.3 1.2 fusion.64
  267.7 1.2 fusion.64
  268.9 1.2 fusion.64
  270.2 1.2 fusion.64
  271.4 1.2 fusion.64
  273.8 1.2 fusion.64
  278.7 69.0 %all-reduce.3.cloned.1.call-done = f32[16,64,128]{2,1,0:T(8,128)} async-done(((f32[16,64,128]{2,1,0:T(8,128)}), f32[16,64,128]{2,1,0:T(8,128)}) %all-reduce.3.cloned.1.call-update) | async-done | bytes 524304 | tf_op jit(solution)/shard_map/psum | solution.py:36
  350.1 2.1 fusion.25
  352.2 2.6 fusion.21
  354.8 3.8 %copy.102 = f32[2,256,1,16,64]{4,3,1,0,2:T(8,128)} copy(f32[2,256,1,16,64]{1,4,3,0,2:T(8,128)S(1)} %fusion.21) | data formatting | bytes 4194304 | tf_op jit(solution)/shard_map/reshape | solution.py:160
  358.6 3.5 reshape.236
  362.1 2.1 multiply_reduce_fusion
  364.2 1.7 multiply_convert_fusion.3
  (198 shorter events, 43.1 us)
Async XLA Ops:
  6.5 19.6 %copy-start = (f32[2,16,64,128]{3,2,1,0:T(8,128)S(1)}, f32[2,16,64,128]{3,2,1,0:T(8,128)}, u32[]{:S(2)}) copy-start(f32[2,16,64,128]{3,2,1,0:T(8,128)} %param.34) | copy-start | bytes 3145732
  6.5 53.2 %all-gather.6.cloned.1.call-start = ((), (), s32[]{:S(2)}) async-start(), calls=%async_computation | async-start | bytes 5242880 | tf_op jit(solution)/shard_map/all_gather | solution.py:76
  7.3 159.2 %all-gather.8.cloned.1.call-start = ((), (), s32[]{:S(2)}) async-start(), calls=%async_computation.1 | async-start | bytes 17301504 | tf_op jit(solution)/shard_map/all_gather | solution.py:22
  7.3 17.3 %copy-start.24 = (s32[9]{0:T(128)S(1)}, s32[9]{0:T(128)}, u32[]{:S(2)}) copy-start(s32[9]{0:T(128)} %param.37) | copy-start | bytes 112
  7.3 17.2 %copy-start.25 = (s32[9]{0:T(128)S(1)}, s32[9]{0:T(128)}, u32[]{:S(2)}) copy-start(s32[9]{0:T(128)} %param.38) | copy-start | bytes 112
  7.3 17.2 %copy-start.26 = (s32[9]{0:T(128)S(1)}, s32[9]{0:T(128)}, u32[]{:S(2)}) copy-start(s32[9]{0:T(128)} %param.39) | copy-start | bytes 112
  7.3 17.6 %copy-start.18 = (bf16[2,3,2,128]{3,2,1,0:T(2,128)(2,1)S(1)}, bf16[2,3,2,128]{3,2,1,0:T(2,128)(2,1)}, u32[]{:S(2)}) copy-start(bf16[2,3,2,128]{3,2,1,0:T(2,128)(2,1)} %param.36) | copy-start | bytes 9220
  7.3 18.2 %copy-start.16 = (f32[1024]{0:T(1024)S(1)}, f32[1024]{0:T(1024)}, u32[]{:S(2)}) copy-start(f32[1024]{0:T(1024)} %param.27) | copy-start | bytes 12292
  7.4 18.2 %copy-start.23 = (f32[2,128]{1,0:T(2,128)S(1)}, f32[2,128]{1,0:T(2,128)}, u32[]{:S(2)}) copy-start(f32[2,128]{1,0:T(2,128)} %param.29) | copy-start | bytes 3076
  7.4 18.2 %copy-start.13 = (f32[4,1024]{1,0:T(4,128)S(1)}, f32[4,1024]{1,0:T(4,128)}, u32[]{:S(2)}) copy-start(f32[4,1024]{1,0:T(4,128)} %param.26) | copy-start | bytes 49156
  7.4 18.6 %copy-start.17 = (f32[4,2,128]{2,1,0:T(2,128)S(1)}, f32[4,2,128]{2,1,0:T(2,128)}, u32[]{:S(2)}) copy-start(f32[4,2,128]{2,1,0:T(2,128)} %param.28) | copy-start | bytes 12292
  7.4 18.7 %copy-start.29 = (f32[16]{0:T(128)S(1)}, f32[16]{0:T(128)}, u32[]{:S(2)}) copy-start(f32[16]{0:T(128)} %param.30) | copy-start | bytes 196
  26.0 49.5 %copy-start.21 = (s32[2]{0:T(128)}, s32[2]{0:T(128)S(1)}, u32[]{:S(2)}) copy-start(s32[2]{0:T(128)S(1)} %fusion.45) | copy-start | bytes 28
  59.7 15.9 %copy-start.5 = (bf16[512,4096]{1,0:T(8,128)(2,1)S(1)}, bf16[512,4096]{1,0:T(8,128)(2,1)}, u32[]{:S(2)}) copy-start(bf16[512,4096]{1,0:T(8,128)(2,1)} %all-gather.6.cloned.1.call-done) | copy-start | bytes 12582916
  75.5 3.7 copy-start.3
  75.5 2.4 copy-start.27
  79.2 0.9 copy-start.11
  79.3 1.9 copy-start.20
  79.3 6.8 %copy-start.19 = (bf16[2,3,256]{2,0,1:T(2,128)(2,1)S(1)}, bf16[2,3,256]{2,0,1:T(2,128)(2,1)}, u32[]{:S(2)}) copy-start(bf16[2,3,256]{2,0,1:T(2,128)(2,1)} %reshape.217) | copy-start | bytes 9220
  79.3 6.8 %copy-start.22 = (s32[2]{0:T(128)S(1)}, s32[2]{0:T(128)}, u32[]{:S(2)}) copy-start(s32[2]{0:T(128)} %copy-done.21) | copy-start | bytes 28
  79.3 6.7 %copy-start.28 = (bf16[2,3,1024]{2,0,1:T(2,128)(2,1)S(1)}, bf16[2,3,1024]{2,0,1:T(2,128)(2,1)}, u32[]{:S(2)}) copy-start(bf16[2,3,1024]{2,0,1:T(2,128)(2,1)} %param.35) | copy-start | bytes 36868
  79.4 6.7 %collective-permute-start = (bf16[2,3,1280]{2,0,1:T(2,128)(2,1)S(1)}, bf16[2,3,1280]{2,0,1:T(2,128)(2,1)S(1)}, u32[]{:S(2)}, u32[]{:S(2)}) collective-permute-start(bf16[2,3,1280]{2,0,1:T(2,128)(2,1)S(1)} %copy.104), channel_id=1, source_target_pairs={{0,4},{4,8},{8,12},{12,16},{16,20},{20,24},{24,28},{28,32},{32,36}... | collective-permute-start | bytes 46088 | tf_op jit(solution)/shard_map/ppermute | solution.py:17
  88.3 1.1 copy-start.2
  91.0 0.7 copy-start.15
  91.5 2.8 copy-start.6
  94.4 146.4 %all-gather.10.cloned.1.call-start = ((), (), s32[]{:S(2)}) async-start(), calls=%async_computation.2 | async-start | bytes 17301504 | tf_op jit(solution)/shard_map/all_gather | solution.py:22
  95.1 252.6 %all-reduce.3.cloned.1.call-start = ((), (), s32[]{:S(2)}) async-start(), calls=%async_computation.3 | async-start | bytes 1048576 | tf_op jit(solution)/shard_map/psum | solution.py:36
  240.7 108.1 %copy-start.9 = (f32[16,64,128]{2,1,0:T(8,128)S(1)}, f32[16,64,128]{2,1,0:T(8,128)}, u32[]{:S(2)}) copy-start(f32[16,64,128]{2,1,0:T(8,128)} %get-tuple-element.309) | copy-start | bytes 1572868
  348.9 3.3 copy-start.10
  350.0 2.1 copy-start.7
  350.0 2.1 copy-start.8
  350.1 2.1 copy-start.12
  350.1 2.1 copy-start.30
  362.1 2.1 copy-start.4
  362.1 2.1 copy-start.14
  364.2 1.7 copy-start.1
Sparse Core Ops, SparseCore 0:
  9.0 50.6 all-gather.5
  94.5 71.8 all-gather.7
  168.7 72.0 all-gather.9
  243.8 103.8 all-reduce.2
where the time goes:
time: 377 us; the launch traced here: 372 us
  waiting for transfers between devices  164 us (44%)
  other arithmetic  89 us (24%)
  blocking collectives  40.5 us (11%)
  local copies, waits for them, and re-layouts  34.1 us (9%)
  matrix products  29.1 us (8%)
  between operations  13.8 us (4%)
    select_n x124, other arithmetic, turn(): jnp.where(position < mine, new, old)  74.6 us
    psum x1, waiting for transfers between devices, broadcast(): return lax.psum(block, axis)  69 us
    all_gather x2, waiting for transfers between devices, entering(): pieces = jax.tree.map(lambda part: lax.all_gather(part, axis), value)  60.6 us
    all_gather x2, blocking collectives, entering(): pieces = jax.tree.map(lambda part: lax.all_gather(part, axis), value)  40.5 us
    all_gather x1, waiting for transfers between devices, per_device(): piece = lax.all_gather(hidden, 'mp', axis=1, tiled=True)  31.1 us
    unnamed x66, local copies, waits for them, and re-layouts  21.2 us
    dot_general x1, matrix products, per_device(): zx_sum = jnp.dot(piece, flat_zx, preferred_element_type=jnp.float32)  15.7 us
  transfers between devices with their start and end apart: 5, of which 5 were waited for; matrix products, arithmetic and copies ran while one was open for 28% of the time, Pallas kernels for 0%

commit v1 on v0

--- a/solution.py
+++ b/solution.py
@@ -15,25 +15,6 @@
     count = lax.axis_size(axis)
     pairs = [(source, (source + steps) % count) for source in range(count)]
     return lax.ppermute(value, axis, pairs)
-
-
-def entering(value, axis, join, neutral):
-    count, mine = (lax.axis_size(axis), lax.axis_index(axis))
-    pieces = jax.tree.map(lambda part: lax.all_gather(part, axis), value)
-    total = jax.tree.map(
-        lambda part, zero: jnp.full_like(part, 0) + jnp.asarray(zero, part.dtype), value, neutral
-    )
-
-    def turn(position, total):
-        longer = join(total, jax.tree.map(lambda part: part[position], pieces))
-        return jax.tree.map(lambda new, old: jnp.where(position < mine, new, old), longer, total)
-
-    return lax.fori_loop(0, count - 1, turn, total)
-
-
-def broadcast(block, axis, source):
-    block = jnp.where(lax.axis_index(axis) == source, block, jnp.zeros_like(block))
-    return lax.psum(block, axis)
 
 
 def combine(earlier, later):
@@ -137,16 +118,19 @@
     step_b = local_state + jnp.where(
         first[:, None, None, None], grow[:, :, None, None] * bank_state, 0.0
     )
-    carry = jnp.zeros((heads_dev, HEAD_DIM, STATE), jnp.float32)
-    found = []
-    for row in range(blocks):
-        own = (step_a[row], step_b[row])
-        unit = (jnp.ones_like(own[0]), jnp.zeros_like(own[1]))
-        prior_a, prior_b = entering(own, "seq", combine, unit)
-        found.append(prior_a[:, None, None] * carry + prior_b)
-        whole_a, whole_b = combine((prior_a, prior_b), own)
-        carry = broadcast(whole_a[:, None, None] * carry + whole_b, "seq", devices - 1)
-    previous = jnp.stack(found, axis=0)
+    run_a, run_b = step_a, step_b
+    shift = 1
+    while shift < devices:
+        got_a, got_b = from_behind((run_a, run_b), "seq", shift)
+        late = place >= shift
+        lead_a = jnp.stack([jnp.where(late, got_a[0], 1.0), jnp.where(late, got_a[1], got_a[0])])
+        lead_b = jnp.stack([jnp.where(late, got_b[0], 0.0), jnp.where(late, got_b[1], got_b[0])])
+        run_a, run_b = combine((lead_a, lead_b), (run_a, run_b))
+        shift *= 2
+    top_a, top_b = combine((run_a[0], run_b[0]), (run_a[1], run_b[1]))
+    run_b = jnp.stack([run_b[0], top_b])
+    got_b = from_behind(run_b, "seq", 1)
+    previous = jnp.stack([got_b[0], jnp.where(place >= 1, got_b[1], got_b[0])])
     state_in = jnp.where(first[:, None, None, None], bank_state, previous)
     read = jnp.einsum(
         "cqgn,cgjpn->cqgjp",

time: 377 us -> 311 us (0.82)
  blocking collectives: 40.5 us -> 0 us
  other arithmetic: 89 us -> 51.5 us
  starting transfers between devices: 0.38 us -> 6.63 us
    ppermute x1 -> x12, waiting for transfers between devices: 1.82 us -> 132 us  [from_behind(): return lax.ppermute(value, axis, pairs)]
    psum x1 -> x0, waiting for transfers between devices: 69 us -> none  [broadcast(): return lax.psum(block, axis)]
    select_n x124 -> x11, other arithmetic: 74.6 us -> 14 us  [the longest x5 13.9 us: per_device(): jnp.where(late, got_b[0], 0.0)]
    all_gather x2 -> x0, waiting for transfers between devices: 60.6 us -> none  [entering(): pieces = jax.tree.map(lambda part: lax.all_gather(part, axis), value)]
    all_gather x2 -> x0, blocking collectives: 40.5 us -> none  [entering(): pieces = jax.tree.map(lambda part: lax.all_gather(part, axis), value)]
    add x2 -> x5, other arithmetic: 2.31 us -> 20.3 us  [combine(): later[0][..., None, None] * earlier[1] + later[1]]
    ppermute x1 -> x12, starting transfers between devices: 0.26 us -> 6.63 us  [from_behind(): return lax.ppermute(value, axis, pairs)]
    unnamed x66 -> x84, local copies, waits for them, and re-layouts: 21.2 us -> 19.7 us
  transfers between devices with their start and end apart: 5 -> 13, of which waited for: 5 -> 10; matrix products, arithmetic and copies ran while one was open for 28% -> 10% of each run, Pallas kernels for 0% -> 0%
where the time goes in v1:
time: 311 us; the launch traced here: 305 us
  waiting for transfers between devices  167 us (54%)
  other arithmetic  51.5 us (17%)
  local copies, waits for them, and re-layouts  33.1 us (11%)
  matrix products  32.3 us (10%)
  between operations  14.4 us (5%)
  starting transfers between devices  6.63 us (2%)
    ppermute x12, waiting for transfers between devices, from_behind(): return lax.ppermute(value, axis, pairs)  132 us
    all_gather x1, waiting for transfers between devices, per_device(): piece = lax.all_gather(hidden, 'mp', axis=1, tiled=True)  34.2 us
    add x5, other arithmetic, combine(): later[0][..., None, None] * earlier[1] + later[1]  20.3 us
    unnamed x84, local copies, waits for them, and re-layouts  19.7 us
    select_n x5, other arithmetic, per_device(): jnp.where(late, got_b[0], 0.0)  13.9 us
    dot_general x1, matrix products, per_device(): zx_sum = jnp.dot(piece, flat_zx, preferred_element_type=jnp.float32)  13.8 us
    reshape x2, local copies, waits for them, and re-layouts, per_device(): y_total.reshape(rows_dev, inner_dev) * jax.nn.silu(gate.astype(jnp.float32))  8.35 us
    ppermute x12, starting transfers between devices, from_behind(): return lax.ppermute(value, axis, pairs)  6.63 us
  transfers between devices with their start and end apart: 13, of which 10 were waited for; matrix products, arithmetic and copies ran while one was open for 10% of the time, Pallas kernels for 0%

profile of v1, /device:TPU:0, one launch (start us, length us, event | category | flops | bytes accessed | tf_op | source)
XLA Modules:
  0.0 304.9 jit_solution(6130645228840618886)
XLA Ops:
  6.5 0.7 all-gather.2.cloned.1.call-update
  7.4 17.2 %copy.113 = bf16[512,8,2,1024]{3,1,2,0:T(8,128)(2,1)} copy(bf16[512,8,2,1024]{3,2,1,0:T(2,128)(2,1)} %bitcast.103) | data formatting | bytes 33554432
  24.6 0.2 select_reduce_fusion.1
  24.8 0.2 reduce-window.14
  25.1 0.2 compare_reduce_fusion
  25.2 0.2 fusion.46
  25.5 34.2 %all-gather.2.cloned.1.call-done = bf16[512,4096]{1,0:T(8,128)(2,1)} async-done(((bf16[512,1024]{1,0:T(8,128)(2,1)}), bf16[512,4096]{1,0:T(8,128)(2,1)}) %all-gather.2.cloned.1.call-update) | async-done | bytes 4194320 | tf_op jit(solution)/shard_map/all_gather | solution.py:57
  59.7 3.4 %fusion.55 = f32[512,16]{0,1:T(8,128)S(1)} fusion(bf16[512,4096]{1,0:T(8,128)(2,1)} %all-gather.2.cloned.1.call-done, bf16[4096,16]{0,1:T(8,128)(2,1)S(1)} %copy-done.25), kind=kOutput, calls=%fused_computation.136 | convolution fusion | flops 67108864 | bytes 4358144 | tf_op jit(solution)/shard_map/dot_general | solution.py:60
  63.1 0.1 copy_bitcast_fusion.1
  63.2 1.2 reduce-window.18
  64.4 0.2 slice_reduce_fusion
  64.7 0.2 slice_reduce_fusion.1
  64.8 13.8 %convolution_convert_fusion = bf16[512,2048]{1,0:T(8,128)(2,1)S(1)} fusion(bf16[512,4096]{1,0:T(8,128)(2,1)} %all-gather.2.cloned.1.call-done, bf16[4096,2048]{1,0:T(8,128)(2,1)} %bitcast.104), kind=kOutput, calls=%fused_computation.8 | convolution fusion | flops 8590983168 | bytes 23068672 | tf_op jit(solution)/shard_map/dot_general | solution.py:58
  78.7 1.3 copy-done.19
  80.0 1.0 copy-done.36
  81.0 1.3 fusion.20
  82.3 0.1 pad_maximum_fusion
  82.4 0.6 collective-permute-start
  83.0 0.1 fusion.52
  83.3 6.2 %collective-permute-done = bf16[2,3,1280]{2,0,1:T(2,128)(2,1)S(1)} collective-permute-done((bf16[2,3,1280]{2,0,1:T(2,128)(2,1)S(1)}, bf16[2,3,1280]{2,0,1:T(2,128)(2,1)S(1)}, u32[]{:S(2)}, u32[]{:S(2)}) %collective-permute-start) | collective-permute-done | bytes 15392 | tf_op jit(solution)/shard_map/ppermute | solution.py:17
  89.5 0.2 broadcast_select_fusion.11
  89.7 0.3 maximum_convert_fusion
  90.0 1.7 multiply_convert_fusion.2
  91.7 2.1 slice_convert_fusion
  93.9 2.2 copy.87
  96.1 1.7 fusion.23
  97.8 4.6 %copy_add_fusion = (f32[2,16,64,128]{3,0,2,1:T(2,128)S(1)}, f32[2,16,64,128]{3,0,2,1:T(2,128)}) fusion(f32[2,16,64,128]{3,2,1,0:T(8,128)S(1)} %fusion.23, pred[2]{0:T(512)(128)(4,1)S(1)} %compare_reduce_fusion, f32[2,16]{0,1:T(8,128)S(1)} %copy.97, f32[2,16,64,128]{3,2,1,0:T(8,128)S(1)} %copy-done, s32[2]{0:T(128)S(1)} %fusion.46), kind=kOutput, calls=%fused_computation.52 | convolution fusion | flops 7077892 | bytes 4194442 | tf_op jit(solution)/shard_map/cr,rhpn->chpn/dot_general | solution.py:82
  102.5 17.6 %collective-permute-done.5 = f32[2,16,64,128]{3,0,2,1:T(2,128)} collective-permute-done((f32[2,16,64,128]{3,0,2,1:T(2,128)S(1)}, f32[2,16,64,128]{3,0,2,1:T(2,128)}, u32[]{:S(2)}, u32[]{:S(2)}) %collective-permute-start.5) | collective-permute-done | bytes 1048608 | tf_op jit(solution)/shard_map/ppermute | solution.py:17
  120.1 2.8 broadcast_select_fusion.2
  122.9 2.2 fusion.24
  125.1 16.6 %collective-permute-done.1 = f32[2,16]{1,0:T(2,128)S(1)} collective-permute-done((f32[2,16]{1,0:T(2,128)S(1)}, f32[2,16]{1,0:T(2,128)S(1)}, u32[]{:S(2)}, u32[]{:S(2)}) %collective-permute-start.1) | collective-permute-done | bytes 160 | tf_op jit(solution)/shard_map/ppermute | solution.py:17
  141.8 0.1 copy.95
  141.9 6.5 %collective-permute-done.6 = f32[2,16,64,128]{3,0,2,1:T(2,128)} collective-permute-done((f32[2,16,64,128]{3,0,2,1:T(2,128)}, f32[2,16,64,128]{3,0,2,1:T(2,128)}, u32[]{:S(2)}, u32[]{:S(2)}) %collective-permute-start.6) | collective-permute-done | bytes 1048608 | tf_op jit(solution)/shard_map/ppermute | solution.py:17
  148.3 2.8 broadcast_select_fusion.4
  151.1 2.9 fusion.25
  154.0 0.3 collective-permute-start.2
  154.4 24.8 %collective-permute-done.2 = f32[2,16]{1,0:T(2,128)S(1)} collective-permute-done((f32[2,16]{1,0:T(2,128)S(1)}, f32[2,16]{1,0:T(2,128)S(1)}, u32[]{:S(2)}, u32[]{:S(2)}) %collective-permute-start.2) | collective-permute-done | bytes 160 | tf_op jit(solution)/shard_map/ppermute | solution.py:17
  179.1 0.1 copy.94
  179.2 2.8 broadcast_select_fusion.6
  182.1 4.0 %fusion.26 = f32[2,16,64,128]{3,0,2,1:T(2,128)} fusion(f32[1,16,64,128]{3,0,2,1:T(1,128)S(1)} %get-tuple-element.22, f32[1,16,64,128]{3,0,2,1:T(1,128)S(1)} %get-tuple-element.21, f32[2,16]{0,1:T(8,128)S(1)} %copy.94, f32[1,16,64,128]{3,0,2,1:T(1,128)S(1)} %copy-done.6, f32[1,16,64,128]{3,0,2,1:T(1,128)S(1)} %copy-done.2, f32[2,16]{0,1:T(8,128)S(1)} %copy.95, ...), kind=kLoop, calls=%fused_computation.43 | loop fusion | flops 2359296 | bytes 5243264 | tf_op jit(solution)/shard_map/add | solution.py:21
  186.1 1.6 collective-permute-start.3
  187.6 24.0 %collective-permute-done.3 = f32[2,16]{1,0:T(2,128)S(1)} collective-permute-done((f32[2,16]{1,0:T(2,128)S(1)}, f32[2,16]{1,0:T(2,128)S(1)}, u32[]{:S(2)}, u32[]{:S(2)}) %collective-permute-start.3) | collective-permute-done | bytes 160 | tf_op jit(solution)/shard_map/ppermute | solution.py:17
  211.8 0.3 collective-permute-done.8
  212.1 2.8 broadcast_select_fusion.8
  215.0 5.1 %fusion.27 = f32[2,16,64,128]{3,0,2,1:T(2,128)} fusion(f32[1,16,64,128]{3,0,2,1:T(1,128)S(1)} %get-tuple-element.20, f32[1,16,64,128]{3,0,2,1:T(1,128)S(1)} %get-tuple-element.19, f32[2,16]{0,1:T(8,128)S(1)} %copy.93, f32[1,16,64,128]{3,0,2,1:T(1,128)S(1)} %copy-done.13, f32[1,16,64,128]{3,0,2,1:T(1,128)S(1)} %copy-done.10, f32[2,16]{0,1:T(8,128)S(1)} %copy.94, ...), kind=kLoop, calls=%fused_computation.45 | loop fusion | flops 3145728 | bytes 6291968 | tf_op jit(solution)/shard_map/add | solution.py:21
  220.1 2.9 collective-permute-start.9
  223.0 0.9 collective-permute-start.10
  224.0 21.5 %collective-permute-done.10 = f32[2,16]{1,0:T(2,128)S(1)} collective-permute-done((f32[2,16]{1,0:T(2,128)S(1)}, f32[2,16]{1,0:T(2,128)S(1)}, u32[]{:S(2)}, u32[]{:S(2)}) %collective-permute-start.10) | collective-permute-done | bytes 160 | tf_op jit(solution)/shard_map/ppermute | solution.py:17
  245.6 2.8 broadcast_select_fusion.10
  248.4 6.0 %fusion.28 = f32[2,16,64,128]{3,0,2,1:T(2,128)S(1)} fusion(f32[1,16,64,128]{3,0,2,1:T(1,128)S(1)} %get-tuple-element.18, f32[1,16,64,128]{3,0,2,1:T(1,128)S(1)} %get-tuple-element.17, f32[2,16]{0,1:T(8,128)S(1)} %copy.92, f32[1,16,64,128]{3,0,2,1:T(1,128)} %copy-done.18, f32[1,16,64,128]{3,0,2,1:T(1,128)} %copy-done.17, f32[2,16]{0,1:T(8,128)S(1)} %copy.93, ...), kind=kLoop, calls=%fused_computation.47 | loop fusion | flops 3932160 | bytes 7340672 | tf_op jit(solution)/shard_map/add | solution.py:21
  254.4 1.1 fusion.54
  255.5 2.0 pad_maximum_fusion.1
  257.5 0.2 collective-permute-start.11
  257.8 1.9 copy.100
  259.7 1.3 fusion.37
  260.9 14.7 %collective-permute-done.11 = f32[2,16,64,128]{3,0,2,1:T(2,128)} collective-permute-done((f32[2,16,64,128]{3,0,2,1:T(2,128)}, f32[2,16,64,128]{3,0,2,1:T(2,128)}, u32[]{:S(2)}, u32[]{:S(2)}) %collective-permute-start.11) | collective-permute-done | bytes 1048608 | tf_op jit(solution)/shard_map/ppermute | solution.py:17
  275.6 2.7 fusion.53
  278.3 1.2 maximum_select_fusion
  279.5 2.1 fusion.29
  281.6 4.0 %fusion.19 = f32[2,256,1,16,64]{1,4,3,0,2:T(8,128)} fusion(f32[2,16,64,256]{3,2,1,0:T(8,128)S(1)} %fusion.29, f32[2,256,1,16,64]{1,4,3,0,2:T(8,128)S(1)} %bitcast.109, bf16[2,256,16,64]{1,3,2,0:T(8,128)(2,1)S(1)} %bitcast.108, f32[2,16,256]{2,1,0:T(8,128)S(1)} %get-tuple-element.27, f32[2,16,256]{2,1,0:T(8,128)S(1)} %get-tuple-element.30, ...), kind=kOutput, calls=%fused_computation.30 | convolution fusion | flops 281018368 | bytes 8028224 | tf_op jit(solution)/shard_map/cgjqk,ckgjp->cqgjp/dot_general | solution.py:109
  285.6 4.9 %copy.107 = f32[2,256,1,16,64]{4,3,1,0,2:T(8,128)} copy(f32[2,256,1,16,64]{1,4,3,0,2:T(8,128)} %fusion.19) | data formatting | bytes 4194304 | tf_op jit(solution)/shard_map/reshape | solution.py:144
  290.5 3.5 %reshape.416 = f32[512,1024]{1,0:T(8,128)S(1)} reshape(f32[2,256,1,16,64]{4,3,1,0,2:T(8,128)} %copy.107) | data formatting | bytes 4194304 | tf_op jit(solution)/shard_map/reshape | solution.py:144
  294.0 2.1 multiply_reduce_fusion
  296.1 1.7 multiply_convert_fusion.3
  (122 shorter events, 1.1 us)
Async XLA Ops:
  6.5 91.2 %copy-start = (f32[2,16,64,128]{3,2,1,0:T(8,128)S(1)}, f32[2,16,64,128]{3,2,1,0:T(8,128)}, u32[]{:S(2)}) copy-start(f32[2,16,64,128]{3,2,1,0:T(8,128)} %param.30) | copy-start | bytes 3145732
  6.5 53.2 %all-gather.2.cloned.1.call-start = ((), (), s32[]{:S(2)}) async-start(), calls=%async_computation | async-start | bytes 5242880 | tf_op jit(solution)/shard_map/all_gather | solution.py:57
  7.3 17.3 %copy-start.33 = (s32[9]{0:T(128)S(1)}, s32[9]{0:T(128)}, u32[]{:S(2)}) copy-start(s32[9]{0:T(128)} %param.33) | copy-start | bytes 112
  7.3 17.3 %copy-start.34 = (s32[9]{0:T(128)S(1)}, s32[9]{0:T(128)}, u32[]{:S(2)}) copy-start(s32[9]{0:T(128)} %param.34) | copy-start | bytes 112
  7.3 17.3 %copy-start.35 = (s32[9]{0:T(128)S(1)}, s32[9]{0:T(128)}, u32[]{:S(2)}) copy-start(s32[9]{0:T(128)} %param.35) | copy-start | bytes 112
  7.3 17.7 %copy-start.30 = (bf16[2,3,2,128]{3,2,1,0:T(2,128)(2,1)S(1)}, bf16[2,3,2,128]{3,2,1,0:T(2,128)(2,1)}, u32[]{:S(2)}) copy-start(bf16[2,3,2,128]{3,2,1,0:T(2,128)(2,1)} %param.32) | copy-start | bytes 9220
  7.3 17.7 %copy-start.28 = (f32[1024]{0:T(1024)S(1)}, f32[1024]{0:T(1024)}, u32[]{:S(2)}) copy-start(f32[1024]{0:T(1024)} %param.23) | copy-start | bytes 12292
  7.3 17.7 %copy-start.32 = (f32[2,128]{1,0:T(2,128)S(1)}, f32[2,128]{1,0:T(2,128)}, u32[]{:S(2)}) copy-start(f32[2,128]{1,0:T(2,128)} %param.25) | copy-start | bytes 3076
  7.3 17.7 %copy-start.26 = (f32[4,1024]{1,0:T(4,128)S(1)}, f32[4,1024]{1,0:T(4,128)}, u32[]{:S(2)}) copy-start(f32[4,1024]{1,0:T(4,128)} %param.22) | copy-start | bytes 49156
  7.3 18.1 %copy-start.29 = (f32[4,2,128]{2,1,0:T(2,128)S(1)}, f32[4,2,128]{2,1,0:T(2,128)}, u32[]{:S(2)}) copy-start(f32[4,2,128]{2,1,0:T(2,128)} %param.24) | copy-start | bytes 12292
  7.3 18.2 %copy-start.38 = (f32[16]{0:T(128)S(1)}, f32[16]{0:T(128)}, u32[]{:S(2)}) copy-start(f32[16]{0:T(128)} %param.26) | copy-start | bytes 196
  7.4 52.4 %copy-start.25 = (bf16[4096,16]{0,1:T(8,128)(2,1)S(1)}, bf16[4096,16]{0,1:T(8,128)(2,1)}, u32[]{:S(2)}) copy-start(bf16[4096,16]{0,1:T(8,128)(2,1)} %param.21) | copy-start | bytes 393220
  25.5 37.6 %copy-start.31 = (f32[16]{0:T(128)S(1)}, f32[16]{0:T(128)}, u32[]{:S(2)}) copy-start(f32[16]{0:T(128)} %param.27) | copy-start | bytes 196
  64.8 15.1 %copy-start.21 = (bf16[512,4096]{1,0:T(8,128)(2,1)S(1)}, bf16[512,4096]{1,0:T(8,128)(2,1)}, u32[]{:S(2)}) copy-start(bf16[512,4096]{1,0:T(8,128)(2,1)} %all-gather.2.cloned.1.call-done) | copy-start | bytes 12582916
  78.6 1.4 copy-start.19
  78.6 2.4 copy-start.36
  82.2 7.2 %copy-start.37 = (bf16[2,3,1024]{2,0,1:T(2,128)(2,1)S(1)}, bf16[2,3,1024]{2,0,1:T(2,128)(2,1)}, u32[]{:S(2)}) copy-start(bf16[2,3,1024]{2,0,1:T(2,128)(2,1)} %param.31) | copy-start | bytes 36868
  82.4 7.1 %collective-permute-start = (bf16[2,3,1280]{2,0,1:T(2,128)(2,1)S(1)}, bf16[2,3,1280]{2,0,1:T(2,128)(2,1)S(1)}, u32[]{:S(2)}, u32[]{:S(2)}) collective-permute-start(bf16[2,3,1280]{2,0,1:T(2,128)(2,1)S(1)} %copy.109), channel_id=1, source_target_pairs={{0,4},{4,8},{8,12},{12,16},{16,20},{20,24},{24,28},{28,32},{32,36}... | collective-permute-start | bytes 46088 | tf_op jit(solution)/shard_map/ppermute | solution.py:17
  91.7 4.4 %copy-start.16 = (bf16[2,256,1280]{2,1,0:T(8,128)(2,1)}, bf16[2,256,1280]{2,1,0:T(8,128)(2,1)S(1)}, u32[]{:S(2)}) copy-start(bf16[2,256,1280]{2,1,0:T(8,128)(2,1)S(1)} %multiply_convert_fusion.2) | copy-start | bytes 3932164
  102.4 17.6 %collective-permute-start.5 = (f32[2,16,64,128]{3,0,2,1:T(2,128)S(1)}, f32[2,16,64,128]{3,0,2,1:T(2,128)}, u32[]{:S(2)}, u32[]{:S(2)}) collective-permute-start(f32[2,16,64,128]{3,0,2,1:T(2,128)S(1)} %get-tuple-element.44), channel_id=1, source_target_pairs={{0,4},{4,8},{8,12},{12,16},{16,20},{20,24},{24,28},{28,32},{32,36}... | collective-permute-start | bytes 3145736 | tf_op jit(solution)/shard_map/ppermute | solution.py:17
  125.1 23.2 %collective-permute-start.6 = (f32[2,16,64,128]{3,0,2,1:T(2,128)}, f32[2,16,64,128]{3,0,2,1:T(2,128)}, u32[]{:S(2)}, u32[]{:S(2)}) collective-permute-start(f32[2,16,64,128]{3,0,2,1:T(2,128)} %fusion.24), channel_id=1, source_target_pairs={{0,8},{4,12},{8,16},{12,20},{16,24},{20,28},{24,32},{28,36},{32,40... | collective-permute-start | bytes 3145736 | tf_op jit(solution)/shard_map/ppermute | solution.py:17
  125.1 16.6 %collective-permute-start.1 = (f32[2,16]{1,0:T(2,128)S(1)}, f32[2,16]{1,0:T(2,128)S(1)}, u32[]{:S(2)}, u32[]{:S(2)}) collective-permute-start(f32[2,16]{1,0:T(2,128)S(1)} %get-tuple-element.42), channel_id=1, source_target_pairs={{0,4},{4,8},{8,12},{12,16},{16,20},{20,24},{24,28},{28,32},{32,36}... | collective-permute-start | bytes 392 | tf_op jit(solution)/shard_map/ppermute | solution.py:17
  151.1 2.9 copy-start.1
  151.1 2.9 copy-start.5
  154.0 25.2 %collective-permute-start.7 = (f32[2,16,64,128]{3,0,2,1:T(2,128)}, f32[2,16,64,128]{3,0,2,1:T(2,128)}, u32[]{:S(2)}, u32[]{:S(2)}) collective-permute-start(f32[2,16,64,128]{3,0,2,1:T(2,128)} %fusion.25), channel_id=1, source_target_pairs={{0,16},{4,20},{8,24},{12,28},{16,32},{20,36},{24,40},{28,44},{32,4... | collective-permute-start | bytes 3145736 | tf_op jit(solution)/shard_map/ppermute | solution.py:17
  154.0 25.1 %collective-permute-start.2 = (f32[2,16]{1,0:T(2,128)S(1)}, f32[2,16]{1,0:T(2,128)S(1)}, u32[]{:S(2)}, u32[]{:S(2)}) collective-permute-start(f32[2,16]{1,0:T(2,128)S(1)} %maximum_multiply_fusion.5), channel_id=1, source_target_pairs={{0,8},{4,12},{8,16},{12,20},{16,24},{20,28},{24,32},{28,36},{32,40... | collective-permute-start | bytes 392 | tf_op jit(solution)/shard_map/ppermute | solution.py:17
  179.2 2.8 copy-start.2
  179.2 2.8 copy-start.6
  182.0 4.0 %copy-start.9 = (f32[1,16,64,128]{3,0,2,1:T(1,128)}, f32[1,16,64,128]{3,0,2,1:T(1,128)S(1)}, u32[]{:S(2)}) copy-start(f32[1,16,64,128]{3,0,2,1:T(1,128)S(1)} %get-tuple-element.21) | copy-start | bytes 1572868
  182.0 4.0 %copy-start.12 = (f32[1,16,64,128]{3,0,2,1:T(1,128)}, f32[1,16,64,128]{3,0,2,1:T(1,128)S(1)}, u32[]{:S(2)}) copy-start(f32[1,16,64,128]{3,0,2,1:T(1,128)S(1)} %get-tuple-element.22) | copy-start | bytes 1572868
  186.0 26.0 %collective-permute-start.8 = (f32[2,16,64,128]{3,0,2,1:T(2,128)}, f32[2,16,64,128]{3,0,2,1:T(2,128)}, u32[]{:S(2)}, u32[]{:S(2)}) collective-permute-start(f32[2,16,64,128]{3,0,2,1:T(2,128)} %fusion.26), channel_id=1, source_target_pairs={{0,32},{4,36},{8,40},{12,44},{16,48},{20,52},{24,56},{28,60},{32,6... | collective-permute-start | bytes 3145736 | tf_op jit(solution)/shard_map/ppermute | solution.py:17
  186.1 25.6 %collective-permute-start.3 = (f32[2,16]{1,0:T(2,128)S(1)}, f32[2,16]{1,0:T(2,128)S(1)}, u32[]{:S(2)}, u32[]{:S(2)}) collective-permute-start(f32[2,16]{1,0:T(2,128)S(1)} %maximum_multiply_fusion.6), channel_id=1, source_target_pairs={{0,16},{4,20},{8,24},{12,28},{16,32},{20,36},{24,40},{28,44},{32,4... | collective-permute-start | bytes 392 | tf_op jit(solution)/shard_map/ppermute | solution.py:17
  211.6 11.4 %collective-permute-start.4 = (f32[2,16]{1,0:T(2,128)S(1)}, f32[2,16]{1,0:T(2,128)S(1)}, u32[]{:S(2)}, u32[]{:S(2)}) collective-permute-start(f32[2,16]{1,0:T(2,128)S(1)} %maximum_multiply_fusion.7), channel_id=1, source_target_pairs={{0,32},{4,36},{8,40},{12,44},{16,48},{20,52},{24,56},{28,60},{32,6... | collective-permute-start | bytes 392 | tf_op jit(solution)/shard_map/ppermute | solution.py:17
  211.8 3.1 %copy-start.3 = (f32[1,16,64,128]{3,0,2,1:T(1,128)S(1)}, f32[1,16,64,128]{3,0,2,1:T(1,128)}, u32[]{:S(2)}) copy-start(f32[1,16,64,128]{3,0,2,1:T(1,128)} %copy-done.1) | copy-start | bytes 1572868
  211.8 3.2 %copy-start.7 = (f32[1,16,64,128]{3,0,2,1:T(1,128)S(1)}, f32[1,16,64,128]{3,0,2,1:T(1,128)}, u32[]{:S(2)}) copy-start(f32[1,16,64,128]{3,0,2,1:T(1,128)} %copy-done.5) | copy-start | bytes 1572868
  211.8 3.2 %copy-start.10 = (f32[1,16,64,128]{3,0,2,1:T(1,128)S(1)}, f32[1,16,64,128]{3,0,2,1:T(1,128)}, u32[]{:S(2)}) copy-start(f32[1,16,64,128]{3,0,2,1:T(1,128)} %copy-done.9) | copy-start | bytes 1572868
  211.8 3.2 %copy-start.13 = (f32[1,16,64,128]{3,0,2,1:T(1,128)S(1)}, f32[1,16,64,128]{3,0,2,1:T(1,128)}, u32[]{:S(2)}) copy-start(f32[1,16,64,128]{3,0,2,1:T(1,128)} %copy-done.12) | copy-start | bytes 1572868
  214.9 5.2 %copy-start.17 = (f32[1,16,64,128]{3,0,2,1:T(1,128)}, f32[1,16,64,128]{3,0,2,1:T(1,128)S(1)}, u32[]{:S(2)}) copy-start(f32[1,16,64,128]{3,0,2,1:T(1,128)S(1)} %get-tuple-element.19) | copy-start | bytes 1572868
  214.9 5.1 %copy-start.18 = (f32[1,16,64,128]{3,0,2,1:T(1,128)}, f32[1,16,64,128]{3,0,2,1:T(1,128)S(1)}, u32[]{:S(2)}) copy-start(f32[1,16,64,128]{3,0,2,1:T(1,128)S(1)} %get-tuple-element.20) | copy-start | bytes 1572868
  220.1 25.5 %collective-permute-start.9 = (f32[2,16,64,128]{3,0,2,1:T(2,128)}, f32[2,16,64,128]{3,0,2,1:T(2,128)}, u32[]{:S(2)}, u32[]{:S(2)}) collective-permute-start(f32[2,16,64,128]{3,0,2,1:T(2,128)} %fusion.27), channel_id=1, source_target_pairs={{0,64},{4,68},{8,72},{12,76},{16,80},{20,84},{24,88},{28,92},{32,9... | collective-permute-start | bytes 3145736 | tf_op jit(solution)/shard_map/ppermute | solution.py:17
  223.0 22.5 %collective-permute-start.10 = (f32[2,16]{1,0:T(2,128)S(1)}, f32[2,16]{1,0:T(2,128)S(1)}, u32[]{:S(2)}, u32[]{:S(2)}) collective-permute-start(f32[2,16]{1,0:T(2,128)S(1)} %maximum_multiply_fusion.8), channel_id=1, source_target_pairs={{0,64},{4,68},{8,72},{12,76},{16,80},{20,84},{24,88},{28,92},{32,9... | collective-permute-start | bytes 392 | tf_op jit(solution)/shard_map/ppermute | solution.py:17
  224.0 24.3 %copy-start.4 = (f32[1,16,64,128]{3,0,2,1:T(1,128)S(1)}, f32[1,16,64,128]{3,0,2,1:T(1,128)}, u32[]{:S(2)}) copy-start(f32[1,16,64,128]{3,0,2,1:T(1,128)} %copy-done.1) | copy-start | bytes 1572868
  224.0 24.4 %copy-start.8 = (f32[1,16,64,128]{3,0,2,1:T(1,128)S(1)}, f32[1,16,64,128]{3,0,2,1:T(1,128)}, u32[]{:S(2)}) copy-start(f32[1,16,64,128]{3,0,2,1:T(1,128)} %copy-done.5) | copy-start | bytes 1572868
  224.0 24.4 %copy-start.11 = (f32[1,16,64,128]{3,0,2,1:T(1,128)S(1)}, f32[1,16,64,128]{3,0,2,1:T(1,128)}, u32[]{:S(2)}) copy-start(f32[1,16,64,128]{3,0,2,1:T(1,128)} %copy-done.9) | copy-start | bytes 1572868
  224.0 24.4 %copy-start.14 = (f32[1,16,64,128]{3,0,2,1:T(1,128)S(1)}, f32[1,16,64,128]{3,0,2,1:T(1,128)}, u32[]{:S(2)}) copy-start(f32[1,16,64,128]{3,0,2,1:T(1,128)} %copy-done.12) | copy-start | bytes 1572868
  254.4 3.4 %copy-start.15 = (f32[2,256,1024]{2,1,0:T(8,128)S(1)}, f32[2,256,1024]{2,1,0:T(8,128)}, u32[]{:S(2)}) copy-start(f32[2,256,1024]{2,1,0:T(8,128)} %get-tuple-element.11) | copy-start | bytes 6291460
  257.5 18.1 %collective-permute-start.11 = (f32[2,16,64,128]{3,0,2,1:T(2,128)}, f32[2,16,64,128]{3,0,2,1:T(2,128)}, u32[]{:S(2)}, u32[]{:S(2)}) collective-permute-start(f32[2,16,64,128]{3,0,2,1:T(2,128)} %pad_maximum_fusion.1), channel_id=1, source_target_pairs={{0,4},{4,8},{8,12},{12,16},{16,20},{20,24},{24,28},{28,32},{32,36}... | collective-permute-start | bytes 3145736 | tf_op jit(solution)/shard_map/ppermute | solution.py:17
  259.7 18.6 %copy-start.24 = (f32[2,16,64,128]{3,0,2,1:T(2,128)S(1)}, f32[2,16,64,128]{3,0,2,1:T(2,128)}, u32[]{:S(2)}) copy-start(f32[2,16,64,128]{3,0,2,1:T(2,128)} %get-tuple-element.45) | copy-start | bytes 3145732
  279.5 2.1 copy-start.22
  279.5 2.1 copy-start.23
  279.5 2.1 copy-start.39
  294.0 2.1 copy-start.20
  294.0 2.1 copy-start.27
Sparse Core Ops, SparseCore 0:
  9.0 50.6 all-gather.1

commit v2 on v1

--- a/solution.py
+++ b/solution.py
@@ -118,19 +118,39 @@
     step_b = local_state + jnp.where(
         first[:, None, None, None], grow[:, :, None, None] * bank_state, 0.0
     )
-    run_a, run_b = step_a, step_b
-    shift = 1
-    while shift < devices:
-        got_a, got_b = from_behind((run_a, run_b), "seq", shift)
-        late = place >= shift
+    core = place % 2
+    chip = place // 2
+    chips = devices // 2
+    half = heads_dev // 2
+    keep = lambda part, at: lax.dynamic_slice_in_dim(part, at * half, half, axis=1)
+    pair = [(source, source ^ 1) for source in range(devices)]
+    mine = (keep(step_a, core), keep(step_b, core))
+    got = lax.ppermute((keep(step_a, 1 - core), keep(step_b, 1 - core)), "seq", pair)
+    early = jax.tree.map(lambda own, other: jnp.where(core == 0, own, other), mine, got)
+    later = jax.tree.map(lambda own, other: jnp.where(core == 0, other, own), mine, got)
+    run_a, run_b = combine(early, later)
+    span = 1
+    while span < chips:
+        got_a, got_b = from_behind((run_a, run_b), "seq", 2 * span)
+        late = chip >= span
         lead_a = jnp.stack([jnp.where(late, got_a[0], 1.0), jnp.where(late, got_a[1], got_a[0])])
         lead_b = jnp.stack([jnp.where(late, got_b[0], 0.0), jnp.where(late, got_b[1], got_b[0])])
         run_a, run_b = combine((lead_a, lead_b), (run_a, run_b))
-        shift *= 2
+        span *= 2
     top_a, top_b = combine((run_a[0], run_b[0]), (run_a[1], run_b[1]))
     run_b = jnp.stack([run_b[0], top_b])
-    got_b = from_behind(run_b, "seq", 1)
-    previous = jnp.stack([got_b[0], jnp.where(place >= 1, got_b[1], got_b[0])])
+    got_b = from_behind(run_b, "seq", 2)
+    before_chip = jnp.stack(
+        [jnp.where(chip >= 1, got_b[0], 0.0), jnp.where(chip >= 1, got_b[1], got_b[0])]
+    )
+    after_early = early[0][..., None, None] * before_chip + early[1]
+    own_part = jnp.where(core == 0, before_chip, after_early)
+    other_part = lax.ppermute(jnp.where(core == 0, after_early, before_chip), "seq", pair)
+    previous = jnp.where(
+        core == 0,
+        jnp.concatenate([own_part, other_part], axis=1),
+        jnp.concatenate([other_part, own_part], axis=1),
+    )
     state_in = jnp.where(first[:, None, None, None], bank_state, previous)
     read = jnp.einsum(
         "cqgn,cgjpn->cqgjp",

time: 311 us -> 226 us (0.73); the launches traced: 305 us -> 224 us
  waiting for transfers between devices: 167 us -> 110 us
  other arithmetic: 51.5 us -> 30.2 us
    ppermute x12 -> x10, waiting for transfers between devices: 132 us -> 74.7 us  [from_behind(): return lax.ppermute(value, axis, pairs)]
    add x5, other arithmetic: 20.3 us -> 7.6 us  [combine(): later[0][..., None, None] * earlier[1] + later[1]]
    select_n x5 -> x4, other arithmetic: 13.9 us -> 1.89 us  [per_device(): jnp.where(late, got_b[0], 0.0)]
    select_n x1 -> x2, other arithmetic: 0.07 us -> 4.71 us  [the longest x1 2.94 us: per_device(): own_part = jnp.where(core == 0, before_chip, after_early)]
    unnamed x84 -> x54, local copies, waits for them, and re-layouts: 19.7 us -> 20.9 us
    ppermute x12 -> x10, starting transfers between devices: 6.63 us -> 6.52 us  [from_behind(): return lax.ppermute(value, axis, pairs)]
  transfers between devices with their start and end apart: 13 -> 14, of which waited for: 10 -> 8; matrix products, arithmetic and copies ran while one was open for 10% -> 12% of each run, Pallas kernels for 0% -> 0%
where the time goes in v2:
time: 226 us; the launch traced here: 224 us
  waiting for transfers between devices  110 us (49%)
  local copies, waits for them, and re-layouts  32.7 us (14%)
  other arithmetic  30.2 us (13%)
  matrix products  29.5 us (13%)
  between operations  14.1 us (6%)
  starting transfers between devices  7.09 us (3%)
    ppermute x10, waiting for transfers between devices, from_behind(): return lax.ppermute(value, axis, pairs)  74.7 us
    all_gather x1, waiting for transfers between devices, per_device(): piece = lax.all_gather(hidden, 'mp', axis=1, tiled=True)  33.5 us
    unnamed x54, local copies, waits for them, and re-layouts  20.9 us
    dot_general x1, matrix products, per_device(): zx_sum = jnp.dot(piece, flat_zx, preferred_element_type=jnp.float32)  13.8 us
    add x5, other arithmetic, combine(): later[0][..., None, None] * earlier[1] + later[1]  7.6 us
    reshape x2, local copies, waits for them, and re-layouts, per_device(): y_total.reshape(rows_dev, inner_dev) * jax.nn.silu(gate.astype(jnp.float32))  7.28 us
    ppermute x10, starting transfers between devices, from_behind(): return lax.ppermute(value, axis, pairs)  6.52 us
    dot_general x1, matrix products, per_device(): jnp.einsum('cr,rhpn->chpn', pick, state_bank, precision=lax.Precision.HIG...  4.63 us
  transfers between devices with their start and end apart: 14, of which 8 were waited for; matrix products, arithmetic and copies ran while one was open for 12% of the time, Pallas kernels for 0%

profile of v2, /device:TPU:0, one launch (start us, length us, event | category | flops | bytes accessed | tf_op | source)
XLA Modules:
  0.0 223.7 jit_solution(1854592969196583691)
XLA Ops:
  6.5 0.7 all-gather.2.cloned.1.call-update
  7.3 0.9 select_reduce_fusion.1
  8.1 0.2 reduce-window.14
  8.4 17.3 %copy.117 = bf16[512,8,2,1024]{3,1,2,0:T(8,128)(2,1)} copy(bf16[512,8,2,1024]{3,2,1,0:T(2,128)(2,1)} %bitcast.103) | data formatting | bytes 33554432
  25.8 0.2 compare_reduce_fusion
  26.0 0.2 fusion.48
  26.3 33.5 %all-gather.2.cloned.1.call-done = bf16[512,4096]{1,0:T(8,128)(2,1)} async-done(((bf16[512,1024]{1,0:T(8,128)(2,1)}), bf16[512,4096]{1,0:T(8,128)(2,1)}) %all-gather.2.cloned.1.call-update) | async-done | bytes 4194320 | tf_op jit(solution)/shard_map/all_gather | solution.py:57
  59.7 3.4 %fusion.58 = f32[512,16]{0,1:T(8,128)S(1)} fusion(bf16[512,4096]{1,0:T(8,128)(2,1)} %all-gather.2.cloned.1.call-done, bf16[4096,16]{0,1:T(8,128)(2,1)S(1)} %copy-done.11), kind=kOutput, calls=%fused_computation.143 | convolution fusion | flops 67108864 | bytes 4358144 | tf_op jit(solution)/shard_map/dot_general | solution.py:60
  63.1 0.1 copy_bitcast_fusion.1
  63.2 1.2 reduce-window.18
  64.4 0.2 slice_reduce_fusion
  64.7 0.2 slice_reduce_fusion.1
  64.8 13.8 %convolution_convert_fusion = bf16[512,2048]{1,0:T(8,128)(2,1)S(1)} fusion(bf16[512,4096]{1,0:T(8,128)(2,1)} %all-gather.2.cloned.1.call-done, bf16[4096,2048]{1,0:T(8,128)(2,1)} %bitcast.104), kind=kOutput, calls=%fused_computation.8 | convolution fusion | flops 8590983168 | bytes 23068672 | tf_op jit(solution)/shard_map/dot_general | solution.py:58
  78.6 0.1 slice.166
  78.7 2.2 copy-done.21
  81.0 1.3 fusion.20
  82.3 0.1 pad_maximum_fusion
  82.4 0.3 collective-permute-start
  82.7 0.1 fusion.54
  82.8 0.1 copy.100
  82.9 6.2 %collective-permute-done = bf16[2,3,1280]{2,0,1:T(2,128)(2,1)S(1)} collective-permute-done((bf16[2,3,1280]{2,0,1:T(2,128)(2,1)S(1)}, bf16[2,3,1280]{2,0,1:T(2,128)(2,1)S(1)}, u32[]{:S(2)}, u32[]{:S(2)}) %collective-permute-start) | collective-permute-done | bytes 15392 | tf_op jit(solution)/shard_map/ppermute | solution.py:17
  89.1 0.2 broadcast_select_fusion.11
  89.4 0.3 maximum_convert_fusion
  89.6 1.7 multiply_convert_fusion.2
  91.4 2.1 slice_convert_fusion
  93.5 1.5 copy.90
  95.0 0.4 fusion.23
  95.4 0.2 copy-done.20
  95.6 4.6 %copy_add_fusion = (f32[2,16,64,128]{3,0,2,1:T(2,128)S(1)}, f32[2,16,64,128]{3,0,2,1:T(2,128)}) fusion(f32[2,16,64,128]{3,2,1,0:T(8,128)S(1)} %fusion.23, pred[2]{0:T(512)(128)(4,1)S(1)} %compare_reduce_fusion, f32[2,16]{0,1:T(8,128)S(1)} %copy.100, f32[2,16,64,128]{3,2,1,0:T(8,128)S(1)} %copy-done, s32[2]{0:T(128)S(1)} %copy-done.20), kind=kOutput, calls=%fused_computation.42 | convolution fusion | flops 7077892 | bytes 4194442 | tf_op jit(solution)/shard_map/cr,rhpn->chpn/dot_general | solution.py:82
  100.3 1.0 copy-done.8
  101.4 0.1 collective-permute-start.5
  101.5 0.5 collective-permute-start.1
  102.0 1.3 collective-permute-done.1
  103.4 0.1 copy.99
  103.5 1.6 select_add_fusion
  105.4 17.1 %collective-permute-done.6 = f32[2,8,64,128]{3,0,2,1:T(2,128)S(1)} collective-permute-done((f32[2,8,64,128]{3,0,2,1:T(2,128)S(1)}, f32[2,8,64,128]{3,0,2,1:T(2,128)S(1)}, u32[]{:S(2)}, u32[]{:S(2)}) %collective-permute-start.6) | collective-permute-done | bytes 524320 | tf_op jit(solution)/shard_map/ppermute | solution.py:17
  122.5 0.5 broadcast_select_fusion.9
  123.0 0.6 fusion.30
  123.7 2.1 collective-permute-start.3
  125.8 14.6 %collective-permute-done.3 = f32[2,8]{1,0:T(2,128)S(1)} collective-permute-done((f32[2,8]{1,0:T(2,128)S(1)}, f32[2,8]{1,0:T(2,128)S(1)}, u32[]{:S(2)}, u32[]{:S(2)}) %collective-permute-start.3) | collective-permute-done | bytes 96 | tf_op jit(solution)/shard_map/ppermute | solution.py:17
  140.4 0.5 broadcast_select_fusion.1
  140.9 1.9 fusion.31
  142.9 13.5 %collective-permute-done.4 = f32[2,8]{1,0:T(2,128)S(1)} collective-permute-done((f32[2,8]{1,0:T(2,128)S(1)}, f32[2,8]{1,0:T(2,128)S(1)}, u32[]{:S(2)}, u32[]{:S(2)}) %collective-permute-start.4) | collective-permute-done | bytes 96 | tf_op jit(solution)/shard_map/ppermute | solution.py:17
  156.5 0.3 collective-permute-start.10
  156.9 0.5 broadcast_select_fusion.3
  157.3 1.5 fusion.32
  158.9 3.6 %collective-permute-start.9 = (f32[2,8,64,128]{3,0,2,1:T(2,128)S(1)}, f32[2,8,64,128]{3,0,2,1:T(2,128)S(1)}, u32[]{:S(2)}, u32[]{:S(2)}) collective-permute-start(f32[2,8,64,128]{3,0,2,1:T(2,128)S(1)} %fusion.32), channel_id=1, source_target_pairs={{0,64},{4,68},{8,72},{12,76},{16,80},{20,84},{24,88},{28,92},{32,9... | collective-permute-start | bytes 1572872 | tf_op jit(solution)/shard_map/ppermute | solution.py:17
  162.5 9.3 %collective-permute-done.9 = f32[2,8,64,128]{3,0,2,1:T(2,128)S(1)} collective-permute-done((f32[2,8,64,128]{3,0,2,1:T(2,128)S(1)}, f32[2,8,64,128]{3,0,2,1:T(2,128)S(1)}, u32[]{:S(2)}, u32[]{:S(2)}) %collective-permute-start.9) | collective-permute-done | bytes 524320 | tf_op jit(solution)/shard_map/ppermute | solution.py:17
  171.8 0.5 broadcast_select_fusion.5
  172.2 2.0 fusion.33
  174.3 0.5 fusion.56
  174.8 1.3 pad_maximum_fusion.1
  176.2 14.0 %collective-permute-done.11 = f32[2,8,64,128]{3,0,2,1:T(2,128)} collective-permute-done((f32[2,8,64,128]{3,0,2,1:T(2,128)}, f32[2,8,64,128]{3,0,2,1:T(2,128)}, u32[]{:S(2)}, u32[]{:S(2)}) %collective-permute-start.11) | collective-permute-done | bytes 524320 | tf_op jit(solution)/shard_map/ppermute | solution.py:17
  190.2 1.8 broadcast_select_fusion.7
  192.0 2.9 %fusion.35 = (f32[2,8,64,128]{3,0,2,1:T(2,128)}, f32[2,8,64,128]{3,0,2,1:T(2,128)}) fusion(pred[]{:T(512)S(6)} %eq.59, f32[2,8]{0,1:T(8,128)S(1)} %copy.102, f32[1,8,64,128]{3,0,2,1:T(1,128)S(1)} %get-tuple-element.19, f32[1,8,64,128]{3,0,2,1:T(1,128)S(1)} %get-tuple-element.18, f32[2,8,64,128]{3,0,2,1:T(2,128)} %copy-done.10, ...), kind=kLoop, calls=%fused_computation.58 | loop fusion | flops 786432 | bytes 2621509 | tf_op jit(solution)/shard_map/jit(_where)/select_n | solution.py:147
  195.0 1.8 copy.104
  196.8 1.2 fusion.39
  198.0 3.0 %fusion.24 = f32[2,16,64,128]{3,0,2,1:T(2,128)S(1)} fusion(f32[2,16,64,128]{3,0,2,1:T(2,128)} %get-tuple-element.46, f32[2,8,64,128]{3,0,2,1:T(2,128)} %collective-permute-done.12, f32[2,8,64,128]{3,0,2,1:T(2,128)} %get-tuple-element.14, pred[2]{0:T(512)(128)(4,1)S(1)} %compare_reduce_fusion, pred[]{:T(512)S(6)} %eq.59), kind=kLoop, calls=%fused_computation.39 | loop fusion | flops 1048576 | bytes 3145731 | tf_op jit(solution)/shard_map/jit(_where)/select_n | solution.py:154
  201.0 2.1 fusion.25
  203.1 2.6 %fusion.19 = f32[2,256,1,16,64]{1,4,3,0,2:T(8,128)S(1)} fusion(f32[2,16,64,256]{3,2,1,0:T(8,128)S(1)} %fusion.25, f32[2,256,1,16,64]{1,4,3,0,2:T(8,128)S(1)} %bitcast.109, bf16[2,256,16,64]{1,3,2,0:T(8,128)(2,1)S(1)} %bitcast.108, f32[2,16,256]{2,1,0:T(8,128)S(1)} %get-tuple-element.30, f32[2,16,256]{2,1,0:T(8,128)S(1)} %get-tuple-element.33, ...), kind=kOutput, calls=%fused_computation.30 | convolution fusion | flops 281018368 | bytes 8028224 | tf_op jit(solution)/shard_map/cgjqk,ckgjp->cqgjp/dot_general | solution.py:109
  205.8 3.8 %copy.111 = f32[2,256,1,16,64]{4,3,1,0,2:T(8,128)} copy(f32[2,256,1,16,64]{1,4,3,0,2:T(8,128)S(1)} %fusion.19) | data formatting | bytes 4194304 | tf_op jit(solution)/shard_map/reshape | solution.py:164
  209.5 3.5 %reshape.233 = f32[512,1024]{1,0:T(8,128)S(1)} reshape(f32[2,256,1,16,64]{4,3,1,0,2:T(8,128)} %copy.111) | data formatting | bytes 4194304 | tf_op jit(solution)/shard_map/reshape | solution.py:164
  213.1 2.1 multiply_reduce_fusion
  215.2 1.7 multiply_convert_fusion.3
  (96 shorter events, 1.5 us)
Async XLA Ops:
  6.5 88.9 %copy-start = (f32[2,16,64,128]{3,2,1,0:T(8,128)S(1)}, f32[2,16,64,128]{3,2,1,0:T(8,128)}, u32[]{:S(2)}) copy-start(f32[2,16,64,128]{3,2,1,0:T(8,128)} %param.30) | copy-start | bytes 3145732
  6.5 53.2 %all-gather.2.cloned.1.call-start = ((), (), s32[]{:S(2)}) async-start(), calls=%async_computation | async-start | bytes 5242880 | tf_op jit(solution)/shard_map/all_gather | solution.py:57
  8.3 17.3 %copy-start.16 = (bf16[2,3,2,128]{3,2,1,0:T(2,128)(2,1)S(1)}, bf16[2,3,2,128]{3,2,1,0:T(2,128)(2,1)}, u32[]{:S(2)}) copy-start(bf16[2,3,2,128]{3,2,1,0:T(2,128)(2,1)} %param.32) | copy-start | bytes 9220
  8.3 17.4 %copy-start.14 = (f32[1024]{0:T(1024)S(1)}, f32[1024]{0:T(1024)}, u32[]{:S(2)}) copy-start(f32[1024]{0:T(1024)} %param.23) | copy-start | bytes 12292
  8.3 17.4 %copy-start.18 = (f32[2,128]{1,0:T(2,128)S(1)}, f32[2,128]{1,0:T(2,128)}, u32[]{:S(2)}) copy-start(f32[2,128]{1,0:T(2,128)} %param.25) | copy-start | bytes 3076
  8.3 17.4 %copy-start.12 = (f32[4,1024]{1,0:T(4,128)S(1)}, f32[4,1024]{1,0:T(4,128)}, u32[]{:S(2)}) copy-start(f32[4,1024]{1,0:T(4,128)} %param.22) | copy-start | bytes 49156
  8.3 17.8 %copy-start.15 = (f32[4,2,128]{2,1,0:T(2,128)S(1)}, f32[4,2,128]{2,1,0:T(2,128)}, u32[]{:S(2)}) copy-start(f32[4,2,128]{2,1,0:T(2,128)} %param.24) | copy-start | bytes 12292
  8.4 17.9 %copy-start.23 = (f32[16]{0:T(128)S(1)}, f32[16]{0:T(128)}, u32[]{:S(2)}) copy-start(f32[16]{0:T(128)} %param.26) | copy-start | bytes 196
  8.4 51.4 %copy-start.11 = (bf16[4096,16]{0,1:T(8,128)(2,1)S(1)}, bf16[4096,16]{0,1:T(8,128)(2,1)}, u32[]{:S(2)}) copy-start(bf16[4096,16]{0,1:T(8,128)(2,1)} %param.21) | copy-start | bytes 393220
  26.1 63.0 %copy-start.19 = (s32[2]{0:T(128)}, s32[2]{0:T(128)S(1)}, u32[]{:S(2)}) copy-start(s32[2]{0:T(128)S(1)} %fusion.48) | copy-start | bytes 28
  26.3 36.8 %copy-start.17 = (f32[16]{0:T(128)S(1)}, f32[16]{0:T(128)}, u32[]{:S(2)}) copy-start(f32[16]{0:T(128)} %param.27) | copy-start | bytes 196
  64.8 13.9 %copy-start.5 = (bf16[512,4096]{1,0:T(8,128)(2,1)S(1)}, bf16[512,4096]{1,0:T(8,128)(2,1)}, u32[]{:S(2)}) copy-start(bf16[512,4096]{1,0:T(8,128)(2,1)} %all-gather.2.cloned.1.call-done) | copy-start | bytes 12582916
  78.6 3.8 %copy-start.3 = (bf16[512,2048]{1,0:T(8,128)(2,1)}, bf16[512,2048]{1,0:T(8,128)(2,1)S(1)}, u32[]{:S(2)}) copy-start(bf16[512,2048]{1,0:T(8,128)(2,1)S(1)} %convolution_convert_fusion) | copy-start | bytes 6291460
  78.6 2.4 %copy-start.21 = (bf16[4096,2,128]{2,1,0:T(2,128)(2,1)S(1)}, bf16[4096,2,128]{2,1,0:T(2,128)(2,1)}, u32[]{:S(2)}) copy-start(bf16[4096,2,128]{2,1,0:T(2,128)(2,1)} %param.20) | copy-start | bytes 6291460
  82.2 6.9 %copy-start.22 = (bf16[2,3,1024]{2,0,1:T(2,128)(2,1)S(1)}, bf16[2,3,1024]{2,0,1:T(2,128)(2,1)}, u32[]{:S(2)}) copy-start(bf16[2,3,1024]{2,0,1:T(2,128)(2,1)} %param.31) | copy-start | bytes 36868
  82.4 6.7 %collective-permute-start = (bf16[2,3,1280]{2,0,1:T(2,128)(2,1)S(1)}, bf16[2,3,1280]{2,0,1:T(2,128)(2,1)S(1)}, u32[]{:S(2)}, u32[]{:S(2)}) collective-permute-start(bf16[2,3,1280]{2,0,1:T(2,128)(2,1)S(1)} %copy.113), channel_id=1, source_target_pairs={{0,4},{4,8},{8,12},{12,16},{16,20},{20,24},{24,28},{28,32},{32,36}... | collective-permute-start | bytes 46088 | tf_op jit(solution)/shard_map/ppermute | solution.py:17
  91.4 8.9 %copy-start.2 = (bf16[2,256,1280]{2,1,0:T(8,128)(2,1)}, bf16[2,256,1280]{2,1,0:T(8,128)(2,1)S(1)}, u32[]{:S(2)}) copy-start(bf16[2,256,1280]{2,1,0:T(8,128)(2,1)S(1)} %multiply_convert_fusion.2) | copy-start | bytes 3932164
  95.0 5.3 %copy-start.6 = (bf16[2,256,1024]{1,2,0:T(8,128)(2,1)}, bf16[2,256,1024]{1,2,0:T(8,128)(2,1)S(1)}, u32[]{:S(2)}) copy-start(bf16[2,256,1024]{1,2,0:T(8,128)(2,1)S(1)} %copy.90) | copy-start | bytes 3145732
  95.0 0.7 copy-start.20
  100.3 1.0 copy-start.8
  101.4 2.2 collective-permute-start.5
  101.5 1.8 collective-permute-start.1
  103.5 1.9 copy-start.10
  105.1 17.4 %collective-permute-start.6 = (f32[2,8,64,128]{3,0,2,1:T(2,128)S(1)}, f32[2,8,64,128]{3,0,2,1:T(2,128)S(1)}, u32[]{:S(2)}, u32[]{:S(2)}) collective-permute-start(f32[2,8,64,128]{3,0,2,1:T(2,128)S(1)} %select_add_fusion), channel_id=1, source_target_pairs={{0,8},{4,12},{8,16},{12,20},{16,24},{20,28},{24,32},{28,36},{32,40... | collective-permute-start | bytes 1572872 | tf_op jit(solution)/shard_map/ppermute | solution.py:17
  105.2 18.4 %collective-permute-start.2 = (f32[2,8]{1,0:T(2,128)S(1)}, f32[2,8]{1,0:T(2,128)S(1)}, u32[]{:S(2)}, u32[]{:S(2)}) collective-permute-start(f32[2,8]{1,0:T(2,128)S(1)} %get-tuple-element.11), channel_id=1, source_target_pairs={{0,8},{4,12},{8,16},{12,20},{16,24},{20,28},{24,32},{28,36},{32,40... | collective-permute-start | bytes 200 | tf_op jit(solution)/shard_map/ppermute | solution.py:17
  123.6 16.9 %collective-permute-start.7 = (f32[2,8,64,128]{3,0,2,1:T(2,128)S(1)}, f32[2,8,64,128]{3,0,2,1:T(2,128)S(1)}, u32[]{:S(2)}, u32[]{:S(2)}) collective-permute-start(f32[2,8,64,128]{3,0,2,1:T(2,128)S(1)} %fusion.30), channel_id=1, source_target_pairs={{0,16},{4,20},{8,24},{12,28},{16,32},{20,36},{24,40},{28,44},{32,4... | collective-permute-start | bytes 1572872 | tf_op jit(solution)/shard_map/ppermute | solution.py:17
  123.7 16.7 %collective-permute-start.3 = (f32[2,8]{1,0:T(2,128)S(1)}, f32[2,8]{1,0:T(2,128)S(1)}, u32[]{:S(2)}, u32[]{:S(2)}) collective-permute-start(f32[2,8]{1,0:T(2,128)S(1)} %maximum_multiply_fusion.4), channel_id=1, source_target_pairs={{0,16},{4,20},{8,24},{12,28},{16,32},{20,36},{24,40},{28,44},{32,4... | collective-permute-start | bytes 200 | tf_op jit(solution)/shard_map/ppermute | solution.py:17
  142.7 14.1 %collective-permute-start.8 = (f32[2,8,64,128]{3,0,2,1:T(2,128)}, f32[2,8,64,128]{3,0,2,1:T(2,128)S(1)}, u32[]{:S(2)}, u32[]{:S(2)}) collective-permute-start(f32[2,8,64,128]{3,0,2,1:T(2,128)} %fusion.31), channel_id=1, source_target_pairs={{0,32},{4,36},{8,40},{12,44},{16,48},{20,52},{24,56},{28,60},{32,6... | collective-permute-start | bytes 1572872 | tf_op jit(solution)/shard_map/ppermute | solution.py:17
  142.8 13.7 %collective-permute-start.4 = (f32[2,8]{1,0:T(2,128)S(1)}, f32[2,8]{1,0:T(2,128)S(1)}, u32[]{:S(2)}, u32[]{:S(2)}) collective-permute-start(f32[2,8]{1,0:T(2,128)S(1)} %maximum_multiply_fusion.5), channel_id=1, source_target_pairs={{0,32},{4,36},{8,40},{12,44},{16,48},{20,52},{24,56},{28,60},{32,6... | collective-permute-start | bytes 200 | tf_op jit(solution)/shard_map/ppermute | solution.py:17
  156.5 6.0 %collective-permute-start.10 = (f32[2,8]{1,0:T(2,128)S(1)}, f32[2,8]{1,0:T(2,128)S(1)}, u32[]{:S(2)}, u32[]{:S(2)}) collective-permute-start(f32[2,8]{1,0:T(2,128)S(1)} %maximum_multiply_fusion.6), channel_id=1, source_target_pairs={{0,64},{4,68},{8,72},{12,76},{16,80},{20,84},{24,88},{28,92},{32,9... | collective-permute-start | bytes 200 | tf_op jit(solution)/shard_map/ppermute | solution.py:17
  158.9 12.9 %collective-permute-start.9 = (f32[2,8,64,128]{3,0,2,1:T(2,128)S(1)}, f32[2,8,64,128]{3,0,2,1:T(2,128)S(1)}, u32[]{:S(2)}, u32[]{:S(2)}) collective-permute-start(f32[2,8,64,128]{3,0,2,1:T(2,128)S(1)} %fusion.32), channel_id=1, source_target_pairs={{0,64},{4,68},{8,72},{12,76},{16,80},{20,84},{24,88},{28,92},{32,9... | collective-permute-start | bytes 1572872 | tf_op jit(solution)/shard_map/ppermute | solution.py:17
  176.1 18.8 %copy-start.1 = (f32[2,256,1024]{2,1,0:T(8,128)S(1)}, f32[2,256,1024]{2,1,0:T(8,128)}, u32[]{:S(2)}) copy-start(f32[2,256,1024]{2,1,0:T(8,128)} %get-tuple-element.16) | copy-start | bytes 6291460
  176.1 14.1 %collective-permute-start.11 = (f32[2,8,64,128]{3,0,2,1:T(2,128)}, f32[2,8,64,128]{3,0,2,1:T(2,128)}, u32[]{:S(2)}, u32[]{:S(2)}) collective-permute-start(f32[2,8,64,128]{3,0,2,1:T(2,128)} %pad_maximum_fusion.1), channel_id=1, source_target_pairs={{0,8},{4,12},{8,16},{12,20},{16,24},{20,28},{24,32},{28,36},{32,40... | collective-permute-start | bytes 1572872 | tf_op jit(solution)/shard_map/ppermute | solution.py:17
  194.9 3.1 %collective-permute-start.12 = (f32[2,8,64,128]{3,0,2,1:T(2,128)}, f32[2,8,64,128]{3,0,2,1:T(2,128)}, u32[]{:S(2)}, u32[]{:S(2)}) collective-permute-start(f32[2,8,64,128]{3,0,2,1:T(2,128)} %get-tuple-element.15), channel_id=1, source_target_pairs={{0,4},{4,0},{8,12},{12,8},{16,20},{20,16},{24,28},{28,24},{32,36},... | collective-permute-start | bytes 1572872 | tf_op jit(solution)/shard_map/ppermute | solution.py:148
  201.0 2.1 copy-start.7
  201.0 2.1 copy-start.9
  201.0 2.1 copy-start.24
  213.0 2.1 copy-start.4
  213.1 2.1 copy-start.13
Sparse Core Ops, SparseCore 0:
  9.0 50.6 all-gather.1

commit v3 on v2

--- a/solution.py
+++ b/solution.py
@@ -129,6 +129,7 @@
     early = jax.tree.map(lambda own, other: jnp.where(core == 0, own, other), mine, got)
     later = jax.tree.map(lambda own, other: jnp.where(core == 0, other, own), mine, got)
     run_a, run_b = combine(early, later)
+    prior_a, prior_b = jnp.ones_like(run_a), jnp.zeros_like(run_b)
     span = 1
     while span < chips:
         got_a, got_b = from_behind((run_a, run_b), "seq", 2 * span)
@@ -136,13 +137,10 @@
         lead_a = jnp.stack([jnp.where(late, got_a[0], 1.0), jnp.where(late, got_a[1], got_a[0])])
         lead_b = jnp.stack([jnp.where(late, got_b[0], 0.0), jnp.where(late, got_b[1], got_b[0])])
         run_a, run_b = combine((lead_a, lead_b), (run_a, run_b))
+        prior_a, prior_b = combine((lead_a, lead_b), (prior_a, prior_b))
         span *= 2
-    top_a, top_b = combine((run_a[0], run_b[0]), (run_a[1], run_b[1]))
-    run_b = jnp.stack([run_b[0], top_b])
-    got_b = from_behind(run_b, "seq", 2)
-    before_chip = jnp.stack(
-        [jnp.where(chip >= 1, got_b[0], 0.0), jnp.where(chip >= 1, got_b[1], got_b[0])]
-    )
+    lift_a, lift_b = combine((run_a[0], run_b[0]), (prior_a[1], prior_b[1]))
+    before_chip = jnp.stack([prior_b[0], lift_b])
     after_early = early[0][..., None, None] * before_chip + early[1]
     own_part = jnp.where(core == 0, before_chip, after_early)
     other_part = lax.ppermute(jnp.where(core == 0, after_early, before_chip), "seq", pair)

time: 226 us -> 228 us (level)
  waiting for transfers between devices: 110 us -> 95.2 us
  other arithmetic: 30.2 us -> 41.5 us
  local copies, waits for them, and re-layouts: 32.7 us -> 37.7 us
    ppermute x10 -> x9, waiting for transfers between devices: 74.7 us -> 59.3 us  [from_behind(): return lax.ppermute(value, axis, pairs)]
    add x5, other arithmetic: 7.6 us -> 14.6 us  [combine(): later[0][..., None, None] * earlier[1] + later[1]]
    select_n x4, other arithmetic: 1.89 us -> 7.09 us  [per_device(): jnp.where(late, got_b[0], 0.0)]
    unnamed x54 -> x61, local copies, waits for them, and re-layouts: 20.9 us -> 22.8 us
    ppermute x10 -> x9, starting transfers between devices: 6.52 us -> 6.15 us  [from_behind(): return lax.ppermute(value, axis, pairs)]
  transfers between devices with their start and end apart: 14 -> 13, of which waited for: 8 -> 7; matrix products, arithmetic and copies ran while one was open for 12% -> 16% of each run, Pallas kernels for 0% -> 0%
where the time goes in v3:
time: 228 us; the launch traced here: 226 us
  waiting for transfers between devices  95.2 us (42%)
  other arithmetic  41.5 us (18%)
  local copies, waits for them, and re-layouts  37.7 us (17%)
  matrix products  30.8 us (14%)
  between operations  14 us (6%)
  starting transfers between devices  6.67 us (3%)
    ppermute x9, waiting for transfers between devices, from_behind(): return lax.ppermute(value, axis, pairs)  59.3 us
    all_gather x1, waiting for transfers between devices, per_device(): piece = lax.all_gather(hidden, 'mp', axis=1, tiled=True)  33.5 us
    unnamed x61, local copies, waits for them, and re-layouts  22.8 us
    add x5, other arithmetic, combine(): later[0][..., None, None] * earlier[1] + later[1]  14.6 us
    dot_general x1, matrix products, per_device(): zx_sum = jnp.dot(piece, flat_zx, preferred_element_type=jnp.float32)  13.8 us
    reshape x2, local copies, waits for them, and re-layouts, per_device(): y_total.reshape(rows_dev, inner_dev) * jax.nn.silu(gate.astype(jnp.float32))  7.27 us
    select_n x4, other arithmetic, per_device(): jnp.where(late, got_b[0], 0.0)  7.09 us
    ppermute x9, starting transfers between devices, from_behind(): return lax.ppermute(value, axis, pairs)  6.15 us
  transfers between devices with their start and end apart: 13, of which 7 were waited for; matrix products, arithmetic and copies ran while one was open for 16% of the time, Pallas kernels for 0%

profile of v3, /device:TPU:0, one launch (start us, length us, event | category | flops | bytes accessed | tf_op | source)
XLA Modules:
  0.0 225.9 jit_solution(6518084601911083640)
XLA Ops:
  6.5 0.7 all-gather.2.cloned.1.call-update
  7.3 0.9 select_reduce_fusion.1
  8.1 0.2 reduce-window.14
  8.4 17.3 %copy.129 = bf16[512,8,2,1024]{3,1,2,0:T(8,128)(2,1)} copy(bf16[512,8,2,1024]{3,2,1,0:T(2,128)(2,1)} %bitcast.103) | data formatting | bytes 33554432
  25.8 0.2 compare_reduce_fusion
  26.0 0.2 fusion.48
  26.3 33.5 %all-gather.2.cloned.1.call-done = bf16[512,4096]{1,0:T(8,128)(2,1)} async-done(((bf16[512,1024]{1,0:T(8,128)(2,1)}), bf16[512,4096]{1,0:T(8,128)(2,1)}) %all-gather.2.cloned.1.call-update) | async-done | bytes 4194320 | tf_op jit(solution)/shard_map/all_gather | solution.py:57
  59.7 3.4 %fusion.65 = f32[512,16]{0,1:T(8,128)S(1)} fusion(bf16[512,4096]{1,0:T(8,128)(2,1)} %all-gather.2.cloned.1.call-done, bf16[4096,16]{0,1:T(8,128)(2,1)S(1)} %copy-done.14), kind=kOutput, calls=%fused_computation.151 | convolution fusion | flops 67108864 | bytes 4358144 | tf_op jit(solution)/shard_map/dot_general | solution.py:60
  63.1 0.1 copy_bitcast_fusion.1
  63.2 1.2 reduce-window.18
  64.4 0.2 slice_reduce_fusion
  64.7 0.2 slice_reduce_fusion.1
  64.8 13.8 %convolution_convert_fusion = bf16[512,2048]{1,0:T(8,128)(2,1)S(1)} fusion(bf16[512,4096]{1,0:T(8,128)(2,1)} %all-gather.2.cloned.1.call-done, bf16[4096,2048]{1,0:T(8,128)(2,1)} %bitcast.104), kind=kOutput, calls=%fused_computation.8 | convolution fusion | flops 8590983168 | bytes 23068672 | tf_op jit(solution)/shard_map/dot_general | solution.py:58
  78.7 2.2 copy-done.24
  81.0 1.3 fusion.20
  82.4 0.3 collective-permute-start
  82.9 6.2 %collective-permute-done = bf16[2,3,1280]{2,0,1:T(2,128)(2,1)S(1)} collective-permute-done((bf16[2,3,1280]{2,0,1:T(2,128)(2,1)S(1)}, bf16[2,3,1280]{2,0,1:T(2,128)(2,1)S(1)}, u32[]{:S(2)}, u32[]{:S(2)}) %collective-permute-start) | collective-permute-done | bytes 15392 | tf_op jit(solution)/shard_map/ppermute | solution.py:17
  89.1 0.2 broadcast_select_fusion.9
  89.4 0.3 maximum_convert_fusion
  89.6 1.7 multiply_convert_fusion.2
  91.4 1.4 slice_convert_fusion
  92.8 2.3 %copy.99 = bf16[2,256,1024]{1,2,0:T(8,128)(2,1)} copy(bf16[2,256,1024]{2,1,0:T(8,128)(2,1)} %get-tuple-element.20) | data formatting | bytes 2097152 | tf_op jit(solution)/shard_map/slice | solution.py:95
  95.0 1.7 fusion.23
  96.7 4.6 %copy_add_fusion = (f32[2,16,64,128]{3,0,2,1:T(2,128)S(1)}, f32[2,16,64,128]{3,0,2,1:T(2,128)}) fusion(f32[2,16,64,128]{3,2,1,0:T(8,128)S(1)} %fusion.23, pred[2]{0:T(512)(128)(4,1)S(1)} %compare_reduce_fusion, f32[2,16]{0,1:T(8,128)S(1)} %copy.109, f32[2,16,64,128]{3,2,1,0:T(8,128)S(1)} %copy-done, s32[2]{0:T(128)S(1)} %fusion.48), kind=kOutput, calls=%fused_computation.42 | convolution fusion | flops 7077892 | bytes 4194442 | tf_op jit(solution)/shard_map/cr,rhpn->chpn/dot_general | solution.py:82
  101.4 1.0 copy-done.11
  102.4 0.8 constant_dynamic-slice_fusion
  103.3 0.5 collective-permute-start.1
  103.8 1.7 collective-permute-done.1
  105.6 2.4 %select_add_fusion = f32[2,8,64,128]{3,0,2,1:T(2,128)} fusion(f32[2,8,64,128]{3,0,2,1:T(2,128)} %collective-permute-done.5, pred[]{:T(512)S(6)} %eq.59, f32[2,16,64,128]{3,0,2,1:T(2,128)} %copy-done.11, s32[]{:T(128)S(6)} %select_n.211, f32[2,8]{0,1:T(8,128)S(1)} %copy.108), kind=kLoop, calls=%fused_computation.61 | loop fusion | flops 524288 | bytes 1572933 | tf_op jit(solution)/shard_map/add | solution.py:21
  108.2 17.4 %collective-permute-done.6 = f32[2,8,64,128]{3,0,2,1:T(2,128)} collective-permute-done((f32[2,8,64,128]{3,0,2,1:T(2,128)}, f32[2,8,64,128]{3,0,2,1:T(2,128)}, u32[]{:S(2)}, u32[]{:S(2)}) %collective-permute-start.6) | collective-permute-done | bytes 524320 | tf_op jit(solution)/shard_map/ppermute | solution.py:17
  125.6 1.8 broadcast_select_fusion.1
  127.4 0.7 copy-done.1
  128.1 2.5 %multiply_add_fusion.3 = f32[2,8,64,128]{3,0,2,1:T(2,128)} fusion(f32[2,8,64,128]{3,0,2,1:T(2,128)} %select_add_fusion, f32[2,8]{0,1:T(8,128)S(1)} %copy.107, f32[1,8,64,128]{3,0,2,1:T(1,128)S(1)} %get-tuple-element.30, f32[1,8,64,128]{3,0,2,1:T(1,128)S(1)} %get-tuple-element.29), kind=kLoop, calls=%fused_computation.60 | loop fusion | flops 393216 | bytes 1572928 | tf_op jit(solution)/shard_map/add | solution.py:21
  130.6 2.1 collective-permute-start.3
  132.7 14.9 %collective-permute-done.3 = f32[2,8]{1,0:T(2,128)S(1)} collective-permute-done((f32[2,8]{1,0:T(2,128)S(1)}, f32[2,8]{1,0:T(2,128)S(1)}, u32[]{:S(2)}, u32[]{:S(2)}) %collective-permute-start.3) | collective-permute-done | bytes 96 | tf_op jit(solution)/shard_map/ppermute | solution.py:17
  147.6 1.8 broadcast_select_fusion.3
  149.4 0.7 copy-done.7
  150.1 3.0 %multiply_add_fusion.2 = f32[2,8,64,128]{3,0,2,1:T(2,128)} fusion(f32[2,8]{0,1:T(8,128)S(1)} %copy.106, f32[1,8,64,128]{3,0,2,1:T(1,128)S(1)} %get-tuple-element.28, f32[1,8,64,128]{3,0,2,1:T(1,128)S(1)} %get-tuple-element.27, f32[2,8,64,128]{3,0,2,1:T(2,128)} %select_add_fusion, f32[1,8,64,128]{3,0,2,1:T(1,128)} %copy-done.1, ...), kind=kLoop, calls=%fused_computation.59 | loop fusion | flops 786432 | bytes 2097280 | tf_op jit(solution)/shard_map/add | solution.py:21
  153.1 0.3 collective-permute-start.4
  153.5 13.4 %collective-permute-done.4 = f32[2,8]{1,0:T(2,128)} collective-permute-done((f32[2,8]{1,0:T(2,128)S(1)}, f32[2,8]{1,0:T(2,128)}, u32[]{:S(2)}, u32[]{:S(2)}) %collective-permute-start.4) | collective-permute-done | bytes 96 | tf_op jit(solution)/shard_map/ppermute | solution.py:17
  166.9 0.7 broadcast_select_fusion.21
  167.7 0.6 fusion.51
  168.3 0.7 slice.186
  169.1 1.8 broadcast_select_fusion.5
  170.9 0.7 copy-done.9
  171.5 3.6 %multiply_add_fusion.1 = f32[2,8,64,128]{3,0,2,1:T(2,128)} fusion(f32[2,8]{0,1:T(8,128)S(1)} %copy.105, f32[1,8,64,128]{3,0,2,1:T(1,128)S(1)} %get-tuple-element.26, f32[1,8,64,128]{3,0,2,1:T(1,128)S(1)} %get-tuple-element.25, f32[1,8,64,128]{3,0,2,1:T(1,128)} %copy-done.8, f32[1,8,64,128]{3,0,2,1:T(1,128)} %copy-done.7, f32[2,8]{0,1:T(8,128)S(1)} %copy.106, ...), kind=kLoop, calls=%fused_computation.58 | loop fusion | flops 1179648 | bytes 2621632 | tf_op jit(solution)/shard_map/add | solution.py:21
  175.1 3.5 %collective-permute-start.9 = (f32[2,8,64,128]{3,0,2,1:T(2,128)}, f32[2,8,64,128]{3,0,2,1:T(2,128)}, u32[]{:S(2)}, u32[]{:S(2)}) collective-permute-start(f32[2,8,64,128]{3,0,2,1:T(2,128)} %multiply_add_fusion.1), channel_id=1, source_target_pairs={{0,64},{4,68},{8,72},{12,76},{16,80},{20,84},{24,88},{28,92},{32,9... | collective-permute-start | bytes 1572872 | tf_op jit(solution)/shard_map/ppermute | solution.py:17
  178.7 0.8 broadcast_select_fusion.13
  179.4 0.6 maximum_multiply_fusion
  180.3 0.7 slice_bitcast_fusion
  180.9 7.4 %collective-permute-done.9 = f32[2,8,64,128]{3,0,2,1:T(2,128)} collective-permute-done((f32[2,8,64,128]{3,0,2,1:T(2,128)}, f32[2,8,64,128]{3,0,2,1:T(2,128)}, u32[]{:S(2)}, u32[]{:S(2)}) %collective-permute-start.9) | collective-permute-done | bytes 524320 | tf_op jit(solution)/shard_map/ppermute | solution.py:17
  188.3 1.8 broadcast_select_fusion.7
  190.1 3.2 %fusion.31 = f32[2,8,64,128]{3,0,2,1:T(2,128)S(1)} fusion(f32[1,8,64,128]{3,0,2,1:T(1,128)S(1)} %get-tuple-element.24, f32[1,8,64,128]{3,0,2,1:T(1,128)S(1)} %get-tuple-element.23, f32[2,8]{0,1:T(8,128)S(1)} %copy.112, f32[2,8]{0,1:T(8,128)S(1)} %copy.111, f32[2,8]{0,1:T(8,128)S(1)} %copy.104, f32[1,8,64,128]{3,0,2,1:T(1,128)} %copy-done.10, ...), kind=kLoop, calls=%fused_computation.50 | loop fusion | flops 1310720 | bytes 2621632 | tf_op jit(solution)/shard_map/add | solution.py:21
  193.3 2.0 fusion.63
  195.3 1.9 fusion.33
  197.2 1.8 copy.116
  199.0 1.2 fusion.39
  200.2 2.9 %fusion.24 = f32[2,16,64,128]{3,0,2,1:T(2,128)S(1)} fusion(f32[2,16,64,128]{3,0,2,1:T(2,128)} %get-tuple-element.48, f32[2,8,64,128]{3,0,2,1:T(2,128)} %collective-permute-done.11, f32[2,8,64,128]{3,0,2,1:T(2,128)} %get-tuple-element.17, pred[2]{0:T(512)(128)(4,1)S(1)} %copy-done.22, pred[]{:T(512)S(6)} %eq.59), kind=kLoop, calls=%fused_computation.39 | loop fusion | flops 1048576 | bytes 3145731 | tf_op jit(solution)/shard_map/jit(_where)/select_n | solution.py:152
  203.2 2.1 fusion.25
  205.3 2.6 %fusion.19 = f32[2,256,1,16,64]{1,4,3,0,2:T(8,128)S(1)} fusion(f32[2,16,64,256]{3,2,1,0:T(8,128)S(1)} %fusion.25, f32[2,256,1,16,64]{1,4,3,0,2:T(8,128)S(1)} %bitcast.109, bf16[2,256,16,64]{1,3,2,0:T(8,128)(2,1)S(1)} %bitcast.108, f32[2,16,256]{2,1,0:T(8,128)S(1)} %get-tuple-element.31, f32[2,16,256]{2,1,0:T(8,128)S(1)} %get-tuple-element.34, ...), kind=kOutput, calls=%fused_computation.30 | convolution fusion | flops 281018368 | bytes 8028224 | tf_op jit(solution)/shard_map/cgjqk,ckgjp->cqgjp/dot_general | solution.py:109
  207.9 3.8 %copy.123 = f32[2,256,1,16,64]{4,3,1,0,2:T(8,128)} copy(f32[2,256,1,16,64]{1,4,3,0,2:T(8,128)S(1)} %fusion.19) | data formatting | bytes 4194304 | tf_op jit(solution)/shard_map/reshape | solution.py:162
  211.7 3.5 %reshape.294 = f32[512,1024]{1,0:T(8,128)S(1)} reshape(f32[2,256,1,16,64]{4,3,1,0,2:T(8,128)} %copy.123) | data formatting | bytes 4194304 | tf_op jit(solution)/shard_map/reshape | solution.py:162
  215.2 2.1 multiply_reduce_fusion
  217.3 1.7 multiply_convert_fusion.3
  (102 shorter events, 1.8 us)
Async XLA Ops:
  6.5 90.2 %copy-start = (f32[2,16,64,128]{3,2,1,0:T(8,128)S(1)}, f32[2,16,64,128]{3,2,1,0:T(8,128)}, u32[]{:S(2)}) copy-start(f32[2,16,64,128]{3,2,1,0:T(8,128)} %param.30) | copy-start | bytes 3145732
  6.5 53.2 %all-gather.2.cloned.1.call-start = ((), (), s32[]{:S(2)}) async-start(), calls=%async_computation | async-start | bytes 5242880 | tf_op jit(solution)/shard_map/all_gather | solution.py:57
  8.3 17.3 %copy-start.19 = (bf16[2,3,2,128]{3,2,1,0:T(2,128)(2,1)S(1)}, bf16[2,3,2,128]{3,2,1,0:T(2,128)(2,1)}, u32[]{:S(2)}) copy-start(bf16[2,3,2,128]{3,2,1,0:T(2,128)(2,1)} %param.32) | copy-start | bytes 9220
  8.3 17.4 %copy-start.17 = (f32[1024]{0:T(1024)S(1)}, f32[1024]{0:T(1024)}, u32[]{:S(2)}) copy-start(f32[1024]{0:T(1024)} %param.23) | copy-start | bytes 12292
  8.3 17.4 %copy-start.23 = (f32[2,128]{1,0:T(2,128)S(1)}, f32[2,128]{1,0:T(2,128)}, u32[]{:S(2)}) copy-start(f32[2,128]{1,0:T(2,128)} %param.25) | copy-start | bytes 3076
  8.3 17.4 %copy-start.15 = (f32[4,1024]{1,0:T(4,128)S(1)}, f32[4,1024]{1,0:T(4,128)}, u32[]{:S(2)}) copy-start(f32[4,1024]{1,0:T(4,128)} %param.22) | copy-start | bytes 49156
  8.3 17.8 %copy-start.18 = (f32[4,2,128]{2,1,0:T(2,128)S(1)}, f32[4,2,128]{2,1,0:T(2,128)}, u32[]{:S(2)}) copy-start(f32[4,2,128]{2,1,0:T(2,128)} %param.24) | copy-start | bytes 12292
  8.4 17.9 %copy-start.26 = (f32[16]{0:T(128)S(1)}, f32[16]{0:T(128)}, u32[]{:S(2)}) copy-start(f32[16]{0:T(128)} %param.26) | copy-start | bytes 196
  8.4 51.4 %copy-start.14 = (bf16[4096,16]{0,1:T(8,128)(2,1)S(1)}, bf16[4096,16]{0,1:T(8,128)(2,1)}, u32[]{:S(2)}) copy-start(bf16[4096,16]{0,1:T(8,128)(2,1)} %param.21) | copy-start | bytes 393220
  26.0 70.8 %copy-start.21 = (pred[2]{0:T(512)(128)(4,1)}, pred[2]{0:T(512)(128)(4,1)S(1)}, u32[]{:S(2)}) copy-start(pred[2]{0:T(512)(128)(4,1)S(1)} %compare_reduce_fusion) | copy-start | bytes 10
  26.3 36.9 %copy-start.20 = (f32[16]{0:T(128)S(1)}, f32[16]{0:T(128)}, u32[]{:S(2)}) copy-start(f32[16]{0:T(128)} %param.27) | copy-start | bytes 196
  64.8 13.9 %copy-start.5 = (bf16[512,4096]{1,0:T(8,128)(2,1)S(1)}, bf16[512,4096]{1,0:T(8,128)(2,1)}, u32[]{:S(2)}) copy-start(bf16[512,4096]{1,0:T(8,128)(2,1)} %all-gather.2.cloned.1.call-done) | copy-start | bytes 12582916
  78.6 3.6 %copy-start.3 = (bf16[512,2048]{1,0:T(8,128)(2,1)}, bf16[512,2048]{1,0:T(8,128)(2,1)S(1)}, u32[]{:S(2)}) copy-start(bf16[512,2048]{1,0:T(8,128)(2,1)S(1)} %convolution_convert_fusion) | copy-start | bytes 6291460
  78.6 2.4 %copy-start.24 = (bf16[4096,2,128]{2,1,0:T(2,128)(2,1)S(1)}, bf16[4096,2,128]{2,1,0:T(2,128)(2,1)}, u32[]{:S(2)}) copy-start(bf16[4096,2,128]{2,1,0:T(2,128)(2,1)} %param.20) | copy-start | bytes 6291460
  82.2 6.9 %copy-start.25 = (bf16[2,3,1024]{2,0,1:T(2,128)(2,1)S(1)}, bf16[2,3,1024]{2,0,1:T(2,128)(2,1)}, u32[]{:S(2)}) copy-start(bf16[2,3,1024]{2,0,1:T(2,128)(2,1)} %param.31) | copy-start | bytes 36868
  82.4 6.7 %collective-permute-start = (bf16[2,3,1280]{2,0,1:T(2,128)(2,1)S(1)}, bf16[2,3,1280]{2,0,1:T(2,128)(2,1)S(1)}, u32[]{:S(2)}, u32[]{:S(2)}) collective-permute-start(bf16[2,3,1280]{2,0,1:T(2,128)(2,1)S(1)} %copy.125), channel_id=1, source_target_pairs={{0,4},{4,8},{8,12},{12,16},{16,20},{20,24},{24,28},{28,32},{32,36}... | collective-permute-start | bytes 46088 | tf_op jit(solution)/shard_map/ppermute | solution.py:17
  91.4 1.4 copy-start.2
  101.4 1.0 copy-start.11
  103.2 2.4 %collective-permute-start.5 = (f32[2,8,64,128]{3,0,2,1:T(2,128)}, f32[2,8,64,128]{3,0,2,1:T(2,128)}, u32[]{:S(2)}, u32[]{:S(2)}) collective-permute-start(f32[2,8,64,128]{3,0,2,1:T(2,128)} %constant_dynamic-slice_fusion), channel_id=1, source_target_pairs={{0,4},{4,0},{8,12},{12,8},{16,20},{20,16},{24,28},{28,24},{32,36},... | collective-permute-start | bytes 1572872 | tf_op jit(solution)/shard_map/ppermute | solution.py:128
  103.3 2.2 collective-permute-start.1
  108.0 17.6 %collective-permute-start.6 = (f32[2,8,64,128]{3,0,2,1:T(2,128)}, f32[2,8,64,128]{3,0,2,1:T(2,128)}, u32[]{:S(2)}, u32[]{:S(2)}) collective-permute-start(f32[2,8,64,128]{3,0,2,1:T(2,128)} %select_add_fusion), channel_id=1, source_target_pairs={{0,8},{4,12},{8,16},{12,20},{16,24},{20,28},{24,32},{28,36},{32,40... | collective-permute-start | bytes 1572872 | tf_op jit(solution)/shard_map/ppermute | solution.py:17
  108.0 22.6 %collective-permute-start.2 = (f32[2,8]{1,0:T(2,128)S(1)}, f32[2,8]{1,0:T(2,128)S(1)}, u32[]{:S(2)}, u32[]{:S(2)}) collective-permute-start(f32[2,8]{1,0:T(2,128)S(1)} %get-tuple-element.14), channel_id=1, source_target_pairs={{0,8},{4,12},{8,16},{12,20},{16,24},{20,28},{24,32},{28,36},{32,40... | collective-permute-start | bytes 200 | tf_op jit(solution)/shard_map/ppermute | solution.py:17
  127.4 0.7 copy-start.1
  130.6 17.0 %collective-permute-start.7 = (f32[2,8,64,128]{3,0,2,1:T(2,128)}, f32[2,8,64,128]{3,0,2,1:T(2,128)}, u32[]{:S(2)}, u32[]{:S(2)}) collective-permute-start(f32[2,8,64,128]{3,0,2,1:T(2,128)} %multiply_add_fusion.3), channel_id=1, source_target_pairs={{0,16},{4,20},{8,24},{12,28},{16,32},{20,36},{24,40},{28,44},{32,4... | collective-permute-start | bytes 1572872 | tf_op jit(solution)/shard_map/ppermute | solution.py:17
  130.6 17.0 %collective-permute-start.3 = (f32[2,8]{1,0:T(2,128)S(1)}, f32[2,8]{1,0:T(2,128)S(1)}, u32[]{:S(2)}, u32[]{:S(2)}) collective-permute-start(f32[2,8]{1,0:T(2,128)S(1)} %fusion.57), channel_id=1, source_target_pairs={{0,16},{4,20},{8,24},{12,28},{16,32},{20,36},{24,40},{28,44},{32,4... | collective-permute-start | bytes 200 | tf_op jit(solution)/shard_map/ppermute | solution.py:17
  149.4 0.7 copy-start.7
  149.4 3.7 %copy-start.8 = (f32[1,8,64,128]{3,0,2,1:T(1,128)}, f32[1,8,64,128]{3,0,2,1:T(1,128)S(1)}, u32[]{:S(2)}) copy-start(f32[1,8,64,128]{3,0,2,1:T(1,128)S(1)} %get-tuple-element.28) | copy-start | bytes 786436
  153.1 16.0 %collective-permute-start.8 = (f32[2,8,64,128]{3,0,2,1:T(2,128)}, f32[2,8,64,128]{3,0,2,1:T(2,128)}, u32[]{:S(2)}, u32[]{:S(2)}) collective-permute-start(f32[2,8,64,128]{3,0,2,1:T(2,128)} %multiply_add_fusion.2), channel_id=1, source_target_pairs={{0,32},{4,36},{8,40},{12,44},{16,48},{20,52},{24,56},{28,60},{32,6... | collective-permute-start | bytes 1572872 | tf_op jit(solution)/shard_map/ppermute | solution.py:17
  153.1 13.8 %collective-permute-start.4 = (f32[2,8]{1,0:T(2,128)S(1)}, f32[2,8]{1,0:T(2,128)}, u32[]{:S(2)}, u32[]{:S(2)}) collective-permute-start(f32[2,8]{1,0:T(2,128)S(1)} %fusion.54), channel_id=1, source_target_pairs={{0,32},{4,36},{8,40},{12,44},{16,48},{20,52},{24,56},{28,60},{32,6... | collective-permute-start | bytes 200 | tf_op jit(solution)/shard_map/ppermute | solution.py:17
  168.3 10.4 %collective-permute-start.10 = (f32[2,8]{1,0:T(2,128)}, f32[2,8]{1,0:T(2,128)}, u32[]{:S(2)}, u32[]{:S(2)}) collective-permute-start(f32[2,8]{1,0:T(2,128)} %fusion.51), channel_id=1, source_target_pairs={{0,64},{4,68},{8,72},{12,76},{16,80},{20,84},{24,88},{28,92},{32,9... | collective-permute-start | bytes 200 | tf_op jit(solution)/shard_map/ppermute | solution.py:17
  170.8 0.7 copy-start.9
  170.8 4.3 %copy-start.10 = (f32[1,8,64,128]{3,0,2,1:T(1,128)}, f32[1,8,64,128]{3,0,2,1:T(1,128)S(1)}, u32[]{:S(2)}) copy-start(f32[1,8,64,128]{3,0,2,1:T(1,128)S(1)} %get-tuple-element.26) | copy-start | bytes 786436
  175.1 13.2 %collective-permute-start.9 = (f32[2,8,64,128]{3,0,2,1:T(2,128)}, f32[2,8,64,128]{3,0,2,1:T(2,128)}, u32[]{:S(2)}, u32[]{:S(2)}) collective-permute-start(f32[2,8,64,128]{3,0,2,1:T(2,128)} %multiply_add_fusion.1), channel_id=1, source_target_pairs={{0,64},{4,68},{8,72},{12,76},{16,80},{20,84},{24,88},{28,92},{32,9... | collective-permute-start | bytes 1572872 | tf_op jit(solution)/shard_map/ppermute | solution.py:17
  190.1 5.1 %copy-start.12 = (f32[2,16,64,128]{3,0,2,1:T(2,128)S(1)}, f32[2,16,64,128]{3,0,2,1:T(2,128)}, u32[]{:S(2)}) copy-start(f32[2,16,64,128]{3,0,2,1:T(2,128)} %copy-done.11) | copy-start | bytes 3145732
  197.1 3.1 %collective-permute-start.11 = (f32[2,8,64,128]{3,0,2,1:T(2,128)}, f32[2,8,64,128]{3,0,2,1:T(2,128)}, u32[]{:S(2)}, u32[]{:S(2)}) collective-permute-start(f32[2,8,64,128]{3,0,2,1:T(2,128)} %get-tuple-element.18), channel_id=1, source_target_pairs={{0,4},{4,0},{8,12},{12,8},{16,20},{20,16},{24,28},{28,24},{32,36},... | collective-permute-start | bytes 1572872 | tf_op jit(solution)/shard_map/ppermute | solution.py:146
  197.2 3.1 %copy-start.22 = (pred[2]{0:T(512)(128)(4,1)S(1)}, pred[2]{0:T(512)(128)(4,1)}, u32[]{:S(2)}) copy-start(pred[2]{0:T(512)(128)(4,1)} %copy-done.21) | copy-start | bytes 10
  203.2 2.1 copy-start.6
  203.2 2.1 copy-start.13
  203.2 2.1 copy-start.27
  215.2 2.1 copy-start.4
  215.2 2.1 copy-start.16
Sparse Core Ops, SparseCore 0:
  9.0 50.6 all-gather.1

commit v4 on v3

--- a/solution.py
+++ b/solution.py
@@ -18,7 +18,7 @@
 
 
 def combine(earlier, later):
-    return (earlier[0] * later[0], later[0][..., None, None] * earlier[1] + later[1])
+    return (earlier[0] * later[0], later[0][:, None, None] * earlier[1] + later[1])
 
 
 def per_device(
@@ -122,7 +122,12 @@
     chip = place // 2
     chips = devices // 2
     half = heads_dev // 2
-    keep = lambda part, at: lax.dynamic_slice_in_dim(part, at * half, half, axis=1)
+    rows = blocks * half
+
+    def keep(part, at):
+        piece = lax.dynamic_slice_in_dim(part, at * half, half, axis=1)
+        return piece.reshape((rows,) + part.shape[2:])
+
     pair = [(source, source ^ 1) for source in range(devices)]
     mine = (keep(step_a, core), keep(step_b, core))
     got = lax.ppermute((keep(step_a, 1 - core), keep(step_b, 1 - core)), "seq", pair)
@@ -130,20 +135,26 @@
     later = jax.tree.map(lambda own, other: jnp.where(core == 0, other, own), mine, got)
     run_a, run_b = combine(early, later)
     prior_a, prior_b = jnp.ones_like(run_a), jnp.zeros_like(run_b)
+
+    def wrap(part, neutral, late):
+        moved = jnp.concatenate([jnp.full_like(part[:half], neutral), part[: rows - half]], axis=0)
+        return jnp.where(late, part, moved)
+
     span = 1
     while span < chips:
         got_a, got_b = from_behind((run_a, run_b), "seq", 2 * span)
         late = chip >= span
-        lead_a = jnp.stack([jnp.where(late, got_a[0], 1.0), jnp.where(late, got_a[1], got_a[0])])
-        lead_b = jnp.stack([jnp.where(late, got_b[0], 0.0), jnp.where(late, got_b[1], got_b[0])])
-        run_a, run_b = combine((lead_a, lead_b), (run_a, run_b))
-        prior_a, prior_b = combine((lead_a, lead_b), (prior_a, prior_b))
+        lead = (wrap(got_a, 1.0, late), wrap(got_b, 0.0, late))
+        run_a, run_b = combine(lead, (run_a, run_b))
+        prior_a, prior_b = combine(lead, (prior_a, prior_b))
         span *= 2
-    lift_a, lift_b = combine((run_a[0], run_b[0]), (prior_a[1], prior_b[1]))
-    before_chip = jnp.stack([prior_b[0], lift_b])
-    after_early = early[0][..., None, None] * before_chip + early[1]
+    lift = combine((run_a[:half], run_b[:half]), (prior_a[half:], prior_b[half:]))[1]
+    before_chip = jnp.concatenate([prior_b[:half], lift], axis=0)
+    after_early = early[0][:, None, None] * before_chip + early[1]
     own_part = jnp.where(core == 0, before_chip, after_early)
     other_part = lax.ppermute(jnp.where(core == 0, after_early, before_chip), "seq", pair)
+    split_rows = lambda part: part.reshape((blocks, half) + part.shape[1:])
+    own_part, other_part = split_rows(own_part), split_rows(other_part)
     previous = jnp.where(
         core == 0,
         jnp.concatenate([own_part, other_part], axis=1),

time: 228 us -> 218 us (0.956)
  other arithmetic: 41.5 us -> 23.2 us
  local copies, waits for them, and re-layouts: 37.7 us -> 44.1 us
  waiting for transfers between devices: 95.2 us -> 97.6 us
    select_n x8 -> x1, other arithmetic: 8.61 us -> 0.07 us  [per_device(): step_a = jnp.where(first[:, None], 0.0, grow)]
    add x5, other arithmetic: 14.6 us -> 9.44 us  [combine(): later[0][:, None, None] * earlier[1] + later[1]]
    slice x2 -> x6, local copies, waits for them, and re-layouts: 0.86 us -> 4.1 us  [the longest x4 3.87 us: wrap(): part[:rows - half]]
    reshape x0 -> x4, local copies, waits for them, and re-layouts: none -> 3.06 us  [the longest x2 2.9 us: per_device(): split_rows = lambda part: part.reshape((blocks, half) + part.shape[1:])]
    ppermute x9, waiting for transfers between devices: 59.3 us -> 61.8 us  [from_behind(): return lax.ppermute(value, axis, pairs)]
    unnamed x61 -> x52, local copies, waits for them, and re-layouts: 22.8 us -> 22.3 us
  transfers between devices with their start and end apart: 13 -> 13, of which waited for: 7 -> 10; matrix products, arithmetic and copies ran while one was open for 16% -> 13% of each run, Pallas kernels for 0% -> 0%
where the time goes in v4:
time: 218 us; the launch traced here: 214 us
  waiting for transfers between devices  97.6 us (45%)
  local copies, waits for them, and re-layouts  44.1 us (20%)
  matrix products  30.7 us (14%)
  other arithmetic  23.2 us (11%)
  between operations  14 us (6%)
  starting transfers between devices  4.6 us (2%)
    ppermute x9, waiting for transfers between devices, from_behind(): return lax.ppermute(value, axis, pairs)  61.8 us
    all_gather x1, waiting for transfers between devices, per_device(): piece = lax.all_gather(hidden, 'mp', axis=1, tiled=True)  33.6 us
    unnamed x52, local copies, waits for them, and re-layouts  22.3 us
    dot_general x1, matrix products, per_device(): zx_sum = jnp.dot(piece, flat_zx, preferred_element_type=jnp.float32)  15.7 us
    add x5, other arithmetic, combine(): later[0][:, None, None] * earlier[1] + later[1]  9.44 us
    reshape x2, local copies, waits for them, and re-layouts, per_device(): y_total.reshape(rows_dev, inner_dev) * jax.nn.silu(gate.astype(jnp.float32))  7.27 us
    dot_general x1, matrix products, per_device(): jnp.einsum('cr,rhpn->chpn', pick, state_bank, precision=lax.Precision.HIG...  4.64 us
  transfers between devices with their start and end apart: 13, of which 10 were waited for; matrix products, arithmetic and copies ran while one was open for 13% of the time, Pallas kernels for 0%

profile of v4, /device:TPU:0, one launch (start us, length us, event | category | flops | bytes accessed | tf_op | source)
XLA Modules:
  0.0 214.1 jit_solution(4180637219123480850)
XLA Ops:
  6.5 0.7 all-gather.2.cloned.1.call-update
  7.3 0.9 select_reduce_fusion.1
  8.2 0.2 reduce-window.14
  8.4 17.2 %copy.111 = bf16[512,8,2,1024]{3,1,2,0:T(8,128)(2,1)} copy(bf16[512,8,2,1024]{3,2,1,0:T(2,128)(2,1)} %bitcast.120) | data formatting | bytes 33554432
  25.7 0.2 compare_reduce_fusion
  25.9 0.2 fusion.46
  26.2 33.6 %all-gather.2.cloned.1.call-done = bf16[512,4096]{1,0:T(8,128)(2,1)} async-done(((bf16[512,1024]{1,0:T(8,128)(2,1)}), bf16[512,4096]{1,0:T(8,128)(2,1)}) %all-gather.2.cloned.1.call-update) | async-done | bytes 4194320 | tf_op jit(solution)/shard_map/all_gather | solution.py:57
  59.8 15.7 %convolution_convert_fusion = bf16[512,2048]{1,0:T(8,128)(2,1)S(1)} fusion(bf16[512,4096]{1,0:T(8,128)(2,1)} %all-gather.2.cloned.1.call-done, bf16[4096,2048]{1,0:T(8,128)(2,1)} %bitcast.121), kind=kOutput, calls=%fused_computation.8 | convolution fusion | flops 8590983168 | bytes 23068672 | tf_op jit(solution)/shard_map/dot_general | solution.py:58
  75.6 2.2 %copy-done.20 = bf16[4096,2,128]{2,1,0:T(2,128)(2,1)S(1)} copy-done((bf16[4096,2,128]{2,1,0:T(2,128)(2,1)S(1)}, bf16[4096,2,128]{2,1,0:T(2,128)(2,1)}, u32[]{:S(2)}) %copy-start.20) | copy-done | bytes 2097176
  77.8 1.3 fusion.20
  79.3 0.3 collective-permute-start
  79.6 0.5 copy-done.12
  80.1 1.2 fusion.63
  81.3 1.2 reduce-window.18
  82.5 0.2 slice_reduce_fusion
  82.8 0.2 slice_reduce_fusion.1
  83.0 0.1 fusion.57
  83.2 2.8 %collective-permute-done = bf16[2,3,1280]{2,0,1:T(2,128)(2,1)S(1)} collective-permute-done((bf16[2,3,1280]{2,0,1:T(2,128)(2,1)S(1)}, bf16[2,3,1280]{2,0,1:T(2,128)(2,1)S(1)}, u32[]{:S(2)}, u32[]{:S(2)}) %collective-permute-start) | collective-permute-done | bytes 15392 | tf_op jit(solution)/shard_map/ppermute | solution.py:17
  86.0 0.2 broadcast_select_fusion
  86.3 0.3 maximum_convert_fusion
  86.6 1.7 multiply_convert_fusion.2
  88.3 1.4 slice_convert_fusion
  89.7 2.3 %copy.84 = bf16[2,256,1024]{1,2,0:T(8,128)(2,1)} copy(bf16[2,256,1024]{2,1,0:T(8,128)(2,1)} %get-tuple-element.24) | data formatting | bytes 2097152 | tf_op jit(solution)/shard_map/slice | solution.py:95
  91.9 1.7 fusion.23
  93.6 4.6 %copy_add_fusion = (f32[2,16,64,128]{3,0,2,1:T(2,128)S(1)}, f32[2,16,64,128]{3,0,2,1:T(2,128)}) fusion(f32[2,16,64,128]{3,2,1,0:T(8,128)S(1)} %fusion.23, pred[2]{0:T(512)(128)(4,1)S(1)} %compare_reduce_fusion, f32[2,16]{0,1:T(8,128)S(1)} %copy.89, f32[2,16,64,128]{3,2,1,0:T(8,128)S(1)} %copy-done, s32[2]{0:T(128)S(1)} %fusion.46), kind=kOutput, calls=%fused_computation.42 | convolution fusion | flops 7077892 | bytes 4194442 | tf_op jit(solution)/shard_map/cr,rhpn->chpn/dot_general | solution.py:82
  98.3 0.9 constant_dynamic-slice_fusion
  99.1 0.9 copy.92
  100.2 0.5 collective-permute-start.1
  100.7 1.5 collective-permute-done.1
  102.3 1.1 copy.91
  103.4 0.8 copy-done.4
  104.2 2.0 fusion.30
  106.2 17.6 %collective-permute-done.6 = f32[16,64,128]{2,1,0:T(8,128)} collective-permute-done((f32[16,64,128]{2,1,0:T(8,128)}, f32[16,64,128]{2,1,0:T(8,128)}, u32[]{:S(2)}, u32[]{:S(2)}) %collective-permute-start.6) | collective-permute-done | bytes 524320 | tf_op jit(solution)/shard_map/ppermute | solution.py:17
  123.8 1.0 slice.137
  124.8 2.0 multiply_add_fusion.3
  126.8 13.5 %collective-permute-done.2 = f32[16]{0:T(128)S(1)} collective-permute-done((f32[16]{0:T(128)S(1)}, f32[16]{0:T(128)S(1)}, u32[]{:S(2)}, u32[]{:S(2)}) %collective-permute-start.2) | collective-permute-done | bytes 96 | tf_op jit(solution)/shard_map/ppermute | solution.py:17
  140.3 3.5 %collective-permute-done.7 = f32[16,64,128]{2,1,0:T(8,128)} collective-permute-done((f32[16,64,128]{2,1,0:T(8,128)}, f32[16,64,128]{2,1,0:T(8,128)}, u32[]{:S(2)}, u32[]{:S(2)}) %collective-permute-start.7) | collective-permute-done | bytes 524320 | tf_op jit(solution)/shard_map/ppermute | solution.py:17
  143.8 1.0 slice.138
  144.8 0.7 copy-done.8
  145.5 2.0 multiply_add_fusion.2
  147.5 11.7 %collective-permute-done.3 = f32[16]{0:T(128)S(1)} collective-permute-done((f32[16]{0:T(128)S(1)}, f32[16]{0:T(128)S(1)}, u32[]{:S(2)}, u32[]{:S(2)}) %collective-permute-start.3) | collective-permute-done | bytes 96 | tf_op jit(solution)/shard_map/ppermute | solution.py:17
  159.3 2.0 collective-permute-done.8
  161.3 1.0 slice.139
  162.2 0.7 copy-done.9
  163.0 2.0 multiply_add_fusion.1
  165.0 0.6 collective-permute-start.4
  165.5 9.0 %collective-permute-done.4 = f32[16]{0:T(128)S(1)} collective-permute-done((f32[16]{0:T(128)S(1)}, f32[16]{0:T(128)S(1)}, u32[]{:S(2)}, u32[]{:S(2)}) %collective-permute-start.4) | collective-permute-done | bytes 96 | tf_op jit(solution)/shard_map/ppermute | solution.py:17
  174.6 3.3 %collective-permute-start.10 = (f32[16]{0:T(128)S(1)}, f32[16]{0:T(128)S(1)}, u32[]{:S(2)}, u32[]{:S(2)}) collective-permute-start(f32[16]{0:T(128)S(1)} %fusion.52), channel_id=1, source_target_pairs={{0,64},{4,68},{8,72},{12,76},{16,80},{20,84},{24,88},{28,92},{32,9... | collective-permute-start | bytes 200 | tf_op jit(solution)/shard_map/ppermute | solution.py:17
  177.8 1.8 collective-permute-done.10
  179.8 1.0 slice.140
  180.8 1.4 add_add_fusion
  182.2 1.1 fusion.62
  183.3 1.2 fusion.32
  184.5 1.8 copy.98
  186.4 1.3 fusion.37
  187.7 1.4 copy.93
  189.1 1.4 copy.94
  190.6 0.8 fusion.24
  191.5 2.1 fusion.25
  193.5 2.6 %fusion.19 = f32[2,256,1,16,64]{1,4,3,0,2:T(8,128)S(1)} fusion(f32[2,16,64,256]{3,2,1,0:T(8,128)S(1)} %fusion.25, f32[2,256,1,16,64]{1,4,3,0,2:T(8,128)S(1)} %bitcast.127, bf16[2,256,16,64]{1,3,2,0:T(8,128)(2,1)S(1)} %bitcast.125, f32[2,16,256]{2,1,0:T(8,128)S(1)} %get-tuple-element.29, f32[2,16,256]{2,1,0:T(8,128)S(1)} %get-tuple-element.32, ...), kind=kOutput, calls=%fused_computation.30 | convolution fusion | flops 281018368 | bytes 8028224 | tf_op jit(solution)/shard_map/cgjqk,ckgjp->cqgjp/dot_general | solution.py:109
  196.2 3.8 %copy.105 = f32[2,256,1,16,64]{4,3,1,0,2:T(8,128)} copy(f32[2,256,1,16,64]{1,4,3,0,2:T(8,128)S(1)} %fusion.19) | data formatting | bytes 4194304 | tf_op jit(solution)/shard_map/reshape | solution.py:173
  199.9 3.5 %reshape.260 = f32[512,1024]{1,0:T(8,128)S(1)} reshape(f32[2,256,1,16,64]{4,3,1,0,2:T(8,128)} %copy.105) | data formatting | bytes 4194304 | tf_op jit(solution)/shard_map/reshape | solution.py:173
  203.5 2.1 multiply_reduce_fusion
  205.6 1.7 multiply_convert_fusion.3
  (86 shorter events, 1.5 us)
Async XLA Ops:
  6.5 87.1 %copy-start = (f32[2,16,64,128]{3,2,1,0:T(8,128)S(1)}, f32[2,16,64,128]{3,2,1,0:T(8,128)}, u32[]{:S(2)}) copy-start(f32[2,16,64,128]{3,2,1,0:T(8,128)} %param.30) | copy-start | bytes 3145732
  6.5 53.2 %all-gather.2.cloned.1.call-start = ((), (), s32[]{:S(2)}) async-start(), calls=%async_computation | async-start | bytes 5242880 | tf_op jit(solution)/shard_map/all_gather | solution.py:57
  8.3 17.3 %copy-start.17 = (bf16[2,3,2,128]{3,2,1,0:T(2,128)(2,1)S(1)}, bf16[2,3,2,128]{3,2,1,0:T(2,128)(2,1)}, u32[]{:S(2)}) copy-start(bf16[2,3,2,128]{3,2,1,0:T(2,128)(2,1)} %param.32) | copy-start | bytes 9220
  8.3 17.3 %copy-start.15 = (f32[1024]{0:T(1024)S(1)}, f32[1024]{0:T(1024)}, u32[]{:S(2)}) copy-start(f32[1024]{0:T(1024)} %param.23) | copy-start | bytes 12292
  8.3 17.3 %copy-start.19 = (f32[2,128]{1,0:T(2,128)S(1)}, f32[2,128]{1,0:T(2,128)}, u32[]{:S(2)}) copy-start(f32[2,128]{1,0:T(2,128)} %param.25) | copy-start | bytes 3076
  8.3 17.4 %copy-start.13 = (f32[4,1024]{1,0:T(4,128)S(1)}, f32[4,1024]{1,0:T(4,128)}, u32[]{:S(2)}) copy-start(f32[4,1024]{1,0:T(4,128)} %param.22) | copy-start | bytes 49156
  8.4 17.7 %copy-start.16 = (f32[4,2,128]{2,1,0:T(2,128)S(1)}, f32[4,2,128]{2,1,0:T(2,128)}, u32[]{:S(2)}) copy-start(f32[4,2,128]{2,1,0:T(2,128)} %param.24) | copy-start | bytes 12292
  8.4 17.8 %copy-start.22 = (f32[16]{0:T(128)S(1)}, f32[16]{0:T(128)}, u32[]{:S(2)}) copy-start(f32[16]{0:T(128)} %param.26) | copy-start | bytes 196
  59.8 15.9 %copy-start.6 = (bf16[512,4096]{1,0:T(8,128)(2,1)S(1)}, bf16[512,4096]{1,0:T(8,128)(2,1)}, u32[]{:S(2)}) copy-start(bf16[512,4096]{1,0:T(8,128)(2,1)} %all-gather.2.cloned.1.call-done) | copy-start | bytes 12582916
  75.5 3.6 %copy-start.2 = (bf16[512,2048]{1,0:T(8,128)(2,1)}, bf16[512,2048]{1,0:T(8,128)(2,1)S(1)}, u32[]{:S(2)}) copy-start(bf16[512,2048]{1,0:T(8,128)(2,1)S(1)} %convolution_convert_fusion) | copy-start | bytes 6291460
  75.5 2.4 %copy-start.20 = (bf16[4096,2,128]{2,1,0:T(2,128)(2,1)S(1)}, bf16[4096,2,128]{2,1,0:T(2,128)(2,1)}, u32[]{:S(2)}) copy-start(bf16[4096,2,128]{2,1,0:T(2,128)(2,1)} %param.20) | copy-start | bytes 6291460
  79.1 0.9 copy-start.12
  79.3 1.9 copy-start.18
  79.3 6.7 %copy-start.21 = (bf16[2,3,1024]{2,0,1:T(2,128)(2,1)S(1)}, bf16[2,3,1024]{2,0,1:T(2,128)(2,1)}, u32[]{:S(2)}) copy-start(bf16[2,3,1024]{2,0,1:T(2,128)(2,1)} %param.31) | copy-start | bytes 36868
  79.3 6.7 %collective-permute-start = (bf16[2,3,1280]{2,0,1:T(2,128)(2,1)S(1)}, bf16[2,3,1280]{2,0,1:T(2,128)(2,1)S(1)}, u32[]{:S(2)}, u32[]{:S(2)}) collective-permute-start(bf16[2,3,1280]{2,0,1:T(2,128)(2,1)S(1)} %copy.107), channel_id=1, source_target_pairs={{0,4},{4,8},{8,12},{12,16},{16,20},{20,24},{24,28},{28,32},{32,36}... | collective-permute-start | bytes 46088 | tf_op jit(solution)/shard_map/ppermute | solution.py:17
  88.3 1.4 copy-start.1
  100.0 3.4 %collective-permute-start.5 = (f32[16,64,128]{2,1,0:T(8,128)}, f32[16,64,128]{2,1,0:T(8,128)}, u32[]{:S(2)}, u32[]{:S(2)}) collective-permute-start(f32[16,64,128]{2,1,0:T(8,128)} %bitcast.16), channel_id=1, source_target_pairs={{0,4},{4,0},{8,12},{12,8},{16,20},{20,16},{24,28},{28,24},{32,36},... | collective-permute-start | bytes 1572872 | tf_op jit(solution)/shard_map/ppermute | solution.py:133
  100.2 2.1 collective-permute-start.1
  103.4 0.8 copy-start.4
  106.2 17.6 %collective-permute-start.6 = (f32[16,64,128]{2,1,0:T(8,128)}, f32[16,64,128]{2,1,0:T(8,128)}, u32[]{:S(2)}, u32[]{:S(2)}) collective-permute-start(f32[16,64,128]{2,1,0:T(8,128)} %fusion.30), channel_id=1, source_target_pairs={{0,8},{4,12},{8,16},{12,20},{16,24},{20,28},{24,32},{28,36},{32,40... | collective-permute-start | bytes 1572872 | tf_op jit(solution)/shard_map/ppermute | solution.py:17
  126.8 17.1 %collective-permute-start.7 = (f32[16,64,128]{2,1,0:T(8,128)}, f32[16,64,128]{2,1,0:T(8,128)}, u32[]{:S(2)}, u32[]{:S(2)}) collective-permute-start(f32[16,64,128]{2,1,0:T(8,128)} %multiply_add_fusion.3), channel_id=1, source_target_pairs={{0,16},{4,20},{8,24},{12,28},{16,32},{20,36},{24,40},{28,44},{32,4... | collective-permute-start | bytes 1572872 | tf_op jit(solution)/shard_map/ppermute | solution.py:17
  126.8 13.5 %collective-permute-start.2 = (f32[16]{0:T(128)S(1)}, f32[16]{0:T(128)S(1)}, u32[]{:S(2)}, u32[]{:S(2)}) collective-permute-start(f32[16]{0:T(128)S(1)} %get-tuple-element.18), channel_id=1, source_target_pairs={{0,8},{4,12},{8,16},{12,20},{16,24},{20,28},{24,32},{28,36},{32,40... | collective-permute-start | bytes 200 | tf_op jit(solution)/shard_map/ppermute | solution.py:17
  144.8 0.7 copy-start.8
  147.5 13.8 %collective-permute-start.8 = (f32[16,64,128]{2,1,0:T(8,128)}, f32[16,64,128]{2,1,0:T(8,128)}, u32[]{:S(2)}, u32[]{:S(2)}) collective-permute-start(f32[16,64,128]{2,1,0:T(8,128)} %multiply_add_fusion.2), channel_id=1, source_target_pairs={{0,32},{4,36},{8,40},{12,44},{16,48},{20,52},{24,56},{28,60},{32,6... | collective-permute-start | bytes 1572872 | tf_op jit(solution)/shard_map/ppermute | solution.py:17
  147.5 11.7 %collective-permute-start.3 = (f32[16]{0:T(128)S(1)}, f32[16]{0:T(128)S(1)}, u32[]{:S(2)}, u32[]{:S(2)}) collective-permute-start(f32[16]{0:T(128)S(1)} %get-tuple-element.16), channel_id=1, source_target_pairs={{0,16},{4,20},{8,24},{12,28},{16,32},{20,36},{24,40},{28,44},{32,4... | collective-permute-start | bytes 200 | tf_op jit(solution)/shard_map/ppermute | solution.py:17
  162.2 0.7 copy-start.9
  165.0 14.8 %collective-permute-start.9 = (f32[16,64,128]{2,1,0:T(8,128)}, f32[16,64,128]{2,1,0:T(8,128)}, u32[]{:S(2)}, u32[]{:S(2)}) collective-permute-start(f32[16,64,128]{2,1,0:T(8,128)} %multiply_add_fusion.1), channel_id=1, source_target_pairs={{0,64},{4,68},{8,72},{12,76},{16,80},{20,84},{24,88},{28,92},{32,9... | collective-permute-start | bytes 1572872 | tf_op jit(solution)/shard_map/ppermute | solution.py:17
  165.0 9.5 %collective-permute-start.4 = (f32[16]{0:T(128)S(1)}, f32[16]{0:T(128)S(1)}, u32[]{:S(2)}, u32[]{:S(2)}) collective-permute-start(f32[16]{0:T(128)S(1)} %fusion.55), channel_id=1, source_target_pairs={{0,32},{4,36},{8,40},{12,44},{16,48},{20,52},{24,56},{28,60},{32,6... | collective-permute-start | bytes 200 | tf_op jit(solution)/shard_map/ppermute | solution.py:17
  174.6 5.1 %collective-permute-start.10 = (f32[16]{0:T(128)S(1)}, f32[16]{0:T(128)S(1)}, u32[]{:S(2)}, u32[]{:S(2)}) collective-permute-start(f32[16]{0:T(128)S(1)} %fusion.52), channel_id=1, source_target_pairs={{0,64},{4,68},{8,72},{12,76},{16,80},{20,84},{24,88},{28,92},{32,9... | collective-permute-start | bytes 200 | tf_op jit(solution)/shard_map/ppermute | solution.py:17
  180.8 2.5 %copy-start.5 = (f32[2,8,64,128]{3,2,1,0:T(8,128)S(1)}, f32[2,8,64,128]{3,2,1,0:T(8,128)}, u32[]{:S(2)}) copy-start(f32[2,8,64,128]{3,2,1,0:T(8,128)} %copy-done.4) | copy-start | bytes 1572868
  184.5 4.6 %collective-permute-start.11 = (f32[16,64,128]{2,1,0:T(8,128)}, f32[16,64,128]{2,1,0:T(8,128)}, u32[]{:S(2)}, u32[]{:S(2)}) collective-permute-start(f32[16,64,128]{2,1,0:T(8,128)} %get-tuple-element.22), channel_id=1, source_target_pairs={{0,4},{4,0},{8,12},{12,8},{16,20},{20,16},{24,28},{28,24},{32,36},... | collective-permute-start | bytes 1572872 | tf_op jit(solution)/shard_map/ppermute | solution.py:155
  186.4 4.2 %copy-start.11 = (f32[2,16,64,128]{3,0,2,1:T(2,128)S(1)}, f32[2,16,64,128]{3,0,2,1:T(2,128)}, u32[]{:S(2)}) copy-start(f32[2,16,64,128]{3,0,2,1:T(2,128)} %get-tuple-element.39) | copy-start | bytes 3145732
  191.4 2.1 copy-start.7
  191.4 2.1 copy-start.10
  191.4 2.1 copy-start.23
  203.4 2.1 copy-start.3
  203.5 2.1 copy-start.14
Sparse Core Ops, SparseCore 0:
  9.0 50.7 all-gather.1

commit v5 on v4

--- a/solution.py
+++ b/solution.py
@@ -62,7 +62,14 @@
     bc = bc_sum.astype(jnp.bfloat16)
     gate = zx[:, :inner_dev]
     mixin = jnp.concatenate([zx[:, inner_dev:], bc], axis=1).reshape(blocks, BLOCK, channels)
-    own_tails = mixin[:, BLOCK - (KERNEL - 1) :, :]
+    tail_rows = piece.reshape(blocks, BLOCK, WIDTH)[:, BLOCK - (KERNEL - 1) :, :]
+    own_tails = jnp.concatenate(
+        [
+            jnp.einsum("ckw,wz->ckz", tail_rows, w_zx[:, 1, :], preferred_element_type=jnp.float32),
+            jnp.einsum("ckw,wz->ckz", tail_rows, flat_bc, preferred_element_type=jnp.float32),
+        ],
+        axis=2,
+    ).astype(jnp.bfloat16)
     arrived = from_behind(own_tails, "seq", 1)
     wrapped = jnp.concatenate([jnp.zeros_like(arrived[:1]), arrived[:-1]], axis=0)
     before = jnp.where(place > 0, arrived, wrapped)
@@ -125,8 +132,8 @@
     rows = blocks * half
 
     def keep(part, at):
-        piece = lax.dynamic_slice_in_dim(part, at * half, half, axis=1)
-        return piece.reshape((rows,) + part.shape[2:])
+        chosen = jnp.where(at == 0, part[:, :half], part[:, half:])
+        return chosen.reshape((rows,) + part.shape[2:])
 
     pair = [(source, source ^ 1) for source in range(devices)]
     mine = (keep(step_a, core), keep(step_b, core))
@@ -162,11 +169,11 @@
     )
     state_in = jnp.where(first[:, None, None, None], bank_state, previous)
     read = jnp.einsum(
-        "cqgn,cgjpn->cqgjp",
+        "cqgn,cgmn->cqgm",
         cq.astype(jnp.float32),
-        state_in.reshape(blocks, groups_dev, per_group, HEAD_DIM, STATE),
+        state_in.reshape(blocks, groups_dev, per_group * HEAD_DIM, STATE),
         precision=lax.Precision.HIGHEST,
-    )
+    ).reshape(blocks, BLOCK, groups_dev, per_group, HEAD_DIM)
     growth = jnp.exp(cum).reshape(blocks, BLOCK, groups_dev, per_group, 1)
     skip = d_skip.reshape(1, 1, groups_dev, per_group, 1)
     y_total = y_intra + growth * read + skip * xs.astype(jnp.float32)

time: 218 us -> 225 us (1.032)
  waiting for transfers between devices: 97.6 us -> 70.6 us
  local copies, waits for them, and re-layouts: 44.1 us -> 65.6 us
  matrix products: 30.7 us -> 39 us
  starting transfers between devices: 4.6 us -> 7.56 us
    all_gather x1, waiting for transfers between devices: 33.6 us -> 10.1 us  [per_device(): piece = lax.all_gather(hidden, 'mp', axis=1, tiled=True)]
    slice x2, local copies, waits for them, and re-layouts: 0.17 us -> 20.5 us  [the longest x1 20.4 us: per_device(): w_zx[:, 1, :]]
    dot_general x1 -> x3, matrix products: 2.06 us -> 12.7 us  [the longest x1 8.58 us: per_device(): jnp.einsum('ckw,wz->ckz', tail_rows, w_zx[:, 1, :], preferred_element_typ...]
    dot_general x1, matrix products: 15.7 us -> 11.2 us  [per_device(): zx_sum = jnp.dot(piece, flat_zx, preferred_element_type=jnp.float32)]
    ppermute x9, waiting for transfers between devices: 61.8 us -> 58.2 us  [from_behind(): return lax.ppermute(value, axis, pairs)]
    reshape x2 -> x3, local copies, waits for them, and re-layouts: 0.16 us -> 3.34 us  [the longest x1 3.17 us: per_device(): flat_bc = w_bc.reshape(WIDTH, 2 * gstate_dev)]
    dynamic_slice x4 -> x0, local copies, waits for them, and re-layouts: 2.89 us -> none  [keep(): piece = lax.dynamic_slice_in_dim(part, at * half, half, axis=1)]
    unnamed x52 -> x53, local copies, waits for them, and re-layouts: 22.3 us -> 20.9 us
  transfers between devices with their start and end apart: 13 -> 13, of which waited for: 10 -> 9; matrix products, arithmetic and copies ran while one was open for 13% -> 30% of each run, Pallas kernels for 0% -> 0%
where the time goes in v5:
time: 225 us; the launch traced here: 221 us
  waiting for transfers between devices  70.6 us (31%)
  local copies, waits for them, and re-layouts  65.6 us (29%)
  matrix products  39 us (17%)
  other arithmetic  24.4 us (11%)
  between operations  14 us (6%)
  starting transfers between devices  7.56 us (3%)
    ppermute x9, waiting for transfers between devices, from_behind(): return lax.ppermute(value, axis, pairs)  58.2 us
    unnamed x53, local copies, waits for them, and re-layouts  20.9 us
    slice x1, local copies, waits for them, and re-layouts, per_device(): w_zx[:, 1, :]  20.4 us
    dot_general x1, matrix products, per_device(): zx_sum = jnp.dot(piece, flat_zx, preferred_element_type=jnp.float32)  11.2 us
    all_gather x1, waiting for transfers between devices, per_device(): piece = lax.all_gather(hidden, 'mp', axis=1, tiled=True)  10.1 us
    add x5, other arithmetic, combine(): later[0][:, None, None] * earlier[1] + later[1]  9.41 us
    dot_general x1, matrix products, per_device(): jnp.einsum('ckw,wz->ckz', tail_rows, w_zx[:, 1, :], preferred_element_typ...  8.58 us
    reshape x2, local copies, waits for them, and re-layouts, per_device(): y_total.reshape(rows_dev, inner_dev) * jax.nn.silu(gate.astype(jnp.float32))  7.28 us
  transfers between devices with their start and end apart: 13, of which 9 were waited for; matrix products, arithmetic and copies ran while one was open for 30% of the time, Pallas kernels for 0%

profile of v5, /device:TPU:0, one launch (start us, length us, event | category | flops | bytes accessed | tf_op | source)
XLA Modules:
  0.0 221.0 jit_solution(8625480417685713877)
XLA Ops:
  6.5 0.7 all-gather.2.cloned.1.call-update
  7.3 0.9 select_reduce_fusion
  8.3 20.4 %slice.110 = bf16[4096,1,1024]{2,1,0:T(2,128)(2,1)} slice(bf16[4096,2,1024]{2,1,0:T(2,128)(2,1)} %param.19), slice={[0:4096], [1:2], [0:1024]} | slice | bytes 16777216 | tf_op jit(solution)/shard_map/slice | solution.py:68
  28.7 3.2 %reshape.281 = bf16[4096,256,1]{1,0,2:T(8,128)(2,1)S(1)} reshape(bf16[4096,2,128]{2,1,0:T(2,128)(2,1)} %param.20) | data formatting | bytes 4194304 | tf_op jit(solution)/shard_map/reshape | solution.py:56
  32.0 17.2 %copy.141 = bf16[512,8,2,1024]{3,1,2,0:T(8,128)(2,1)} copy(bf16[512,8,2,1024]{3,2,1,0:T(2,128)(2,1)} %bitcast.121) | data formatting | bytes 33554432
  49.2 0.2 compare_reduce_fusion
  49.7 10.1 %all-gather.2.cloned.1.call-done = bf16[512,4096]{1,0:T(8,128)(2,1)} async-done(((bf16[512,1024]{1,0:T(8,128)(2,1)}), bf16[512,4096]{1,0:T(8,128)(2,1)}) %all-gather.2.cloned.1.call-update) | async-done | bytes 4194320 | tf_op jit(solution)/shard_map/all_gather | solution.py:57
  59.7 8.6 %fusion = bf16[2,3,1024]{2,1,0:T(4,128)(2,1)S(1)} fusion(bf16[4096,1,1024]{2,1,0:T(2,128)(2,1)} %slice.110, bf16[2,256,4096]{2,1,0:T(8,128)(2,1)} %bitcast.124), kind=kOutput, calls=%fused_computation.1 | convolution fusion | flops 50331648 | bytes 16855040 | tf_op jit(solution)/shard_map/ckw,wz->ckz/dot_general | solution.py:68
  68.3 2.1 fusion.40
  70.4 0.3 collective-permute-start
  70.7 11.2 %convolution_convert_fusion = bf16[512,2048]{1,0:T(8,128)(2,1)S(1)} fusion(bf16[512,4096]{1,0:T(8,128)(2,1)} %all-gather.2.cloned.1.call-done, bf16[4096,2048]{1,0:T(8,128)(2,1)S(1)} %bitcast.122), kind=kOutput, calls=%fused_computation.10 | convolution fusion | flops 8590983168 | bytes 23068672 | tf_op jit(solution)/shard_map/dot_general | solution.py:58
  82.0 1.0 copy-done.14
  83.0 1.2 fusion.66
  84.3 1.2 reduce-window.18
  86.1 3.5 %fusion.20 = bf16[512,256]{1,0:T(8,128)(2,1)S(1)} fusion(bf16[512,4096]{1,0:T(8,128)(2,1)} %all-gather.2.cloned.1.call-done, bf16[512,8,2,128]{3,2,1,0:T(2,128)(2,1)S(1)} %bitcast.130), kind=kOutput, calls=%fused_computation.37 | convolution fusion | flops 1073872896 | bytes 6553600 | tf_op jit(solution)/shard_map/dot_general | solution.py:59
  89.9 0.4 copy-done.22
  90.3 0.2 broadcast_select_fusion.2
  90.5 0.3 maximum_convert_fusion
  90.8 1.7 multiply_convert_fusion.2
  92.6 1.4 fusion.64
  94.0 2.3 %copy.115 = bf16[2,256,1024]{1,2,0:T(8,128)(2,1)} copy(bf16[2,256,1024]{2,1,0:T(8,128)(2,1)} %get-tuple-element.23) | data formatting | bytes 2097152 | tf_op jit(solution)/shard_map/slice | solution.py:102
  96.2 1.7 fusion.23
  97.9 4.6 %copy_add_fusion = (f32[2,16,64,128]{3,0,2,1:T(2,128)S(1)}, f32[2,16,64,128]{3,0,2,1:T(2,128)}) fusion(f32[2,16,64,128]{3,2,1,0:T(8,128)S(1)} %fusion.23, pred[2]{0:T(512)(128)(4,1)S(1)} %compare_reduce_fusion, f32[2,16]{0,1:T(8,128)S(1)} %copy.120, f32[2,16,64,128]{3,2,1,0:T(8,128)S(1)} %copy-done, s32[2]{0:T(128)S(1)} %fusion.48), kind=kOutput, calls=%fused_computation.43 | convolution fusion | flops 7077892 | bytes 4194442 | tf_op jit(solution)/shard_map/cr,rhpn->chpn/dot_general | solution.py:89
  102.5 1.2 broadcast_select_fusion.1
  103.7 0.9 copy.123
  104.5 1.6 collective-permute-start.5
  106.4 1.6 collective-permute-done.1
  108.1 1.1 copy.122
  109.2 0.8 copy-done.5
  109.9 2.0 fusion.30
  112.0 1.5 collective-permute-start.6
  113.5 16.3 %collective-permute-done.6 = f32[16,64,128]{2,1,0:T(8,128)} collective-permute-done((f32[16,64,128]{2,1,0:T(8,128)}, f32[16,64,128]{2,1,0:T(8,128)}, u32[]{:S(2)}, u32[]{:S(2)}) %collective-permute-start.6) | collective-permute-done | bytes 524320 | tf_op jit(solution)/shard_map/ppermute | solution.py:17
  129.8 1.0 slice.163
  130.8 2.0 multiply_add_fusion.3
  132.8 0.3 collective-permute-start.2
  133.1 14.4 %collective-permute-done.2 = f32[16]{0:T(128)S(1)} collective-permute-done((f32[16]{0:T(128)S(1)}, f32[16]{0:T(128)S(1)}, u32[]{:S(2)}, u32[]{:S(2)}) %collective-permute-start.2) | collective-permute-done | bytes 96 | tf_op jit(solution)/shard_map/ppermute | solution.py:17
  147.6 2.5 %collective-permute-done.7 = f32[16,64,128]{2,1,0:T(8,128)} collective-permute-done((f32[16,64,128]{2,1,0:T(8,128)}, f32[16,64,128]{2,1,0:T(8,128)}, u32[]{:S(2)}, u32[]{:S(2)}) %collective-permute-start.7) | collective-permute-done | bytes 524320 | tf_op jit(solution)/shard_map/ppermute | solution.py:17
  150.1 1.0 slice.164
  151.1 0.7 copy-done.9
  151.7 2.0 multiply_add_fusion.2
  153.7 11.9 %collective-permute-done.3 = f32[16]{0:T(128)S(1)} collective-permute-done((f32[16]{0:T(128)S(1)}, f32[16]{0:T(128)S(1)}, u32[]{:S(2)}, u32[]{:S(2)}) %collective-permute-start.3) | collective-permute-done | bytes 96 | tf_op jit(solution)/shard_map/ppermute | solution.py:17
  165.8 2.0 collective-permute-done.8
  167.7 1.0 slice.165
  168.7 0.7 copy-done.10
  169.4 2.0 multiply_add_fusion.1
  171.4 0.6 collective-permute-start.4
  172.0 9.2 %collective-permute-done.4 = f32[16]{0:T(128)S(1)} collective-permute-done((f32[16]{0:T(128)S(1)}, f32[16]{0:T(128)S(1)}, u32[]{:S(2)}, u32[]{:S(2)}) %collective-permute-start.4) | collective-permute-done | bytes 96 | tf_op jit(solution)/shard_map/ppermute | solution.py:17
  181.2 3.3 %collective-permute-start.10 = (f32[16]{0:T(128)S(1)}, f32[16]{0:T(128)S(1)}, u32[]{:S(2)}, u32[]{:S(2)}) collective-permute-start(f32[16]{0:T(128)S(1)} %fusion.54), channel_id=1, source_target_pairs={{0,64},{4,68},{8,72},{12,76},{16,80},{20,84},{24,88},{28,92},{32,9... | collective-permute-start | bytes 200 | tf_op jit(solution)/shard_map/ppermute | solution.py:17
  184.5 1.8 collective-permute-done.10
  186.5 1.0 slice.166
  187.5 1.4 add_add_fusion
  188.8 1.1 fusion.65
  189.9 1.2 fusion.32
  191.2 2.1 copy.129
  193.3 1.3 fusion.36
  194.6 1.4 copy.124
  196.0 1.4 copy.125
  197.5 0.8 fusion.24
  198.4 2.1 fusion.25
  200.5 2.6 %fusion.19 = f32[2,256,1,16,64]{1,4,3,0,2:T(8,128)S(1)} fusion(f32[2,256,1,16,64]{1,4,3,0,2:T(8,128)S(1)} %bitcast.131, f32[2,256,1,16,64]{1,4,3,0,2:T(8,128)S(1)} %bitcast.132, bf16[2,256,16,64]{1,3,2,0:T(8,128)(2,1)S(1)} %bitcast.128, f32[2,16,256]{2,1,0:T(8,128)S(1)} %get-tuple-element.29, f32[2,16,256]{2,1,0:T(8,128)S(1)} %get-tuple-element.32, ...), kind=kOutput, calls=%fused_computation.31 | convolution fusion | flops 281018368 | bytes 8028224 | tf_op jit(solution)/shard_map/cgjqk,ckgjp->cqgjp/dot_general | solution.py:116
  203.1 3.8 %copy.135 = f32[2,256,1,16,64]{4,3,1,0,2:T(8,128)} copy(f32[2,256,1,16,64]{1,4,3,0,2:T(8,128)S(1)} %fusion.19) | data formatting | bytes 4194304 | tf_op jit(solution)/shard_map/reshape | solution.py:180
  206.9 3.5 %reshape.285 = f32[512,1024]{1,0:T(8,128)S(1)} reshape(f32[2,256,1,16,64]{4,3,1,0,2:T(8,128)} %copy.135) | data formatting | bytes 4194304 | tf_op jit(solution)/shard_map/reshape | solution.py:180
  210.4 2.1 multiply_reduce_fusion
  212.5 1.7 multiply_convert_fusion.3
  (94 shorter events, 2.2 us)
Async XLA Ops:
  6.5 91.3 %copy-start = (f32[2,16,64,128]{3,2,1,0:T(8,128)S(1)}, f32[2,16,64,128]{3,2,1,0:T(8,128)}, u32[]{:S(2)}) copy-start(f32[2,16,64,128]{3,2,1,0:T(8,128)} %param.30) | copy-start | bytes 3145732
  6.5 53.2 %all-gather.2.cloned.1.call-start = ((), (), s32[]{:S(2)}) async-start(), calls=%async_computation | async-start | bytes 5242880 | tf_op jit(solution)/shard_map/all_gather | solution.py:57
  28.7 3.2 %copy-start.19 = (bf16[2,3,2,128]{3,2,1,0:T(2,128)(2,1)S(1)}, bf16[2,3,2,128]{3,2,1,0:T(2,128)(2,1)}, u32[]{:S(2)}) copy-start(bf16[2,3,2,128]{3,2,1,0:T(2,128)(2,1)} %param.32) | copy-start | bytes 9220
  31.9 17.2 %copy-start.17 = (f32[1024]{0:T(1024)S(1)}, f32[1024]{0:T(1024)}, u32[]{:S(2)}) copy-start(f32[1024]{0:T(1024)} %param.23) | copy-start | bytes 12292
  31.9 17.2 %copy-start.21 = (f32[2,128]{1,0:T(2,128)S(1)}, f32[2,128]{1,0:T(2,128)}, u32[]{:S(2)}) copy-start(f32[2,128]{1,0:T(2,128)} %param.25) | copy-start | bytes 3076
  31.9 17.2 %copy-start.15 = (f32[4,1024]{1,0:T(4,128)S(1)}, f32[4,1024]{1,0:T(4,128)}, u32[]{:S(2)}) copy-start(f32[4,1024]{1,0:T(4,128)} %param.22) | copy-start | bytes 49156
  32.0 17.6 %copy-start.18 = (f32[4,2,128]{2,1,0:T(2,128)S(1)}, f32[4,2,128]{2,1,0:T(2,128)}, u32[]{:S(2)}) copy-start(f32[4,2,128]{2,1,0:T(2,128)} %param.24) | copy-start | bytes 12292
  32.0 17.7 %copy-start.23 = (f32[16]{0:T(128)S(1)}, f32[16]{0:T(128)}, u32[]{:S(2)}) copy-start(f32[16]{0:T(128)} %param.26) | copy-start | bytes 196
  59.7 11.0 %copy-start.1 = (bf16[512,8,2,1024]{3,1,2,0:T(8,128)(2,1)S(1)}, bf16[512,8,2,1024]{3,1,2,0:T(8,128)(2,1)}, u32[]{:S(2)}) copy-start(bf16[512,8,2,1024]{3,1,2,0:T(8,128)(2,1)} %copy.141) | copy-start | bytes 50331652
  70.4 19.4 %collective-permute-start = (bf16[2,3,1280]{2,0,1:T(2,128)(2,1)S(1)}, bf16[2,3,1280]{2,0,1:T(2,128)(2,1)S(1)}, u32[]{:S(2)}, u32[]{:S(2)}) collective-permute-start(bf16[2,3,1280]{2,0,1:T(2,128)(2,1)S(1)} %pad_maximum_fusion.4), channel_id=1, source_target_pairs={{0,4},{4,8},{8,12},{12,16},{16,20},{20,24},{24,28},{28,32},{32,36}... | collective-permute-start | bytes 46088 | tf_op jit(solution)/shard_map/ppermute | solution.py:17
  70.7 11.2 %copy-start.7 = (bf16[512,4096]{1,0:T(8,128)(2,1)S(1)}, bf16[512,4096]{1,0:T(8,128)(2,1)}, u32[]{:S(2)}) copy-start(bf16[512,4096]{1,0:T(8,128)(2,1)} %all-gather.2.cloned.1.call-done) | copy-start | bytes 12582916
  81.9 2.2 %copy-start.3 = (bf16[512,2048]{1,0:T(8,128)(2,1)}, bf16[512,2048]{1,0:T(8,128)(2,1)S(1)}, u32[]{:S(2)}) copy-start(bf16[512,2048]{1,0:T(8,128)(2,1)S(1)} %convolution_convert_fusion) | copy-start | bytes 6291460
  82.0 1.0 copy-start.14
  83.0 1.2 copy-start.20
  83.0 3.0 %copy-start.11 = (bf16[4096,2,128]{2,1,0:T(2,128)(2,1)S(1)}, bf16[4096,2,128]{2,1,0:T(2,128)(2,1)}, u32[]{:S(2)}) copy-start(bf16[4096,2,128]{2,1,0:T(2,128)(2,1)} %param.20) | copy-start | bytes 6291460
  86.0 3.5 %slice-start = ((bf16[512,2048]{1,0:T(8,128)(2,1)}), bf16[512,1024]{1,0:T(8,128)(2,1)S(1)}, s32[]{:S(2)}) async-start(bf16[512,2048]{1,0:T(8,128)(2,1)} %copy-done.3), calls=%async_computation.1 | async-start | bytes 2097152 | tf_op jit(solution)/shard_map/slice | solution.py:64
  89.6 0.7 copy-start.22
  92.5 1.4 copy-start.2
  104.5 4.6 %collective-permute-start.5 = (f32[16,64,128]{2,1,0:T(8,128)}, f32[16,64,128]{2,1,0:T(8,128)}, u32[]{:S(2)}, u32[]{:S(2)}) collective-permute-start(f32[16,64,128]{2,1,0:T(8,128)} %bitcast.19), channel_id=1, source_target_pairs={{0,4},{4,0},{8,12},{12,8},{16,20},{20,16},{24,28},{28,24},{32,36},... | collective-permute-start | bytes 1572872 | tf_op jit(solution)/shard_map/ppermute | solution.py:140
  106.3 1.7 collective-permute-start.1
  109.2 0.8 copy-start.5
  112.0 17.8 %collective-permute-start.6 = (f32[16,64,128]{2,1,0:T(8,128)}, f32[16,64,128]{2,1,0:T(8,128)}, u32[]{:S(2)}, u32[]{:S(2)}) collective-permute-start(f32[16,64,128]{2,1,0:T(8,128)} %fusion.30), channel_id=1, source_target_pairs={{0,8},{4,12},{8,16},{12,20},{16,24},{20,28},{24,32},{28,36},{32,40... | collective-permute-start | bytes 1572872 | tf_op jit(solution)/shard_map/ppermute | solution.py:17
  132.8 17.3 %collective-permute-start.7 = (f32[16,64,128]{2,1,0:T(8,128)}, f32[16,64,128]{2,1,0:T(8,128)}, u32[]{:S(2)}, u32[]{:S(2)}) collective-permute-start(f32[16,64,128]{2,1,0:T(8,128)} %multiply_add_fusion.3), channel_id=1, source_target_pairs={{0,16},{4,20},{8,24},{12,28},{16,32},{20,36},{24,40},{28,44},{32,4... | collective-permute-start | bytes 1572872 | tf_op jit(solution)/shard_map/ppermute | solution.py:17
  132.8 14.7 %collective-permute-start.2 = (f32[16]{0:T(128)S(1)}, f32[16]{0:T(128)S(1)}, u32[]{:S(2)}, u32[]{:S(2)}) collective-permute-start(f32[16]{0:T(128)S(1)} %get-tuple-element.18), channel_id=1, source_target_pairs={{0,8},{4,12},{8,16},{12,20},{16,24},{20,28},{24,32},{28,36},{32,40... | collective-permute-start | bytes 200 | tf_op jit(solution)/shard_map/ppermute | solution.py:17
  151.0 0.7 copy-start.9
  153.7 14.0 %collective-permute-start.8 = (f32[16,64,128]{2,1,0:T(8,128)}, f32[16,64,128]{2,1,0:T(8,128)}, u32[]{:S(2)}, u32[]{:S(2)}) collective-permute-start(f32[16,64,128]{2,1,0:T(8,128)} %multiply_add_fusion.2), channel_id=1, source_target_pairs={{0,32},{4,36},{8,40},{12,44},{16,48},{20,52},{24,56},{28,60},{32,6... | collective-permute-start | bytes 1572872 | tf_op jit(solution)/shard_map/ppermute | solution.py:17
  153.7 12.0 %collective-permute-start.3 = (f32[16]{0:T(128)S(1)}, f32[16]{0:T(128)S(1)}, u32[]{:S(2)}, u32[]{:S(2)}) collective-permute-start(f32[16]{0:T(128)S(1)} %get-tuple-element.16), channel_id=1, source_target_pairs={{0,16},{4,20},{8,24},{12,28},{16,32},{20,36},{24,40},{28,44},{32,4... | collective-permute-start | bytes 200 | tf_op jit(solution)/shard_map/ppermute | solution.py:17
  168.7 0.7 copy-start.10
  171.4 15.1 %collective-permute-start.9 = (f32[16,64,128]{2,1,0:T(8,128)}, f32[16,64,128]{2,1,0:T(8,128)}, u32[]{:S(2)}, u32[]{:S(2)}) collective-permute-start(f32[16,64,128]{2,1,0:T(8,128)} %multiply_add_fusion.1), channel_id=1, source_target_pairs={{0,64},{4,68},{8,72},{12,76},{16,80},{20,84},{24,88},{28,92},{32,9... | collective-permute-start | bytes 1572872 | tf_op jit(solution)/shard_map/ppermute | solution.py:17
  171.4 9.7 %collective-permute-start.4 = (f32[16]{0:T(128)S(1)}, f32[16]{0:T(128)S(1)}, u32[]{:S(2)}, u32[]{:S(2)}) collective-permute-start(f32[16]{0:T(128)S(1)} %fusion.57), channel_id=1, source_target_pairs={{0,32},{4,36},{8,40},{12,44},{16,48},{20,52},{24,56},{28,60},{32,6... | collective-permute-start | bytes 200 | tf_op jit(solution)/shard_map/ppermute | solution.py:17
  181.2 5.1 %collective-permute-start.10 = (f32[16]{0:T(128)S(1)}, f32[16]{0:T(128)S(1)}, u32[]{:S(2)}, u32[]{:S(2)}) collective-permute-start(f32[16]{0:T(128)S(1)} %fusion.54), channel_id=1, source_target_pairs={{0,64},{4,68},{8,72},{12,76},{16,80},{20,84},{24,88},{28,92},{32,9... | collective-permute-start | bytes 200 | tf_op jit(solution)/shard_map/ppermute | solution.py:17
  187.4 2.5 %copy-start.6 = (f32[2,8,64,128]{3,2,1,0:T(8,128)S(1)}, f32[2,8,64,128]{3,2,1,0:T(8,128)}, u32[]{:S(2)}) copy-start(f32[2,8,64,128]{3,2,1,0:T(8,128)} %copy-done.5) | copy-start | bytes 1572868
  191.2 4.9 %collective-permute-start.11 = (f32[16,64,128]{2,1,0:T(8,128)}, f32[16,64,128]{2,1,0:T(8,128)}, u32[]{:S(2)}, u32[]{:S(2)}) collective-permute-start(f32[16,64,128]{2,1,0:T(8,128)} %get-tuple-element.22), channel_id=1, source_target_pairs={{0,4},{4,0},{8,12},{12,8},{16,20},{20,16},{24,28},{28,24},{32,36},... | collective-permute-start | bytes 1572872 | tf_op jit(solution)/shard_map/ppermute | solution.py:162
  193.3 4.2 %copy-start.13 = (f32[2,16,64,128]{3,0,2,1:T(2,128)S(1)}, f32[2,16,64,128]{3,0,2,1:T(2,128)}, u32[]{:S(2)}) copy-start(f32[2,16,64,128]{3,0,2,1:T(2,128)} %get-tuple-element.39) | copy-start | bytes 3145732
  198.3 2.1 copy-start.8
  198.3 2.1 copy-start.12
  198.4 2.1 copy-start.24
  210.4 2.1 copy-start.4
  210.4 2.1 copy-start.16
Sparse Core Ops, SparseCore 0:
  9.0 50.6 all-gather.1

commit v6 on v4

--- a/solution.py
+++ b/solution.py
@@ -133,23 +133,51 @@
     got = lax.ppermute((keep(step_a, 1 - core), keep(step_b, 1 - core)), "seq", pair)
     early = jax.tree.map(lambda own, other: jnp.where(core == 0, own, other), mine, got)
     later = jax.tree.map(lambda own, other: jnp.where(core == 0, other, own), mine, got)
-    run_a, run_b = combine(early, later)
-    prior_a, prior_b = jnp.ones_like(run_a), jnp.zeros_like(run_b)
-
-    def wrap(part, neutral, late):
-        moved = jnp.concatenate([jnp.full_like(part[:half], neutral), part[: rows - half]], axis=0)
+    run_b = combine(early, later)[1]
+    gathered = lax.all_gather(step_a, "seq")
+    grown = gathered[0::2] * gathered[1::2]
+    grown = grown.transpose(1, 0, 2).reshape(2 * chips, heads_dev)
+    grown = jnp.where(core == 0, grown[:, :half], grown[:, half:])
+    ahead = lambda part, back: jnp.concatenate([jnp.ones_like(part[:back]), part[: part.shape[0] - back]], axis=0)
+
+    def window(low, high):
+        total = jnp.ones_like(grown)
+        for back in range(low, high):
+            total = total * ahead(grown, back)
+        spots = jnp.stack([lax.dynamic_index_in_dim(total, chip, keepdims=False),
+                           lax.dynamic_index_in_dim(total, chips + chip, keepdims=False)])
+        return spots
+
+    quarter = half // 2
+    groups = lambda part: [part.reshape((blocks, 2, quarter) + part.shape[1:])[:, g].reshape((blocks * quarter,) + part.shape[1:]) for g in range(2)]
+    weights = lambda spots: [spots[:, g * quarter:(g + 1) * quarter].reshape(blocks * quarter) for g in range(2)]
+    lanes = groups(run_b)
+    priors = [jnp.zeros_like(lane) for lane in lanes]
+    spans = [1 << i for i in range(chips.bit_length() - 1)]
+    turn = len(spans) // 2
+    orders = [spans, spans[turn:] + spans[:turn]]
+
+    def wrap(part, late):
+        moved = jnp.concatenate([jnp.zeros_like(part[:quarter]), part[: part.shape[0] - quarter]], axis=0)
         return jnp.where(late, part, moved)
 
-    span = 1
-    while span < chips:
-        got_a, got_b = from_behind((run_a, run_b), "seq", 2 * span)
-        late = chip >= span
-        lead = (wrap(got_a, 1.0, late), wrap(got_b, 0.0, late))
-        run_a, run_b = combine(lead, (run_a, run_b))
-        prior_a, prior_b = combine(lead, (prior_a, prior_b))
-        span *= 2
-    lift = combine((run_a[:half], run_b[:half]), (prior_a[half:], prior_b[half:]))[1]
-    before_chip = jnp.concatenate([prior_b[:half], lift], axis=0)
+    for step in range(len(orders[0])):
+        for g in range(2):
+            span = orders[g][step]
+            got = from_behind(lanes[g], "seq", 2 * span)
+            lead = wrap(got, chip >= span)
+            inner_w = weights(window(0, span))[g]
+            outer_w = weights(window(1, span))[g]
+            lanes[g] = inner_w[:, None, None] * lead + lanes[g]
+            priors[g] = outer_w[:, None, None] * lead + priors[g]
+    lift_w = weights(window(1, chips))
+    joined = []
+    for g in range(2):
+        lift = lift_w[g][quarter:, None, None] * lanes[g][:quarter] + priors[g][quarter:]
+        joined.append(jnp.concatenate([priors[g][:quarter], lift], axis=0))
+    before_chip = jnp.concatenate(
+        [part.reshape((blocks, quarter) + part.shape[1:]) for part in joined], axis=1
+    ).reshape(run_b.shape)
     after_early = early[0][:, None, None] * before_chip + early[1]
     own_part = jnp.where(core == 0, before_chip, after_early)
     other_part = lax.ppermute(jnp.where(core == 0, after_early, before_chip), "seq", pair)

time: 218 us -> 243 us (1.11)
  waiting for transfers between devices: 97.6 us -> 71.4 us
  local copies, waits for them, and re-layouts: 44.1 us -> 69.8 us
  blocking collectives: 0 us -> 24.2 us
  other arithmetic: 23.2 us -> 27.5 us
    ppermute x9, waiting for transfers between devices: 61.8 us -> 37.1 us  [from_behind(): return lax.ppermute(value, axis, pairs)]
    all_gather x0 -> x1, blocking collectives: none -> 24.2 us  [per_device(): gathered = lax.all_gather(step_a, 'seq')]
    mul x0 -> x14, local copies, waits for them, and re-layouts: none -> 14.3 us  [the longest x6 7.7 us: per_device(): priors[g] = outer_w[:, None, None] * lead + priors[g]]
    add x0 -> x8, other arithmetic: none -> 11.2 us  [the longest x6 9.78 us: per_device(): lanes[g] = inner_w[:, None, None] * lead + lanes[g]]
    add x5 -> x1, other arithmetic: 9.44 us -> 1.18 us  [combine(): later[0][:, None, None] * earlier[1] + later[1]]
    slice x7 -> x18, local copies, waits for them, and re-layouts: 4.27 us -> 11.6 us  [the longest x8 5.5 us: wrap(): part[:part.shape[0] - quarter]]
    ppermute x9, starting transfers between devices: 4.09 us -> 1.29 us  [from_behind(): return lax.ppermute(value, axis, pairs)]
    unnamed x52 -> x76, local copies, waits for them, and re-layouts: 22.3 us -> 24.3 us
  transfers between devices with their start and end apart: 13 -> 13, of which waited for: 10 -> 6; matrix products, arithmetic and copies ran while one was open for 13% -> 34% of each run, Pallas kernels for 0% -> 0%
where the time goes in v6:
time: 243 us; the launch traced here: 241 us
  waiting for transfers between devices  71.4 us (29%)
  local copies, waits for them, and re-layouts  69.8 us (29%)
  matrix products  30.7 us (13%)
  other arithmetic  27.5 us (11%)
  blocking collectives  24.2 us (10%)
  between operations  14.2 us (6%)
  starting transfers between devices  2.65 us (1%)
    ppermute x9, waiting for transfers between devices, from_behind(): return lax.ppermute(value, axis, pairs)  37.1 us
    all_gather x1, waiting for transfers between devices, per_device(): piece = lax.all_gather(hidden, 'mp', axis=1, tiled=True)  33.5 us
    unnamed x76, local copies, waits for them, and re-layouts  24.3 us
    all_gather x1, blocking collectives, per_device(): gathered = lax.all_gather(step_a, 'seq')  24.2 us
    dot_general x1, matrix products, per_device(): zx_sum = jnp.dot(piece, flat_zx, preferred_element_type=jnp.float32)  15.8 us
    add x6, other arithmetic, per_device(): lanes[g] = inner_w[:, None, None] * lead + lanes[g]  9.78 us
    mul x6, local copies, waits for them, and re-layouts, per_device(): priors[g] = outer_w[:, None, None] * lead + priors[g]  7.7 us
    reshape x2, local copies, waits for them, and re-layouts, per_device(): y_total.reshape(rows_dev, inner_dev) * jax.nn.silu(gate.astype(jnp.float32))  7.28 us
  transfers between devices with their start and end apart: 13, of which 6 were waited for; matrix products, arithmetic and copies ran while one was open for 34% of the time, Pallas kernels for 0%

profile of v6, /device:TPU:0, one launch (start us, length us, event | category | flops | bytes accessed | tf_op | source)
XLA Modules:
  0.0 240.5 jit_solution(18339605436788582156)
XLA Ops:
  6.5 0.7 all-gather.2.cloned.1.call-update
  7.3 0.9 select_reduce_fusion.1
  8.4 17.3 %copy.192 = bf16[512,8,2,1024]{3,1,2,0:T(8,128)(2,1)} copy(bf16[512,8,2,1024]{3,2,1,0:T(2,128)(2,1)} %bitcast.155) | data formatting | bytes 33554432
  26.3 33.5 %all-gather.2.cloned.1.call-done = bf16[512,4096]{1,0:T(8,128)(2,1)} async-done(((bf16[512,1024]{1,0:T(8,128)(2,1)}), bf16[512,4096]{1,0:T(8,128)(2,1)}) %all-gather.2.cloned.1.call-update) | async-done | bytes 4194320 | tf_op jit(solution)/shard_map/all_gather | solution.py:57
  59.7 15.8 %convolution_convert_fusion = bf16[512,2048]{1,0:T(8,128)(2,1)S(1)} fusion(bf16[512,4096]{1,0:T(8,128)(2,1)} %all-gather.2.cloned.1.call-done, bf16[4096,2048]{1,0:T(8,128)(2,1)} %bitcast.156), kind=kOutput, calls=%fused_computation.8 | convolution fusion | flops 8590983168 | bytes 23068672 | tf_op jit(solution)/shard_map/dot_general | solution.py:58
  75.7 2.2 copy-done.32
  77.9 1.3 fusion.20
  80.1 1.2 fusion.63
  81.4 1.2 reduce-window.18
  83.6 0.7 fusion.52
  84.6 1.0 collective-permute-start.1
  85.7 24.2 %all_gather.8 = f32[32,2,16]{2,1,0:T(2,128)S(1)} all-gather(f32[1,2,16]{2,1,0:T(2,128)S(1)} %bitcast_select_fusion.4), channel_id=1, replica_groups=mesh['seq'=32,'mp'=4] {'seq'}, dimensions={0}, use_global_device_ids=true | all-gather | bytes 4224 | tf_op jit(solution)/shard_map/all_gather | solution.py:137
  114.9 1.7 multiply_convert_fusion.2
  116.7 1.4 slice_convert_fusion
  118.1 2.2 copy.150
  120.3 1.7 fusion.23
  122.0 4.6 %copy_add_fusion = (f32[2,16,64,128]{3,0,2,1:T(2,128)S(1)}, f32[2,16,64,128]{3,0,2,1:T(2,128)}) fusion(f32[2,16,64,128]{3,2,1,0:T(8,128)S(1)} %fusion.23, pred[2]{0:T(512)(128)(4,1)S(1)} %compare_reduce_fusion, f32[2,16]{0,1:T(8,128)S(1)} %copy.164, f32[2,16,64,128]{3,2,1,0:T(8,128)S(1)} %copy-done, s32[2]{0:T(128)S(1)} %fusion.46), kind=kOutput, calls=%fused_computation.42 | convolution fusion | flops 7077892 | bytes 4194442 | tf_op jit(solution)/shard_map/cr,rhpn->chpn/dot_general | solution.py:82
  126.6 0.9 constant_dynamic-slice_fusion.8
  127.5 0.9 copy.167
  129.4 1.1 copy.166
  130.6 0.7 copy-done.4
  131.3 1.2 fusion.31
  132.5 0.9 fusion.53
  134.9 11.3 %collective-permute-done.3 = f32[8,64,128]{2,1,0:T(8,128)} collective-permute-done((f32[8,64,128]{2,1,0:T(8,128)}, f32[8,64,128]{2,1,0:T(8,128)}, u32[]{:S(2)}, u32[]{:S(2)}) %collective-permute-start.3) | collective-permute-done | bytes 262176 | tf_op jit(solution)/shard_map/ppermute | solution.py:17
  146.2 0.9 slice.350
  147.8 1.7 multiply_add_fusion.5
  150.9 1.8 multiply_add_fusion.2
  153.0 13.8 %collective-permute-done.4 = f32[8,64,128]{2,1,0:T(8,128)} collective-permute-done((f32[8,64,128]{2,1,0:T(8,128)}, f32[8,64,128]{2,1,0:T(8,128)}, u32[]{:S(2)}, u32[]{:S(2)}) %collective-permute-start.4) | collective-permute-done | bytes 262176 | tf_op jit(solution)/shard_map/ppermute | solution.py:17
  166.8 0.9 slice.351
  168.4 1.7 multiply_add_fusion.4
  170.2 0.7 mul.507
  171.0 1.3 mul.554
  172.3 0.9 slice.361
  173.9 1.8 multiply_add_fusion.1
  175.6 5.2 %collective-permute-done.5 = f32[8,64,128]{2,1,0:T(8,128)} collective-permute-done((f32[8,64,128]{2,1,0:T(8,128)}, f32[8,64,128]{2,1,0:T(8,128)}, u32[]{:S(2)}, u32[]{:S(2)}) %collective-permute-start.5) | collective-permute-done | bytes 262176 | tf_op jit(solution)/shard_map/ppermute | solution.py:17
  180.8 0.9 slice.352
  182.4 1.7 multiply_add_fusion.3
  184.9 1.3 mul.526
  186.2 1.3 mul.529
  187.5 1.2 mul.502
  188.7 1.3 mul.546
  190.0 1.3 mul.552
  191.3 1.3 mul.550
  192.5 1.3 mul.565
  193.8 1.3 mul.562
  195.1 1.2 mul.570
  196.3 0.9 slice.362
  197.2 1.0 multiply_add_fusion
  198.4 0.9 slice.353
  199.3 1.2 add_add_fusion.1
  200.6 1.0 fusion.54
  201.6 6.8 %collective-permute-done.10 = f32[8,64,128]{2,1,0:T(8,128)S(1)} collective-permute-done((f32[8,64,128]{2,1,0:T(8,128)S(1)}, f32[8,64,128]{2,1,0:T(8,128)S(1)}, u32[]{:S(2)}, u32[]{:S(2)}) %collective-permute-start.10) | collective-permute-done | bytes 262176 | tf_op jit(solution)/shard_map/ppermute | solution.py:17
  209.5 1.3 bitcast_select_fusion.1
  210.8 1.9 copy.179
  212.7 1.3 fusion.37
  214.0 1.4 copy.174
  215.4 1.4 copy.175
  216.9 0.8 fusion.24
  217.8 2.1 fusion.25
  219.9 2.6 %fusion.19 = f32[2,256,1,16,64]{1,4,3,0,2:T(8,128)S(1)} fusion(f32[2,16,64,256]{3,2,1,0:T(8,128)S(1)} %fusion.25, f32[2,256,1,16,64]{1,4,3,0,2:T(8,128)S(1)} %bitcast.185, bf16[2,256,16,64]{1,3,2,0:T(8,128)(2,1)S(1)} %bitcast.160, f32[2,16,256]{2,1,0:T(8,128)S(1)} %copy-done.17, f32[2,16,256]{2,1,0:T(8,128)S(1)} %copy-done.16, ...), kind=kOutput, calls=%fused_computation.30 | convolution fusion | flops 281018368 | bytes 8028224 | tf_op jit(solution)/shard_map/cgjqk,ckgjp->cqgjp/dot_general | solution.py:109
  222.5 3.8 %copy.186 = f32[2,256,1,16,64]{4,3,1,0,2:T(8,128)} copy(f32[2,256,1,16,64]{1,4,3,0,2:T(8,128)S(1)} %fusion.19) | data formatting | bytes 4194304 | tf_op jit(solution)/shard_map/reshape | solution.py:201
  226.3 3.5 %reshape.329 = f32[512,1024]{1,0:T(8,128)S(1)} reshape(f32[2,256,1,16,64]{4,3,1,0,2:T(8,128)} %copy.186) | data formatting | bytes 4194304 | tf_op jit(solution)/shard_map/reshape | solution.py:201
  229.9 2.1 multiply_reduce_fusion
  232.0 1.7 multiply_convert_fusion.3
  (176 shorter events, 17.1 us)
Async XLA Ops:
  6.5 115.5 %copy-start = (f32[2,16,64,128]{3,2,1,0:T(8,128)S(1)}, f32[2,16,64,128]{3,2,1,0:T(8,128)}, u32[]{:S(2)}) copy-start(f32[2,16,64,128]{3,2,1,0:T(8,128)} %param.30) | copy-start | bytes 3145732
  6.5 53.2 %all-gather.2.cloned.1.call-start = ((), (), s32[]{:S(2)}) async-start(), calls=%async_computation | async-start | bytes 5242880 | tf_op jit(solution)/shard_map/all_gather | solution.py:57
  8.4 17.3 %copy-start.23 = (bf16[2,3,2,128]{3,2,1,0:T(2,128)(2,1)S(1)}, bf16[2,3,2,128]{3,2,1,0:T(2,128)(2,1)}, u32[]{:S(2)}) copy-start(bf16[2,3,2,128]{3,2,1,0:T(2,128)(2,1)} %param.32) | copy-start | bytes 9220
  8.4 17.4 %copy-start.21 = (f32[1024]{0:T(1024)S(1)}, f32[1024]{0:T(1024)}, u32[]{:S(2)}) copy-start(f32[1024]{0:T(1024)} %param.23) | copy-start | bytes 12292
  8.4 17.4 %copy-start.26 = (f32[2,128]{1,0:T(2,128)S(1)}, f32[2,128]{1,0:T(2,128)}, u32[]{:S(2)}) copy-start(f32[2,128]{1,0:T(2,128)} %param.25) | copy-start | bytes 3076
  8.4 17.4 %copy-start.19 = (f32[4,1024]{1,0:T(4,128)S(1)}, f32[4,1024]{1,0:T(4,128)}, u32[]{:S(2)}) copy-start(f32[4,1024]{1,0:T(4,128)} %param.22) | copy-start | bytes 49156
  8.4 17.8 %copy-start.22 = (f32[4,2,128]{2,1,0:T(2,128)S(1)}, f32[4,2,128]{2,1,0:T(2,128)}, u32[]{:S(2)}) copy-start(f32[4,2,128]{2,1,0:T(2,128)} %param.24) | copy-start | bytes 12292
  8.4 17.9 %copy-start.34 = (f32[16]{0:T(128)S(1)}, f32[16]{0:T(128)}, u32[]{:S(2)}) copy-start(f32[16]{0:T(128)} %param.26) | copy-start | bytes 196
  59.7 15.9 %copy-start.6 = (bf16[512,4096]{1,0:T(8,128)(2,1)S(1)}, bf16[512,4096]{1,0:T(8,128)(2,1)}, u32[]{:S(2)}) copy-start(bf16[512,4096]{1,0:T(8,128)(2,1)} %all-gather.2.cloned.1.call-done) | copy-start | bytes 12582916
  75.5 3.6 %copy-start.2 = (bf16[512,2048]{1,0:T(8,128)(2,1)}, bf16[512,2048]{1,0:T(8,128)(2,1)S(1)}, u32[]{:S(2)}) copy-start(bf16[512,2048]{1,0:T(8,128)(2,1)S(1)} %convolution_convert_fusion) | copy-start | bytes 6291460
  75.6 2.4 copy-start.32
  79.2 0.9 copy-start.15
  79.4 1.9 copy-start.24
  79.4 35.0 %copy-start.33 = (bf16[2,3,1024]{2,0,1:T(2,128)(2,1)S(1)}, bf16[2,3,1024]{2,0,1:T(2,128)(2,1)}, u32[]{:S(2)}) copy-start(bf16[2,3,1024]{2,0,1:T(2,128)(2,1)} %param.31) | copy-start | bytes 36868
  79.4 35.0 %collective-permute-start = (bf16[2,3,1280]{2,0,1:T(2,128)(2,1)S(1)}, bf16[2,3,1280]{2,0,1:T(2,128)(2,1)S(1)}, u32[]{:S(2)}, u32[]{:S(2)}) collective-permute-start(bf16[2,3,1280]{2,0,1:T(2,128)(2,1)S(1)} %copy.188), channel_id=1, source_target_pairs={{0,4},{4,8},{8,12},{12,16},{16,20},{20,24},{24,28},{28,32},{32,36}... | collective-permute-start | bytes 46088 | tf_op jit(solution)/shard_map/ppermute | solution.py:17
  84.6 44.9 %collective-permute-start.1 = (f32[16]{0:T(128)S(1)}, f32[16]{0:T(128)S(1)}, u32[]{:S(2)}, u32[]{:S(2)}) collective-permute-start(f32[16]{0:T(128)S(1)} %reshape.313), channel_id=1, source_target_pairs={{0,4},{4,0},{8,12},{12,8},{16,20},{20,16},{24,28},{28,24},{32,36},... | collective-permute-start | bytes 200 | tf_op jit(solution)/shard_map/ppermute | solution.py:133
  116.7 1.4 copy-start.1
  128.4 2.3 collective-permute-start.2
  130.5 0.8 copy-start.4
  133.4 12.8 %collective-permute-start.3 = (f32[8,64,128]{2,1,0:T(8,128)}, f32[8,64,128]{2,1,0:T(8,128)}, u32[]{:S(2)}, u32[]{:S(2)}) collective-permute-start(f32[8,64,128]{2,1,0:T(8,128)} %bitcast.19), channel_id=1, source_target_pairs={{0,8},{4,12},{8,16},{12,20},{16,24},{20,28},{24,32},{28,36},{32,40... | collective-permute-start | bytes 786440 | tf_op jit(solution)/shard_map/ppermute | solution.py:17
  134.7 16.2 %collective-permute-start.7 = (f32[8,64,128]{2,1,0:T(8,128)}, f32[8,64,128]{2,1,0:T(8,128)S(1)}, u32[]{:S(2)}, u32[]{:S(2)}) collective-permute-start(f32[8,64,128]{2,1,0:T(8,128)} %bitcast.189), channel_id=1, source_target_pairs={{0,32},{4,36},{8,40},{12,44},{16,48},{20,52},{24,56},{28,60},{32,6... | collective-permute-start | bytes 786440 | tf_op jit(solution)/shard_map/ppermute | solution.py:17
  147.1 0.6 copy-start.9
  149.5 17.3 %collective-permute-start.4 = (f32[8,64,128]{2,1,0:T(8,128)}, f32[8,64,128]{2,1,0:T(8,128)}, u32[]{:S(2)}, u32[]{:S(2)}) collective-permute-start(f32[8,64,128]{2,1,0:T(8,128)} %multiply_add_fusion.5), channel_id=1, source_target_pairs={{0,16},{4,20},{8,24},{12,28},{16,32},{20,36},{24,40},{28,44},{32,4... | collective-permute-start | bytes 786440 | tf_op jit(solution)/shard_map/ppermute | solution.py:17
  152.7 19.6 %collective-permute-start.8 = (f32[8,64,128]{2,1,0:T(8,128)}, f32[8,64,128]{2,1,0:T(8,128)}, u32[]{:S(2)}, u32[]{:S(2)}) collective-permute-start(f32[8,64,128]{2,1,0:T(8,128)} %multiply_add_fusion.2), channel_id=1, source_target_pairs={{0,64},{4,68},{8,72},{12,76},{16,80},{20,84},{24,88},{28,92},{32,9... | collective-permute-start | bytes 786440 | tf_op jit(solution)/shard_map/ppermute | solution.py:17
  167.7 0.7 copy-start.12
  170.1 10.7 %collective-permute-start.5 = (f32[8,64,128]{2,1,0:T(8,128)}, f32[8,64,128]{2,1,0:T(8,128)}, u32[]{:S(2)}, u32[]{:S(2)}) collective-permute-start(f32[8,64,128]{2,1,0:T(8,128)} %multiply_add_fusion.4), channel_id=1, source_target_pairs={{0,32},{4,36},{8,40},{12,44},{16,48},{20,52},{24,56},{28,60},{32,6... | collective-permute-start | bytes 786440 | tf_op jit(solution)/shard_map/ppermute | solution.py:17
  173.2 0.7 copy-start.10
  175.6 20.7 %collective-permute-start.9 = (f32[8,64,128]{2,1,0:T(8,128)}, f32[8,64,128]{2,1,0:T(8,128)}, u32[]{:S(2)}, u32[]{:S(2)}) collective-permute-start(f32[8,64,128]{2,1,0:T(8,128)} %multiply_add_fusion.1), channel_id=1, source_target_pairs={{0,8},{4,12},{8,16},{12,20},{16,24},{20,28},{24,32},{28,36},{32,40... | collective-permute-start | bytes 786440 | tf_op jit(solution)/shard_map/ppermute | solution.py:17
  181.8 0.7 copy-start.13
  184.2 14.2 %collective-permute-start.6 = (f32[8,64,128]{2,1,0:T(8,128)}, f32[8,64,128]{2,1,0:T(8,128)}, u32[]{:S(2)}, u32[]{:S(2)}) collective-permute-start(f32[8,64,128]{2,1,0:T(8,128)} %multiply_add_fusion.3), channel_id=1, source_target_pairs={{0,64},{4,68},{8,72},{12,76},{16,80},{20,84},{24,88},{28,92},{32,9... | collective-permute-start | bytes 786440 | tf_op jit(solution)/shard_map/ppermute | solution.py:17
  184.9 15.7 %copy-start.25 = (f32[4]{0:T(128)S(1)}, f32[4]{0:T(128)}, u32[]{:S(2)}) copy-start(f32[4]{0:T(128)} %get-tuple-element.11) | copy-start | bytes 52
  196.3 4.3 %copy-start.31 = (f32[8]{0:T(128)S(1)}, f32[8]{0:T(128)}, u32[]{:S(2)}) copy-start(f32[8]{0:T(128)} %mul.546) | copy-start | bytes 100
  198.3 10.1 %copy-start.11 = (f32[4,64,128]{2,1,0:T(8,128)S(1)}, f32[4,64,128]{2,1,0:T(8,128)}, u32[]{:S(2)}) copy-start(f32[4,64,128]{2,1,0:T(8,128)} %copy-done.10) | copy-start | bytes 393220
  198.3 10.1 %copy-start.28 = (f32[8]{0:T(128)S(1)}, f32[8]{0:T(128)}, u32[]{:S(2)}) copy-start(f32[8]{0:T(128)} %mul.550) | copy-start | bytes 100
  198.3 10.1 %copy-start.29 = (f32[8]{0:T(128)S(1)}, f32[8]{0:T(128)}, u32[]{:S(2)}) copy-start(f32[8]{0:T(128)} %mul.565) | copy-start | bytes 100
  198.3 10.1 %copy-start.30 = (f32[8]{0:T(128)S(1)}, f32[8]{0:T(128)}, u32[]{:S(2)}) copy-start(f32[8]{0:T(128)} %mul.562) | copy-start | bytes 100
  198.3 10.1 %collective-permute-start.10 = (f32[8,64,128]{2,1,0:T(8,128)S(1)}, f32[8,64,128]{2,1,0:T(8,128)S(1)}, u32[]{:S(2)}, u32[]{:S(2)}) collective-permute-start(f32[8,64,128]{2,1,0:T(8,128)S(1)} %multiply_add_fusion), channel_id=1, source_target_pairs={{0,16},{4,20},{8,24},{12,28},{16,32},{20,36},{24,40},{28,44},{32,4... | collective-permute-start | bytes 786440 | tf_op jit(solution)/shard_map/ppermute | solution.py:17
  200.6 8.1 %copy-start.27 = (f32[8]{0:T(128)S(1)}, f32[8]{0:T(128)}, u32[]{:S(2)}) copy-start(f32[8]{0:T(128)} %mul.570) | copy-start | bytes 100
  208.4 1.0 copy-start.5
  210.8 4.6 %collective-permute-start.11 = (f32[16,64,128]{2,1,0:T(8,128)}, f32[16,64,128]{2,1,0:T(8,128)}, u32[]{:S(2)}, u32[]{:S(2)}) collective-permute-start(f32[16,64,128]{2,1,0:T(8,128)} %get-tuple-element.26), channel_id=1, source_target_pairs={{0,4},{4,0},{8,12},{12,8},{16,20},{20,16},{24,28},{28,24},{32,36},... | collective-permute-start | bytes 1572872 | tf_op jit(solution)/shard_map/ppermute | solution.py:183
  212.7 4.2 %copy-start.14 = (f32[2,16,64,128]{3,0,2,1:T(2,128)S(1)}, f32[2,16,64,128]{3,0,2,1:T(2,128)}, u32[]{:S(2)}) copy-start(f32[2,16,64,128]{3,0,2,1:T(2,128)} %get-tuple-element.77) | copy-start | bytes 3145732
  217.7 2.1 copy-start.7
  217.8 2.1 copy-start.8
  217.8 2.1 copy-start.16
  217.8 2.1 copy-start.17
  217.8 2.1 copy-start.18
  217.8 2.1 copy-start.35
  229.8 2.1 copy-start.3
  229.8 2.1 copy-start.20
Sparse Core Ops, SparseCore 0:
  9.0 50.6 all-gather.1

commit v7 on v6

--- a/solution.py
+++ b/solution.py
@@ -134,26 +134,22 @@
     early = jax.tree.map(lambda own, other: jnp.where(core == 0, own, other), mine, got)
     later = jax.tree.map(lambda own, other: jnp.where(core == 0, other, own), mine, got)
     run_b = combine(early, later)[1]
-    gathered = lax.all_gather(step_a, "seq")
-    grown = gathered[0::2] * gathered[1::2]
-    grown = grown.transpose(1, 0, 2).reshape(2 * chips, heads_dev)
-    grown = jnp.where(core == 0, grown[:, :half], grown[:, half:])
-    ahead = lambda part, back: jnp.concatenate([jnp.ones_like(part[:back]), part[: part.shape[0] - back]], axis=0)
-
-    def window(low, high):
-        total = jnp.ones_like(grown)
-        for back in range(low, high):
-            total = total * ahead(grown, back)
-        spots = jnp.stack([lax.dynamic_index_in_dim(total, chip, keepdims=False),
-                           lax.dynamic_index_in_dim(total, chips + chip, keepdims=False)])
-        return spots
-
+    spans = [1 << i for i in range(chips.bit_length() - 1)]
+    inner_at, outer_at = {}, {}
+    ra = combine(early, later)[0]
+    pa = jnp.ones_like(ra)
+    for span in spans:
+        inner_at[span], outer_at[span] = ra, pa
+        got = from_behind(ra, "seq", 2 * span)
+        moved = jnp.concatenate([jnp.ones_like(got[:half]), got[: rows - half]], axis=0)
+        lead = jnp.where(chip >= span, got, moved)
+        ra, pa = lead * ra, lead * pa
+    outer_at[chips] = pa
     quarter = half // 2
     groups = lambda part: [part.reshape((blocks, 2, quarter) + part.shape[1:])[:, g].reshape((blocks * quarter,) + part.shape[1:]) for g in range(2)]
-    weights = lambda spots: [spots[:, g * quarter:(g + 1) * quarter].reshape(blocks * quarter) for g in range(2)]
+    weights = lambda flat: [flat.reshape(blocks, half)[:, g * quarter:(g + 1) * quarter].reshape(blocks * quarter) for g in range(2)]
     lanes = groups(run_b)
     priors = [jnp.zeros_like(lane) for lane in lanes]
-    spans = [1 << i for i in range(chips.bit_length() - 1)]
     turn = len(spans) // 2
     orders = [spans, spans[turn:] + spans[:turn]]
 
@@ -166,11 +162,11 @@
             span = orders[g][step]
             got = from_behind(lanes[g], "seq", 2 * span)
             lead = wrap(got, chip >= span)
-            inner_w = weights(window(0, span))[g]
-            outer_w = weights(window(1, span))[g]
+            inner_w = weights(inner_at[span])[g]
+            outer_w = weights(outer_at[span])[g]
             lanes[g] = inner_w[:, None, None] * lead + lanes[g]
             priors[g] = outer_w[:, None, None] * lead + priors[g]
-    lift_w = weights(window(1, chips))
+    lift_w = weights(outer_at[chips])
     joined = []
     for g in range(2):
         lift = lift_w[g][quarter:, None, None] * lanes[g][:quarter] + priors[g][quarter:]

time: 243 us -> 221 us (0.909)
  blocking collectives: 24.2 us -> 0 us
  local copies, waits for them, and re-layouts: 69.8 us -> 62.4 us
  starting transfers between devices: 2.65 us -> 7.13 us
  waiting for transfers between devices: 71.4 us -> 75.7 us
    all_gather x1 -> x0, blocking collectives: 24.2 us -> none  [per_device(): gathered = lax.all_gather(step_a, 'seq')]
    ppermute x9 -> x13, starting transfers between devices: 1.29 us -> 6.1 us  [from_behind(): return lax.ppermute(value, axis, pairs)]
    ppermute x9 -> x13, waiting for transfers between devices: 37.1 us -> 40.7 us  [from_behind(): return lax.ppermute(value, axis, pairs)]
    slice x9, local copies, waits for them, and re-layouts: 5.2 us -> 1.91 us  [the longest x7 1.6 us: per_device(): flat.reshape(blocks, half)[:, g * quarter:(g + 1) * quarter]]
    mul x8, local copies, waits for them, and re-layouts: 6.59 us -> 3.81 us  [per_device(): lanes[g] = inner_w[:, None, None] * lead + lanes[g]]
    unnamed x76 -> x74, local copies, waits for them, and re-layouts: 24.3 us -> 24.3 us
  transfers between devices with their start and end apart: 13 -> 17, of which waited for: 6 -> 9; matrix products, arithmetic and copies ran while one was open for 34% -> 35% of each run, Pallas kernels for 0% -> 0%
where the time goes in v7:
time: 221 us; the launch traced here: 218 us
  waiting for transfers between devices  75.7 us (34%)
  local copies, waits for them, and re-layouts  62.4 us (28%)
  matrix products  30.7 us (14%)
  other arithmetic  28.1 us (13%)
  between operations  14.2 us (6%)
  starting transfers between devices  7.13 us (3%)
    ppermute x13, waiting for transfers between devices, from_behind(): return lax.ppermute(value, axis, pairs)  40.7 us
    all_gather x1, waiting for transfers between devices, per_device(): piece = lax.all_gather(hidden, 'mp', axis=1, tiled=True)  33.5 us
    unnamed x74, local copies, waits for them, and re-layouts  24.3 us
    dot_general x1, matrix products, per_device(): zx_sum = jnp.dot(piece, flat_zx, preferred_element_type=jnp.float32)  15.8 us
    add x6, other arithmetic, per_device(): lanes[g] = inner_w[:, None, None] * lead + lanes[g]  9.79 us
    reshape x2, local copies, waits for them, and re-layouts, per_device(): y_total.reshape(rows_dev, inner_dev) * jax.nn.silu(gate.astype(jnp.float32))  7.29 us
    mul x6, local copies, waits for them, and re-layouts, per_device(): priors[g] = outer_w[:, None, None] * lead + priors[g]  6.36 us
    ppermute x13, starting transfers between devices, from_behind(): return lax.ppermute(value, axis, pairs)  6.1 us
  transfers between devices with their start and end apart: 17, of which 9 were waited for; matrix products, arithmetic and copies ran while one was open for 35% of the time, Pallas kernels for 0%

profile of v7, /device:TPU:0, one launch (start us, length us, event | category | flops | bytes accessed | tf_op | source)
XLA Modules:
  0.0 218.2 jit_solution(9606861885887391089)
XLA Ops:
  7.3 0.9 select_reduce_fusion.1
  8.4 17.2 %copy.111 = bf16[512,8,2,1024]{3,1,2,0:T(8,128)(2,1)} copy(bf16[512,8,2,1024]{3,2,1,0:T(2,128)(2,1)} %bitcast.142) | data formatting | bytes 33554432
  26.2 33.5 %all-gather.2.cloned.1.call-done = bf16[512,4096]{1,0:T(8,128)(2,1)} async-done(((bf16[512,1024]{1,0:T(8,128)(2,1)}), bf16[512,4096]{1,0:T(8,128)(2,1)}) %all-gather.2.cloned.1.call-update) | async-done | bytes 4194320 | tf_op jit(solution)/shard_map/all_gather | solution.py:57
  59.7 15.8 %convolution_convert_fusion = bf16[512,2048]{1,0:T(8,128)(2,1)S(1)} fusion(bf16[512,4096]{1,0:T(8,128)(2,1)} %all-gather.2.cloned.1.call-done, bf16[4096,2048]{1,0:T(8,128)(2,1)} %bitcast.143), kind=kOutput, calls=%fused_computation.8 | convolution fusion | flops 8590983168 | bytes 23068672 | tf_op jit(solution)/shard_map/dot_general | solution.py:58
  75.7 2.2 %copy-done.31 = bf16[4096,2,128]{2,1,0:T(2,128)(2,1)S(1)} copy-done((bf16[4096,2,128]{2,1,0:T(2,128)(2,1)S(1)}, bf16[4096,2,128]{2,1,0:T(2,128)(2,1)}, u32[]{:S(2)}) %copy-start.31) | copy-done | bytes 2097176
  77.9 1.3 fusion.20
  80.1 1.2 fusion.72
  81.4 1.2 reduce-window.18
  83.6 0.7 fusion.57
  84.7 1.0 collective-permute-start.1
  85.8 0.7 collective-permute-done.1
  86.6 1.6 collective-permute-start.2
  88.9 4.6 %collective-permute-done.2 = f32[16]{0:T(128)S(1)} collective-permute-done((f32[16]{0:T(128)S(1)}, f32[16]{0:T(128)S(1)}, u32[]{:S(2)}, u32[]{:S(2)}) %collective-permute-start.2) | collective-permute-done | bytes 96 | tf_op jit(solution)/shard_map/ppermute | solution.py:17
  96.6 1.7 multiply_convert_fusion.2
  98.3 1.4 slice_convert_fusion
  99.7 2.2 %copy.84 = bf16[2,256,1024]{1,2,0:T(8,128)(2,1)} copy(bf16[2,256,1024]{2,1,0:T(8,128)(2,1)} %get-tuple-element.26) | data formatting | bytes 2097152 | tf_op jit(solution)/shard_map/slice | solution.py:95
  101.9 1.7 fusion.23
  103.6 4.6 %copy_add_fusion = (f32[2,16,64,128]{3,0,2,1:T(2,128)S(1)}, f32[2,16,64,128]{3,0,2,1:T(2,128)}) fusion(f32[2,16,64,128]{3,2,1,0:T(8,128)S(1)} %fusion.23, pred[2]{0:T(512)(128)(4,1)S(1)} %compare_reduce_fusion, f32[2,16]{0,1:T(8,128)S(1)} %copy.89, f32[2,16,64,128]{3,2,1,0:T(8,128)S(1)} %copy-done, s32[2]{0:T(128)S(1)} %fusion.46), kind=kOutput, calls=%fused_computation.42 | convolution fusion | flops 7077892 | bytes 4194442 | tf_op jit(solution)/shard_map/cr,rhpn->chpn/dot_general | solution.py:82
  108.3 0.9 constant_dynamic-slice_fusion
  109.1 0.9 copy.92
  110.2 1.0 collective-permute-start.4
  112.4 2.5 %collective-permute-done.4 = f32[16]{0:T(128)S(1)} collective-permute-done((f32[16]{0:T(128)S(1)}, f32[16]{0:T(128)S(1)}, u32[]{:S(2)}, u32[]{:S(2)}) %collective-permute-start.4) | collective-permute-done | bytes 96 | tf_op jit(solution)/shard_map/ppermute | solution.py:17
  115.0 1.3 collective-permute-start.10
  116.4 1.1 copy.91
  117.5 0.8 copy-done.4
  118.3 1.2 fusion.31
  119.5 0.9 fusion.62
  123.2 10.0 %collective-permute-done.6 = f32[8,64,128]{2,1,0:T(8,128)} collective-permute-done((f32[8,64,128]{2,1,0:T(8,128)}, f32[8,64,128]{2,1,0:T(8,128)}, u32[]{:S(2)}, u32[]{:S(2)}) %collective-permute-start.6) | collective-permute-done | bytes 262176 | tf_op jit(solution)/shard_map/ppermute | solution.py:17
  133.1 0.9 slice.240
  134.7 1.7 multiply_add_fusion.5
  137.2 1.8 multiply_add_fusion.2
  139.0 1.1 collective-permute-start.12
  140.1 11.4 %collective-permute-done.7 = f32[8,64,128]{2,1,0:T(8,128)} collective-permute-done((f32[8,64,128]{2,1,0:T(8,128)}, f32[8,64,128]{2,1,0:T(8,128)}, u32[]{:S(2)}, u32[]{:S(2)}) %collective-permute-start.7) | collective-permute-done | bytes 262176 | tf_op jit(solution)/shard_map/ppermute | solution.py:17
  151.5 0.9 slice.241
  153.0 1.7 multiply_add_fusion.4
  155.4 1.3 reshape.318
  156.7 0.9 slice.251
  158.3 1.8 multiply_add_fusion.1
  160.0 5.5 %collective-permute-done.8 = f32[8,64,128]{2,1,0:T(8,128)} collective-permute-done((f32[8,64,128]{2,1,0:T(8,128)}, f32[8,64,128]{2,1,0:T(8,128)}, u32[]{:S(2)}, u32[]{:S(2)}) %collective-permute-start.8) | collective-permute-done | bytes 262176 | tf_op jit(solution)/shard_map/ppermute | solution.py:17
  165.5 0.9 slice.242
  167.1 1.7 multiply_add_fusion.3
  168.9 1.3 mul.418
  170.2 1.3 mul.437
  171.5 1.3 mul.463
  172.8 1.2 mul.466
  174.0 0.9 slice.252
  174.9 1.0 multiply_add_fusion
  176.1 0.9 collective-permute-done.9
  177.0 0.9 slice.243
  177.9 1.2 add_add_fusion.1
  179.2 1.0 fusion.63
  180.2 5.8 %collective-permute-done.14 = f32[8,64,128]{2,1,0:T(8,128)S(1)} collective-permute-done((f32[8,64,128]{2,1,0:T(8,128)S(1)}, f32[8,64,128]{2,1,0:T(8,128)S(1)}, u32[]{:S(2)}, u32[]{:S(2)}) %collective-permute-start.14) | collective-permute-done | bytes 262176 | tf_op jit(solution)/shard_map/ppermute | solution.py:17
  187.1 1.3 bitcast_select_fusion.1
  188.5 1.9 copy.98
  190.4 1.3 fusion.37
  191.6 1.4 copy.93
  193.1 1.4 copy.94
  194.6 0.8 fusion.24
  195.5 2.1 fusion.25
  197.6 2.6 %fusion.19 = f32[2,256,1,16,64]{1,4,3,0,2:T(8,128)S(1)} fusion(f32[2,16,64,256]{3,2,1,0:T(8,128)S(1)} %fusion.25, f32[2,256,1,16,64]{1,4,3,0,2:T(8,128)S(1)} %bitcast.149, bf16[2,256,16,64]{1,3,2,0:T(8,128)(2,1)S(1)} %bitcast.147, f32[2,16,256]{2,1,0:T(8,128)S(1)} %copy-done.17, f32[2,16,256]{2,1,0:T(8,128)S(1)} %copy-done.16, ...), kind=kOutput, calls=%fused_computation.30 | convolution fusion | flops 281018368 | bytes 8028224 | tf_op jit(solution)/shard_map/cgjqk,ckgjp->cqgjp/dot_general | solution.py:109
  200.2 3.8 %copy.105 = f32[2,256,1,16,64]{4,3,1,0,2:T(8,128)} copy(f32[2,256,1,16,64]{1,4,3,0,2:T(8,128)S(1)} %fusion.19) | data formatting | bytes 4194304 | tf_op jit(solution)/shard_map/reshape | solution.py:197
  204.0 3.5 %reshape.331 = f32[512,1024]{1,0:T(8,128)S(1)} reshape(f32[2,256,1,16,64]{4,3,1,0,2:T(8,128)} %copy.105) | data formatting | bytes 4194304 | tf_op jit(solution)/shard_map/reshape | solution.py:197
  207.5 2.1 multiply_reduce_fusion
  209.6 1.7 multiply_convert_fusion.3
  (158 shorter events, 17.5 us)
Async XLA Ops:
  6.5 97.1 %copy-start = (f32[2,16,64,128]{3,2,1,0:T(8,128)S(1)}, f32[2,16,64,128]{3,2,1,0:T(8,128)}, u32[]{:S(2)}) copy-start(f32[2,16,64,128]{3,2,1,0:T(8,128)} %param.30) | copy-start | bytes 3145732
  6.5 53.2 %all-gather.2.cloned.1.call-start = ((), (), s32[]{:S(2)}) async-start(), calls=%async_computation | async-start | bytes 5242880 | tf_op jit(solution)/shard_map/all_gather | solution.py:57
  8.4 17.3 %copy-start.23 = (bf16[2,3,2,128]{3,2,1,0:T(2,128)(2,1)S(1)}, bf16[2,3,2,128]{3,2,1,0:T(2,128)(2,1)}, u32[]{:S(2)}) copy-start(bf16[2,3,2,128]{3,2,1,0:T(2,128)(2,1)} %param.32) | copy-start | bytes 9220
  8.4 17.3 %copy-start.21 = (f32[1024]{0:T(1024)S(1)}, f32[1024]{0:T(1024)}, u32[]{:S(2)}) copy-start(f32[1024]{0:T(1024)} %param.23) | copy-start | bytes 12292
  8.4 17.3 %copy-start.26 = (f32[2,128]{1,0:T(2,128)S(1)}, f32[2,128]{1,0:T(2,128)}, u32[]{:S(2)}) copy-start(f32[2,128]{1,0:T(2,128)} %param.25) | copy-start | bytes 3076
  8.4 17.4 %copy-start.19 = (f32[4,1024]{1,0:T(4,128)S(1)}, f32[4,1024]{1,0:T(4,128)}, u32[]{:S(2)}) copy-start(f32[4,1024]{1,0:T(4,128)} %param.22) | copy-start | bytes 49156
  8.4 17.8 %copy-start.22 = (f32[4,2,128]{2,1,0:T(2,128)S(1)}, f32[4,2,128]{2,1,0:T(2,128)}, u32[]{:S(2)}) copy-start(f32[4,2,128]{2,1,0:T(2,128)} %param.24) | copy-start | bytes 12292
  8.4 17.8 %copy-start.33 = (f32[16]{0:T(128)S(1)}, f32[16]{0:T(128)}, u32[]{:S(2)}) copy-start(f32[16]{0:T(128)} %param.26) | copy-start | bytes 196
  59.7 15.9 %copy-start.6 = (bf16[512,4096]{1,0:T(8,128)(2,1)S(1)}, bf16[512,4096]{1,0:T(8,128)(2,1)}, u32[]{:S(2)}) copy-start(bf16[512,4096]{1,0:T(8,128)(2,1)} %all-gather.2.cloned.1.call-done) | copy-start | bytes 12582916
  75.6 3.6 %copy-start.2 = (bf16[512,2048]{1,0:T(8,128)(2,1)}, bf16[512,2048]{1,0:T(8,128)(2,1)S(1)}, u32[]{:S(2)}) copy-start(bf16[512,2048]{1,0:T(8,128)(2,1)S(1)} %convolution_convert_fusion) | copy-start | bytes 6291460
  75.6 2.4 %copy-start.31 = (bf16[4096,2,128]{2,1,0:T(2,128)(2,1)S(1)}, bf16[4096,2,128]{2,1,0:T(2,128)(2,1)}, u32[]{:S(2)}) copy-start(bf16[4096,2,128]{2,1,0:T(2,128)(2,1)} %param.20) | copy-start | bytes 6291460
  79.2 0.9 copy-start.15
  79.4 1.9 copy-start.24
  79.4 16.7 %copy-start.32 = (bf16[2,3,1024]{2,0,1:T(2,128)(2,1)S(1)}, bf16[2,3,1024]{2,0,1:T(2,128)(2,1)}, u32[]{:S(2)}) copy-start(bf16[2,3,1024]{2,0,1:T(2,128)(2,1)} %param.31) | copy-start | bytes 36868
  79.4 16.7 %collective-permute-start = (bf16[2,3,1280]{2,0,1:T(2,128)(2,1)S(1)}, bf16[2,3,1280]{2,0,1:T(2,128)(2,1)S(1)}, u32[]{:S(2)}, u32[]{:S(2)}) collective-permute-start(bf16[2,3,1280]{2,0,1:T(2,128)(2,1)S(1)} %copy.107), channel_id=1, source_target_pairs={{0,4},{4,8},{8,12},{12,16},{16,20},{20,24},{24,28},{28,32},{32,36}... | collective-permute-start | bytes 46088 | tf_op jit(solution)/shard_map/ppermute | solution.py:17
  84.7 1.8 collective-permute-start.1
  86.6 6.9 %collective-permute-start.2 = (f32[16]{0:T(128)S(1)}, f32[16]{0:T(128)S(1)}, u32[]{:S(2)}, u32[]{:S(2)}) collective-permute-start(f32[16]{0:T(128)S(1)} %get-tuple-element.20), channel_id=1, source_target_pairs={{0,8},{4,12},{8,16},{12,20},{16,24},{20,28},{24,32},{28,36},{32,40... | collective-permute-start | bytes 200 | tf_op jit(solution)/shard_map/ppermute | solution.py:17
  93.7 16.3 %collective-permute-start.3 = (f32[16]{0:T(128)S(1)}, f32[16]{0:T(128)S(1)}, u32[]{:S(2)}, u32[]{:S(2)}) collective-permute-start(f32[16]{0:T(128)S(1)} %get-tuple-element.18), channel_id=1, source_target_pairs={{0,16},{4,20},{8,24},{12,28},{16,32},{20,36},{24,40},{28,44},{32,4... | collective-permute-start | bytes 200 | tf_op jit(solution)/shard_map/ppermute | solution.py:17
  98.3 1.4 copy-start.1
  110.0 7.5 %collective-permute-start.5 = (f32[16,64,128]{2,1,0:T(8,128)}, f32[16,64,128]{2,1,0:T(8,128)}, u32[]{:S(2)}, u32[]{:S(2)}) collective-permute-start(f32[16,64,128]{2,1,0:T(8,128)} %bitcast.16), channel_id=1, source_target_pairs={{0,4},{4,0},{8,12},{12,8},{16,20},{20,16},{24,28},{28,24},{32,36},... | collective-permute-start | bytes 1572872 | tf_op jit(solution)/shard_map/ppermute | solution.py:133
  110.2 4.8 %collective-permute-start.4 = (f32[16]{0:T(128)S(1)}, f32[16]{0:T(128)S(1)}, u32[]{:S(2)}, u32[]{:S(2)}) collective-permute-start(f32[16]{0:T(128)S(1)} %fusion.55), channel_id=1, source_target_pairs={{0,32},{4,36},{8,40},{12,44},{16,48},{20,52},{24,56},{28,60},{32,6... | collective-permute-start | bytes 200 | tf_op jit(solution)/shard_map/ppermute | solution.py:17
  115.0 6.9 %collective-permute-start.10 = (f32[16]{0:T(128)S(1)}, f32[16]{0:T(128)S(1)}, u32[]{:S(2)}, u32[]{:S(2)}) collective-permute-start(f32[16]{0:T(128)S(1)} %fusion.52), channel_id=1, source_target_pairs={{0,64},{4,68},{8,72},{12,76},{16,80},{20,84},{24,88},{28,92},{32,9... | collective-permute-start | bytes 200 | tf_op jit(solution)/shard_map/ppermute | solution.py:17
  117.5 0.8 copy-start.4
  120.3 12.8 %collective-permute-start.6 = (f32[8,64,128]{2,1,0:T(8,128)}, f32[8,64,128]{2,1,0:T(8,128)}, u32[]{:S(2)}, u32[]{:S(2)}) collective-permute-start(f32[8,64,128]{2,1,0:T(8,128)} %bitcast.18), channel_id=1, source_target_pairs={{0,8},{4,12},{8,16},{12,20},{16,24},{20,28},{24,32},{28,36},{32,40... | collective-permute-start | bytes 786440 | tf_op jit(solution)/shard_map/ppermute | solution.py:17
  122.6 14.6 %collective-permute-start.11 = (f32[8,64,128]{2,1,0:T(8,128)}, f32[8,64,128]{2,1,0:T(8,128)S(1)}, u32[]{:S(2)}, u32[]{:S(2)}) collective-permute-start(f32[8,64,128]{2,1,0:T(8,128)} %bitcast.153), channel_id=1, source_target_pairs={{0,32},{4,36},{8,40},{12,44},{16,48},{20,52},{24,56},{28,60},{32,6... | collective-permute-start | bytes 786440 | tf_op jit(solution)/shard_map/ppermute | solution.py:17
  134.1 0.7 copy-start.9
  136.5 15.0 %collective-permute-start.7 = (f32[8,64,128]{2,1,0:T(8,128)}, f32[8,64,128]{2,1,0:T(8,128)}, u32[]{:S(2)}, u32[]{:S(2)}) collective-permute-start(f32[8,64,128]{2,1,0:T(8,128)} %multiply_add_fusion.5), channel_id=1, source_target_pairs={{0,16},{4,20},{8,24},{12,28},{16,32},{20,36},{24,40},{28,44},{32,4... | collective-permute-start | bytes 786440 | tf_op jit(solution)/shard_map/ppermute | solution.py:17
  139.0 17.7 %collective-permute-start.12 = (f32[8,64,128]{2,1,0:T(8,128)}, f32[8,64,128]{2,1,0:T(8,128)}, u32[]{:S(2)}, u32[]{:S(2)}) collective-permute-start(f32[8,64,128]{2,1,0:T(8,128)} %multiply_add_fusion.2), channel_id=1, source_target_pairs={{0,64},{4,68},{8,72},{12,76},{16,80},{20,84},{24,88},{28,92},{32,9... | collective-permute-start | bytes 786440 | tf_op jit(solution)/shard_map/ppermute | solution.py:17
  152.4 0.6 copy-start.12
  154.8 10.7 %collective-permute-start.8 = (f32[8,64,128]{2,1,0:T(8,128)}, f32[8,64,128]{2,1,0:T(8,128)}, u32[]{:S(2)}, u32[]{:S(2)}) collective-permute-start(f32[8,64,128]{2,1,0:T(8,128)} %multiply_add_fusion.4), channel_id=1, source_target_pairs={{0,32},{4,36},{8,40},{12,44},{16,48},{20,52},{24,56},{28,60},{32,6... | collective-permute-start | bytes 786440 | tf_op jit(solution)/shard_map/ppermute | solution.py:17
  156.7 12.1 %copy-start.25 = (f32[2,8]{1,0:T(2,128)S(1)}, f32[2,8]{1,0:T(2,128)}, u32[]{:S(2)}) copy-start(f32[2,8]{1,0:T(2,128)} %reshape.318) | copy-start | bytes 196
  157.6 0.7 copy-start.10
  160.0 13.9 %collective-permute-start.13 = (f32[8,64,128]{2,1,0:T(8,128)}, f32[8,64,128]{2,1,0:T(8,128)}, u32[]{:S(2)}, u32[]{:S(2)}) collective-permute-start(f32[8,64,128]{2,1,0:T(8,128)} %multiply_add_fusion.1), channel_id=1, source_target_pairs={{0,8},{4,12},{8,16},{12,20},{16,24},{20,28},{24,32},{28,36},{32,40... | collective-permute-start | bytes 786440 | tf_op jit(solution)/shard_map/ppermute | solution.py:17
  166.4 0.7 copy-start.13
  168.8 8.2 %collective-permute-start.9 = (f32[8,64,128]{2,1,0:T(8,128)}, f32[8,64,128]{2,1,0:T(8,128)}, u32[]{:S(2)}, u32[]{:S(2)}) collective-permute-start(f32[8,64,128]{2,1,0:T(8,128)} %multiply_add_fusion.3), channel_id=1, source_target_pairs={{0,64},{4,68},{8,72},{12,76},{16,80},{20,84},{24,88},{28,92},{32,9... | collective-permute-start | bytes 786440 | tf_op jit(solution)/shard_map/ppermute | solution.py:17
  175.9 10.1 %copy-start.11 = (f32[4,64,128]{2,1,0:T(8,128)S(1)}, f32[4,64,128]{2,1,0:T(8,128)}, u32[]{:S(2)}) copy-start(f32[4,64,128]{2,1,0:T(8,128)} %copy-done.10) | copy-start | bytes 393220
  175.9 10.1 %copy-start.28 = (f32[8]{0:T(128)S(1)}, f32[8]{0:T(128)}, u32[]{:S(2)}) copy-start(f32[8]{0:T(128)} %mul.451) | copy-start | bytes 100
  176.0 10.1 %copy-start.29 = (f32[8]{0:T(128)S(1)}, f32[8]{0:T(128)}, u32[]{:S(2)}) copy-start(f32[8]{0:T(128)} %mul.463) | copy-start | bytes 100
  176.0 10.1 %copy-start.30 = (f32[8]{0:T(128)S(1)}, f32[8]{0:T(128)}, u32[]{:S(2)}) copy-start(f32[8]{0:T(128)} %mul.466) | copy-start | bytes 100
  176.0 10.1 %collective-permute-start.14 = (f32[8,64,128]{2,1,0:T(8,128)S(1)}, f32[8,64,128]{2,1,0:T(8,128)S(1)}, u32[]{:S(2)}, u32[]{:S(2)}) collective-permute-start(f32[8,64,128]{2,1,0:T(8,128)S(1)} %multiply_add_fusion), channel_id=1, source_target_pairs={{0,16},{4,20},{8,24},{12,28},{16,32},{20,36},{24,40},{28,44},{32,4... | collective-permute-start | bytes 786440 | tf_op jit(solution)/shard_map/ppermute | solution.py:17
  179.1 7.1 %copy-start.27 = (f32[8]{0:T(128)S(1)}, f32[8]{0:T(128)}, u32[]{:S(2)}) copy-start(f32[8]{0:T(128)} %mul.471) | copy-start | bytes 100
  186.1 1.0 copy-start.5
  188.4 4.6 %collective-permute-start.15 = (f32[16,64,128]{2,1,0:T(8,128)}, f32[16,64,128]{2,1,0:T(8,128)}, u32[]{:S(2)}, u32[]{:S(2)}) collective-permute-start(f32[16,64,128]{2,1,0:T(8,128)} %get-tuple-element.24), channel_id=1, source_target_pairs={{0,4},{4,0},{8,12},{12,8},{16,20},{20,16},{24,28},{28,24},{32,36},... | collective-permute-start | bytes 1572872 | tf_op jit(solution)/shard_map/ppermute | solution.py:179
  190.3 4.2 %copy-start.14 = (f32[2,16,64,128]{3,0,2,1:T(2,128)S(1)}, f32[2,16,64,128]{3,0,2,1:T(2,128)}, u32[]{:S(2)}) copy-start(f32[2,16,64,128]{3,0,2,1:T(2,128)} %get-tuple-element.61) | copy-start | bytes 3145732
  195.4 2.1 copy-start.7
  195.4 2.1 copy-start.8
  195.4 2.1 copy-start.16
  195.4 2.1 copy-start.17
  195.4 2.1 copy-start.18
  195.4 2.1 copy-start.34
  207.5 2.1 copy-start.3
  207.5 2.1 copy-start.20
Sparse Core Ops, SparseCore 0:
  9.0 50.6 all-gather.1

commit v8 on v4

--- a/solution.py
+++ b/solution.py
@@ -62,7 +62,10 @@
     bc = bc_sum.astype(jnp.bfloat16)
     gate = zx[:, :inner_dev]
     mixin = jnp.concatenate([zx[:, inner_dev:], bc], axis=1).reshape(blocks, BLOCK, channels)
-    own_tails = mixin[:, BLOCK - (KERNEL - 1) :, :]
+    tail_rows = piece.reshape(blocks, BLOCK, WIDTH)[:, BLOCK - (KERNEL - 1) :, :]
+    tail_zx = jnp.einsum("ckw,wz->ckz", tail_rows, flat_zx[:, inner_dev:], preferred_element_type=jnp.float32)
+    tail_bc = jnp.einsum("ckw,wz->ckz", tail_rows, flat_bc, preferred_element_type=jnp.float32)
+    own_tails = jnp.concatenate([tail_zx, tail_bc], axis=2).astype(jnp.bfloat16)
     arrived = from_behind(own_tails, "seq", 1)
     wrapped = jnp.concatenate([jnp.zeros_like(arrived[:1]), arrived[:-1]], axis=0)
     before = jnp.where(place > 0, arrived, wrapped)

time: 218 us -> 220 us (level)
  waiting for transfers between devices: 97.6 us -> 90.7 us
  matrix products: 30.7 us -> 35 us
  starting transfers between devices: 4.6 us -> 7.75 us
    dot_general x0 -> x2, matrix products: none -> 5.31 us  [the longest x1 4.9 us: per_device(): jnp.einsum('ckw,wz->ckz', tail_rows, flat_zx[:, inner_dev:], preferred_el...]
    ppermute x9, waiting for transfers between devices: 61.8 us -> 58.1 us  [from_behind(): return lax.ppermute(value, axis, pairs)]
    reshape x0 -> x1, local copies, waits for them, and re-layouts: none -> 3.21 us  [per_device(): flat_bc = w_bc.reshape(WIDTH, 2 * gstate_dev)]
    all_gather x1, waiting for transfers between devices: 33.6 us -> 30.4 us  [per_device(): piece = lax.all_gather(hidden, 'mp', axis=1, tiled=True)]
    dot_general x1, matrix products: 15.7 us -> 12.6 us  [per_device(): zx_sum = jnp.dot(piece, flat_zx, preferred_element_type=jnp.float32)]
    dot_general x1, matrix products: 1.28 us -> 3.53 us  [per_device(): bc_sum = jnp.dot(piece, flat_bc, preferred_element_type=jnp.float32)]
    unnamed x52 -> x51, local copies, waits for them, and re-layouts: 22.3 us -> 21 us
  transfers between devices with their start and end apart: 13 -> 13, of which waited for: 10 -> 9; matrix products, arithmetic and copies ran while one was open for 13% -> 22% of each run, Pallas kernels for 0% -> 0%
where the time goes in v8:
time: 220 us; the launch traced here: 217 us
  waiting for transfers between devices  90.7 us (41%)
  local copies, waits for them, and re-layouts  46 us (21%)
  matrix products  35 us (16%)
  other arithmetic  23.1 us (10%)
  between operations  14 us (6%)
  starting transfers between devices  7.75 us (4%)
    ppermute x9, waiting for transfers between devices, from_behind(): return lax.ppermute(value, axis, pairs)  58.1 us
    all_gather x1, waiting for transfers between devices, per_device(): piece = lax.all_gather(hidden, 'mp', axis=1, tiled=True)  30.4 us
    unnamed x51, local copies, waits for them, and re-layouts  21 us
    dot_general x1, matrix products, per_device(): zx_sum = jnp.dot(piece, flat_zx, preferred_element_type=jnp.float32)  12.6 us
    add x5, other arithmetic, combine(): later[0][:, None, None] * earlier[1] + later[1]  9.36 us
    reshape x2, local copies, waits for them, and re-layouts, per_device(): y_total.reshape(rows_dev, inner_dev) * jax.nn.silu(gate.astype(jnp.float32))  7.28 us
    ppermute x9, starting transfers between devices, from_behind(): return lax.ppermute(value, axis, pairs)  5.91 us
    dot_general x1, matrix products, per_device(): jnp.einsum('ckw,wz->ckz', tail_rows, flat_zx[:, inner_dev:], preferred_el...  4.9 us
  transfers between devices with their start and end apart: 13, of which 9 were waited for; matrix products, arithmetic and copies ran while one was open for 22% of the time, Pallas kernels for 0%

profile of v8, /device:TPU:0, one launch (start us, length us, event | category | flops | bytes accessed | tf_op | source)
XLA Modules:
  0.0 216.5 jit_solution(9011421050624569080)
XLA Ops:
  6.5 0.7 all-gather.2.cloned.1.call-update
  7.3 0.9 select_reduce_fusion.1
  8.2 0.2 reduce-window.14
  8.3 17.2 %copy.136 = bf16[512,8,2,1024]{3,1,2,0:T(8,128)(2,1)} copy(bf16[512,8,2,1024]{3,2,1,0:T(2,128)(2,1)} %bitcast.125) | data formatting | bytes 33554432
  25.6 3.2 %reshape.262 = bf16[4096,256,1]{1,0,2:T(8,128)(2,1)S(1)} reshape(bf16[4096,2,128]{2,1,0:T(2,128)(2,1)} %param.20) | data formatting | bytes 4194304 | tf_op jit(solution)/shard_map/reshape | solution.py:56
  28.9 0.2 compare_reduce_fusion
  29.4 30.4 %all-gather.2.cloned.1.call-done = bf16[512,4096]{1,0:T(8,128)(2,1)} async-done(((bf16[512,1024]{1,0:T(8,128)(2,1)}), bf16[512,4096]{1,0:T(8,128)(2,1)}) %all-gather.2.cloned.1.call-update) | async-done | bytes 4194320 | tf_op jit(solution)/shard_map/all_gather | solution.py:57
  59.7 4.9 %fusion = bf16[2,3,1024]{2,1,0:T(4,128)(2,1)S(1)} fusion(bf16[4096,2048]{1,0:T(8,128)(2,1)} %bitcast.126, bf16[2,256,4096]{2,1,0:T(8,128)(2,1)} %bitcast.129), kind=kOutput, calls=%fused_computation.1 | convolution fusion | flops 50331648 | bytes 8466432 | tf_op jit(solution)/shard_map/ckw,wz->ckz/dot_general | solution.py:66
  64.7 0.4 fusion.42
  65.1 0.3 collective-permute-start
  65.4 12.6 %convolution_convert_fusion = bf16[512,2048]{1,0:T(8,128)(2,1)S(1)} fusion(bf16[512,4096]{1,0:T(8,128)(2,1)S(1)} %copy-done.6, bf16[4096,2048]{1,0:T(8,128)(2,1)} %bitcast.127), kind=kOutput, calls=%fused_computation.10 | convolution fusion | flops 8590983168 | bytes 23068672 | tf_op jit(solution)/shard_map/dot_general | solution.py:58
  78.0 1.0 copy-done.13
  79.0 1.2 fusion.67
  80.3 1.2 reduce-window.18
  82.1 3.5 %fusion.21 = bf16[512,256]{1,0:T(8,128)(2,1)S(1)} fusion(bf16[512,4096]{1,0:T(8,128)(2,1)} %all-gather.2.cloned.1.call-done, bf16[512,8,2,128]{3,2,1,0:T(2,128)(2,1)S(1)} %bitcast.134), kind=kOutput, calls=%fused_computation.38 | convolution fusion | flops 1073872896 | bytes 6553600 | tf_op jit(solution)/shard_map/dot_general | solution.py:59
  85.9 0.4 copy-done.21
  86.3 0.2 broadcast_select_fusion
  86.5 0.3 maximum_convert_fusion
  86.8 1.7 multiply_convert_fusion.2
  88.6 1.4 slice_convert_fusion
  90.0 2.3 %copy.110 = bf16[2,256,1024]{1,2,0:T(8,128)(2,1)} copy(bf16[2,256,1024]{2,1,0:T(8,128)(2,1)} %get-tuple-element.24) | data formatting | bytes 2097152 | tf_op jit(solution)/shard_map/slice | solution.py:98
  92.2 1.7 fusion.24
  93.9 4.6 %copy_add_fusion = (f32[2,16,64,128]{3,0,2,1:T(2,128)S(1)}, f32[2,16,64,128]{3,0,2,1:T(2,128)}) fusion(f32[2,16,64,128]{3,2,1,0:T(8,128)S(1)} %fusion.24, pred[2]{0:T(512)(128)(4,1)S(1)} %compare_reduce_fusion, f32[2,16]{0,1:T(8,128)S(1)} %copy.115, f32[2,16,64,128]{3,2,1,0:T(8,128)S(1)} %copy-done, s32[2]{0:T(128)S(1)} %fusion.50), kind=kOutput, calls=%fused_computation.44 | convolution fusion | flops 7077892 | bytes 4194442 | tf_op jit(solution)/shard_map/cr,rhpn->chpn/dot_general | solution.py:85
  98.6 0.9 constant_dynamic-slice_fusion
  99.4 0.9 copy.118
  100.3 1.6 collective-permute-start.5
  102.4 1.5 collective-permute-done.1
  103.8 1.1 copy.117
  104.9 0.8 copy-done.4
  105.7 2.0 fusion.31
  107.7 1.6 collective-permute-start.6
  109.3 16.3 %collective-permute-done.6 = f32[16,64,128]{2,1,0:T(8,128)} collective-permute-done((f32[16,64,128]{2,1,0:T(8,128)}, f32[16,64,128]{2,1,0:T(8,128)}, u32[]{:S(2)}, u32[]{:S(2)}) %collective-permute-start.6) | collective-permute-done | bytes 524320 | tf_op jit(solution)/shard_map/ppermute | solution.py:17
  125.5 1.0 slice.142
  126.5 2.0 multiply_add_fusion.3
  128.5 0.3 collective-permute-start.2
  128.8 14.4 %collective-permute-done.2 = f32[16]{0:T(128)S(1)} collective-permute-done((f32[16]{0:T(128)S(1)}, f32[16]{0:T(128)S(1)}, u32[]{:S(2)}, u32[]{:S(2)}) %collective-permute-start.2) | collective-permute-done | bytes 96 | tf_op jit(solution)/shard_map/ppermute | solution.py:17
  143.3 2.5 %collective-permute-done.7 = f32[16,64,128]{2,1,0:T(8,128)} collective-permute-done((f32[16,64,128]{2,1,0:T(8,128)}, f32[16,64,128]{2,1,0:T(8,128)}, u32[]{:S(2)}, u32[]{:S(2)}) %collective-permute-start.7) | collective-permute-done | bytes 524320 | tf_op jit(solution)/shard_map/ppermute | solution.py:17
  145.8 1.0 slice.143
  146.8 0.7 copy-done.8
  147.5 2.0 multiply_add_fusion.2
  149.5 11.9 %collective-permute-done.3 = f32[16]{0:T(128)S(1)} collective-permute-done((f32[16]{0:T(128)S(1)}, f32[16]{0:T(128)S(1)}, u32[]{:S(2)}, u32[]{:S(2)}) %collective-permute-start.3) | collective-permute-done | bytes 96 | tf_op jit(solution)/shard_map/ppermute | solution.py:17
  161.5 2.0 collective-permute-done.8
  163.5 1.0 slice.144
  164.4 0.7 copy-done.9
  165.1 2.0 multiply_add_fusion.1
  167.1 0.6 collective-permute-start.4
  167.7 9.2 %collective-permute-done.4 = f32[16]{0:T(128)S(1)} collective-permute-done((f32[16]{0:T(128)S(1)}, f32[16]{0:T(128)S(1)}, u32[]{:S(2)}, u32[]{:S(2)}) %collective-permute-start.4) | collective-permute-done | bytes 96 | tf_op jit(solution)/shard_map/ppermute | solution.py:17
  177.0 3.3 %collective-permute-start.10 = (f32[16]{0:T(128)S(1)}, f32[16]{0:T(128)S(1)}, u32[]{:S(2)}, u32[]{:S(2)}) collective-permute-start(f32[16]{0:T(128)S(1)} %fusion.56), channel_id=1, source_target_pairs={{0,64},{4,68},{8,72},{12,76},{16,80},{20,84},{24,88},{28,92},{32,9... | collective-permute-start | bytes 200 | tf_op jit(solution)/shard_map/ppermute | solution.py:17
  180.2 1.8 collective-permute-done.10
  182.2 1.0 slice.145
  183.2 1.4 add_add_fusion
  184.6 1.1 fusion.66
  185.7 1.2 fusion.33
  186.9 1.8 copy.124
  188.8 1.3 fusion.38
  190.0 1.4 copy.119
  191.5 1.4 copy.120
  193.0 0.8 fusion.25
  193.8 2.1 fusion.26
  195.9 2.6 %fusion.20 = f32[2,256,1,16,64]{1,4,3,0,2:T(8,128)S(1)} fusion(f32[2,16,64,256]{3,2,1,0:T(8,128)S(1)} %fusion.26, f32[2,256,1,16,64]{1,4,3,0,2:T(8,128)S(1)} %bitcast.135, bf16[2,256,16,64]{1,3,2,0:T(8,128)(2,1)S(1)} %bitcast.132, f32[2,16,256]{2,1,0:T(8,128)S(1)} %get-tuple-element.29, f32[2,16,256]{2,1,0:T(8,128)S(1)} %get-tuple-element.32, ...), kind=kOutput, calls=%fused_computation.32 | convolution fusion | flops 281018368 | bytes 8028224 | tf_op jit(solution)/shard_map/cgjqk,ckgjp->cqgjp/dot_general | solution.py:112
  198.6 3.8 %copy.131 = f32[2,256,1,16,64]{4,3,1,0,2:T(8,128)} copy(f32[2,256,1,16,64]{1,4,3,0,2:T(8,128)S(1)} %fusion.20) | data formatting | bytes 4194304 | tf_op jit(solution)/shard_map/reshape | solution.py:176
  202.3 3.5 %reshape.267 = f32[512,1024]{1,0:T(8,128)S(1)} reshape(f32[2,256,1,16,64]{4,3,1,0,2:T(8,128)} %copy.131) | data formatting | bytes 4194304 | tf_op jit(solution)/shard_map/reshape | solution.py:176
  205.9 2.1 multiply_reduce_fusion
  208.0 1.7 multiply_convert_fusion.3
  (91 shorter events, 2.2 us)
Async XLA Ops:
  6.5 87.4 %copy-start = (f32[2,16,64,128]{3,2,1,0:T(8,128)S(1)}, f32[2,16,64,128]{3,2,1,0:T(8,128)}, u32[]{:S(2)}) copy-start(f32[2,16,64,128]{3,2,1,0:T(8,128)} %param.30) | copy-start | bytes 3145732
  6.5 53.2 %all-gather.2.cloned.1.call-start = ((), (), s32[]{:S(2)}) async-start(), calls=%async_computation | async-start | bytes 5242880 | tf_op jit(solution)/shard_map/all_gather | solution.py:57
  25.5 3.3 %copy-start.18 = (bf16[2,3,2,128]{3,2,1,0:T(2,128)(2,1)S(1)}, bf16[2,3,2,128]{3,2,1,0:T(2,128)(2,1)}, u32[]{:S(2)}) copy-start(bf16[2,3,2,128]{3,2,1,0:T(2,128)(2,1)} %param.32) | copy-start | bytes 9220
  25.5 3.3 %copy-start.16 = (f32[1024]{0:T(1024)S(1)}, f32[1024]{0:T(1024)}, u32[]{:S(2)}) copy-start(f32[1024]{0:T(1024)} %param.23) | copy-start | bytes 12292
  25.5 3.3 %copy-start.20 = (f32[2,128]{1,0:T(2,128)S(1)}, f32[2,128]{1,0:T(2,128)}, u32[]{:S(2)}) copy-start(f32[2,128]{1,0:T(2,128)} %param.25) | copy-start | bytes 3076
  25.5 3.3 %copy-start.14 = (f32[4,1024]{1,0:T(4,128)S(1)}, f32[4,1024]{1,0:T(4,128)}, u32[]{:S(2)}) copy-start(f32[4,1024]{1,0:T(4,128)} %param.22) | copy-start | bytes 49156
  25.5 3.7 %copy-start.17 = (f32[4,2,128]{2,1,0:T(2,128)S(1)}, f32[4,2,128]{2,1,0:T(2,128)}, u32[]{:S(2)}) copy-start(f32[4,2,128]{2,1,0:T(2,128)} %param.24) | copy-start | bytes 12292
  25.5 3.8 %copy-start.22 = (f32[16]{0:T(128)S(1)}, f32[16]{0:T(128)}, u32[]{:S(2)}) copy-start(f32[16]{0:T(128)} %param.26) | copy-start | bytes 196
  59.7 4.9 %copy-start.6 = (bf16[512,4096]{1,0:T(8,128)(2,1)S(1)}, bf16[512,4096]{1,0:T(8,128)(2,1)}, u32[]{:S(2)}) copy-start(bf16[512,4096]{1,0:T(8,128)(2,1)} %all-gather.2.cloned.1.call-done) | copy-start | bytes 12582916
  65.1 20.7 %collective-permute-start = (bf16[2,3,1280]{2,0,1:T(2,128)(2,1)S(1)}, bf16[2,3,1280]{2,0,1:T(2,128)(2,1)S(1)}, u32[]{:S(2)}, u32[]{:S(2)}) collective-permute-start(bf16[2,3,1280]{2,0,1:T(2,128)(2,1)S(1)} %pad_maximum_fusion.4), channel_id=1, source_target_pairs={{0,4},{4,8},{8,12},{12,16},{16,20},{20,24},{24,28},{28,32},{32,36}... | collective-permute-start | bytes 46088 | tf_op jit(solution)/shard_map/ppermute | solution.py:17
  78.0 2.2 %copy-start.2 = (bf16[512,2048]{1,0:T(8,128)(2,1)}, bf16[512,2048]{1,0:T(8,128)(2,1)S(1)}, u32[]{:S(2)}) copy-start(bf16[512,2048]{1,0:T(8,128)(2,1)S(1)} %convolution_convert_fusion) | copy-start | bytes 6291460
  78.0 1.0 copy-start.13
  79.0 1.2 copy-start.19
  79.0 3.0 %copy-start.10 = (bf16[4096,2,128]{2,1,0:T(2,128)(2,1)S(1)}, bf16[4096,2,128]{2,1,0:T(2,128)(2,1)}, u32[]{:S(2)}) copy-start(bf16[4096,2,128]{2,1,0:T(2,128)(2,1)} %param.20) | copy-start | bytes 6291460
  82.1 3.5 %slice-start = ((bf16[512,2048]{1,0:T(8,128)(2,1)}), bf16[512,1024]{1,0:T(8,128)(2,1)S(1)}, s32[]{:S(2)}) async-start(bf16[512,2048]{1,0:T(8,128)(2,1)} %copy-done.2), calls=%async_computation.1 | async-start | bytes 2097152 | tf_op jit(solution)/shard_map/slice | solution.py:64
  85.6 0.7 copy-start.21
  88.6 1.4 copy-start.1
  100.3 4.6 %collective-permute-start.5 = (f32[16,64,128]{2,1,0:T(8,128)}, f32[16,64,128]{2,1,0:T(8,128)}, u32[]{:S(2)}, u32[]{:S(2)}) collective-permute-start(f32[16,64,128]{2,1,0:T(8,128)} %bitcast.18), channel_id=1, source_target_pairs={{0,4},{4,0},{8,12},{12,8},{16,20},{20,16},{24,28},{28,24},{32,36},... | collective-permute-start | bytes 1572872 | tf_op jit(solution)/shard_map/ppermute | solution.py:136
  102.1 1.7 collective-permute-start.1
  104.9 0.8 copy-start.4
  107.7 17.8 %collective-permute-start.6 = (f32[16,64,128]{2,1,0:T(8,128)}, f32[16,64,128]{2,1,0:T(8,128)}, u32[]{:S(2)}, u32[]{:S(2)}) collective-permute-start(f32[16,64,128]{2,1,0:T(8,128)} %fusion.31), channel_id=1, source_target_pairs={{0,8},{4,12},{8,16},{12,20},{16,24},{20,28},{24,32},{28,36},{32,40... | collective-permute-start | bytes 1572872 | tf_op jit(solution)/shard_map/ppermute | solution.py:17
  128.5 17.3 %collective-permute-start.7 = (f32[16,64,128]{2,1,0:T(8,128)}, f32[16,64,128]{2,1,0:T(8,128)}, u32[]{:S(2)}, u32[]{:S(2)}) collective-permute-start(f32[16,64,128]{2,1,0:T(8,128)} %multiply_add_fusion.3), channel_id=1, source_target_pairs={{0,16},{4,20},{8,24},{12,28},{16,32},{20,36},{24,40},{28,44},{32,4... | collective-permute-start | bytes 1572872 | tf_op jit(solution)/shard_map/ppermute | solution.py:17
  128.5 14.7 %collective-permute-start.2 = (f32[16]{0:T(128)S(1)}, f32[16]{0:T(128)S(1)}, u32[]{:S(2)}, u32[]{:S(2)}) collective-permute-start(f32[16]{0:T(128)S(1)} %get-tuple-element.18), channel_id=1, source_target_pairs={{0,8},{4,12},{8,16},{12,20},{16,24},{20,28},{24,32},{28,36},{32,40... | collective-permute-start | bytes 200 | tf_op jit(solution)/shard_map/ppermute | solution.py:17
  146.8 0.7 copy-start.8
  149.4 14.0 %collective-permute-start.8 = (f32[16,64,128]{2,1,0:T(8,128)}, f32[16,64,128]{2,1,0:T(8,128)}, u32[]{:S(2)}, u32[]{:S(2)}) collective-permute-start(f32[16,64,128]{2,1,0:T(8,128)} %multiply_add_fusion.2), channel_id=1, source_target_pairs={{0,32},{4,36},{8,40},{12,44},{16,48},{20,52},{24,56},{28,60},{32,6... | collective-permute-start | bytes 1572872 | tf_op jit(solution)/shard_map/ppermute | solution.py:17
  149.4 12.0 %collective-permute-start.3 = (f32[16]{0:T(128)S(1)}, f32[16]{0:T(128)S(1)}, u32[]{:S(2)}, u32[]{:S(2)}) collective-permute-start(f32[16]{0:T(128)S(1)} %get-tuple-element.16), channel_id=1, source_target_pairs={{0,16},{4,20},{8,24},{12,28},{16,32},{20,36},{24,40},{28,44},{32,4... | collective-permute-start | bytes 200 | tf_op jit(solution)/shard_map/ppermute | solution.py:17
  164.4 0.7 copy-start.9
  167.1 15.1 %collective-permute-start.9 = (f32[16,64,128]{2,1,0:T(8,128)}, f32[16,64,128]{2,1,0:T(8,128)}, u32[]{:S(2)}, u32[]{:S(2)}) collective-permute-start(f32[16,64,128]{2,1,0:T(8,128)} %multiply_add_fusion.1), channel_id=1, source_target_pairs={{0,64},{4,68},{8,72},{12,76},{16,80},{20,84},{24,88},{28,92},{32,9... | collective-permute-start | bytes 1572872 | tf_op jit(solution)/shard_map/ppermute | solution.py:17
  167.1 9.7 %collective-permute-start.4 = (f32[16]{0:T(128)S(1)}, f32[16]{0:T(128)S(1)}, u32[]{:S(2)}, u32[]{:S(2)}) collective-permute-start(f32[16]{0:T(128)S(1)} %fusion.59), channel_id=1, source_target_pairs={{0,32},{4,36},{8,40},{12,44},{16,48},{20,52},{24,56},{28,60},{32,6... | collective-permute-start | bytes 200 | tf_op jit(solution)/shard_map/ppermute | solution.py:17
  177.0 5.1 %collective-permute-start.10 = (f32[16]{0:T(128)S(1)}, f32[16]{0:T(128)S(1)}, u32[]{:S(2)}, u32[]{:S(2)}) collective-permute-start(f32[16]{0:T(128)S(1)} %fusion.56), channel_id=1, source_target_pairs={{0,64},{4,68},{8,72},{12,76},{16,80},{20,84},{24,88},{28,92},{32,9... | collective-permute-start | bytes 200 | tf_op jit(solution)/shard_map/ppermute | solution.py:17
  183.2 2.5 %copy-start.5 = (f32[2,8,64,128]{3,2,1,0:T(8,128)S(1)}, f32[2,8,64,128]{3,2,1,0:T(8,128)}, u32[]{:S(2)}) copy-start(f32[2,8,64,128]{3,2,1,0:T(8,128)} %copy-done.4) | copy-start | bytes 1572868
  186.9 4.6 %collective-permute-start.11 = (f32[16,64,128]{2,1,0:T(8,128)}, f32[16,64,128]{2,1,0:T(8,128)}, u32[]{:S(2)}, u32[]{:S(2)}) collective-permute-start(f32[16,64,128]{2,1,0:T(8,128)} %get-tuple-element.22), channel_id=1, source_target_pairs={{0,4},{4,0},{8,12},{12,8},{16,20},{20,16},{24,28},{28,24},{32,36},... | collective-permute-start | bytes 1572872 | tf_op jit(solution)/shard_map/ppermute | solution.py:158
  188.8 4.2 %copy-start.12 = (f32[2,16,64,128]{3,0,2,1:T(2,128)S(1)}, f32[2,16,64,128]{3,0,2,1:T(2,128)}, u32[]{:S(2)}) copy-start(f32[2,16,64,128]{3,0,2,1:T(2,128)} %get-tuple-element.39) | copy-start | bytes 3145732
  193.8 2.1 copy-start.7
  193.8 2.1 copy-start.11
  193.8 2.1 copy-start.23
  205.8 2.1 copy-start.3
  205.9 2.1 copy-start.15
Sparse Core Ops, SparseCore 0:
  9.0 50.6 all-gather.1

commit v9 on v4

--- a/solution.py
+++ b/solution.py
@@ -133,23 +133,37 @@
     got = lax.ppermute((keep(step_a, 1 - core), keep(step_b, 1 - core)), "seq", pair)
     early = jax.tree.map(lambda own, other: jnp.where(core == 0, own, other), mine, got)
     later = jax.tree.map(lambda own, other: jnp.where(core == 0, other, own), mine, got)
-    run_a, run_b = combine(early, later)
-    prior_a, prior_b = jnp.ones_like(run_a), jnp.zeros_like(run_b)
+    quarter = half // 2
+    split_heads = lambda part: [
+        part.reshape((blocks, 2, quarter) + part.shape[1:])[:, g].reshape((blocks * quarter,) + part.shape[1:])
+        for g in range(2)
+    ]
+    chip_a, chip_b = combine(early, later)
+    lanes = [list(pair) for pair in zip(split_heads(chip_a), split_heads(chip_b))]
+    priors = [[jnp.ones_like(lane[0]), jnp.zeros_like(lane[1])] for lane in lanes]
 
     def wrap(part, neutral, late):
-        moved = jnp.concatenate([jnp.full_like(part[:half], neutral), part[: rows - half]], axis=0)
+        moved = jnp.concatenate([jnp.full_like(part[:quarter], neutral), part[: part.shape[0] - quarter]], axis=0)
         return jnp.where(late, part, moved)
 
     span = 1
     while span < chips:
-        got_a, got_b = from_behind((run_a, run_b), "seq", 2 * span)
         late = chip >= span
-        lead = (wrap(got_a, 1.0, late), wrap(got_b, 0.0, late))
-        run_a, run_b = combine(lead, (run_a, run_b))
-        prior_a, prior_b = combine(lead, (prior_a, prior_b))
+        for g in range(2):
+            got_a, got_b = from_behind(tuple(lanes[g]), "seq", 2 * span)
+            lead = (wrap(got_a, 1.0, late), wrap(got_b, 0.0, late))
+            lanes[g] = list(combine(lead, tuple(lanes[g])))
+            priors[g] = list(combine(lead, tuple(priors[g])))
         span *= 2
-    lift = combine((run_a[:half], run_b[:half]), (prior_a[half:], prior_b[half:]))[1]
-    before_chip = jnp.concatenate([prior_b[:half], lift], axis=0)
+    joined = []
+    for g in range(2):
+        run_a, run_b = lanes[g]
+        prior_a, prior_b = priors[g]
+        lift = combine((run_a[:quarter], run_b[:quarter]), (prior_a[quarter:], prior_b[quarter:]))[1]
+        joined.append(jnp.concatenate([prior_b[:quarter], lift], axis=0))
+    before_chip = jnp.concatenate(
+        [part.reshape((blocks, quarter) + part.shape[1:]) for part in joined], axis=1
+    ).reshape(chip_b.shape)
     after_early = early[0][:, None, None] * before_chip + early[1]
     own_part = jnp.where(core == 0, before_chip, after_early)
     other_part = lax.ppermute(jnp.where(core == 0, after_early, before_chip), "seq", pair)

time: 218 us -> 196 us (0.90)
  waiting for transfers between devices: 97.6 us -> 83.2 us
  starting transfers between devices: 4.6 us -> 16 us
  other arithmetic: 23.2 us -> 14.2 us
  local copies, waits for them, and re-layouts: 44.1 us -> 36.1 us
    ppermute x9 -> x17, waiting for transfers between devices: 61.8 us -> 48.2 us  [from_behind(): return lax.ppermute(value, axis, pairs)]
    ppermute x9 -> x17, starting transfers between devices: 4.09 us -> 14.9 us  [from_behind(): return lax.ppermute(value, axis, pairs)]
    add x5 -> x9, other arithmetic: 9.44 us -> 1.06 us  [combine(): later[0][:, None, None] * earlier[1] + later[1]]
    slice x6 -> x13, local copies, waits for them, and re-layouts: 4.1 us -> 0.44 us  [the longest x4 3.87 us: wrap(): part[:rows - half]]
    dynamic_slice x4, local copies, waits for them, and re-layouts: 2.89 us -> 0.23 us  [keep(): piece = lax.dynamic_slice_in_dim(part, at * half, half, axis=1)]
    unnamed x52 -> x44, local copies, waits for them, and re-layouts: 22.3 us -> 20.2 us
  transfers between devices with their start and end apart: 13 -> 21, of which waited for: 10 -> 12; matrix products, arithmetic and copies ran while one was open for 13% -> 21% of each run, Pallas kernels for 0% -> 0%
where the time goes in v9:
time: 196 us; the launch traced here: 194 us
  waiting for transfers between devices  83.2 us (42%)
  local copies, waits for them, and re-layouts  36.1 us (18%)
  matrix products  30.7 us (16%)
  starting transfers between devices  16 us (8%)
  other arithmetic  14.2 us (7%)
  between operations  14.1 us (7%)
    ppermute x17, waiting for transfers between devices, from_behind(): return lax.ppermute(value, axis, pairs)  48.2 us
    all_gather x1, waiting for transfers between devices, per_device(): piece = lax.all_gather(hidden, 'mp', axis=1, tiled=True)  33.5 us
    unnamed x44, local copies, waits for them, and re-layouts  20.2 us
    dot_general x1, matrix products, per_device(): zx_sum = jnp.dot(piece, flat_zx, preferred_element_type=jnp.float32)  15.8 us
    ppermute x17, starting transfers between devices, from_behind(): return lax.ppermute(value, axis, pairs)  14.9 us
    reshape x2, local copies, waits for them, and re-layouts, per_device(): y_total.reshape(rows_dev, inner_dev) * jax.nn.silu(gate.astype(jnp.float32))  7.29 us
    dot_general x1, matrix products, per_device(): jnp.einsum('cr,rhpn->chpn', pick, state_bank, precision=lax.Precision.HIG...  4.63 us
  transfers between devices with their start and end apart: 21, of which 12 were waited for; matrix products, arithmetic and copies ran while one was open for 21% of the time, Pallas kernels for 0%

profile of v9, /device:TPU:0, one launch (start us, length us, event | category | flops | bytes accessed | tf_op | source)
XLA Modules:
  0.0 194.3 jit_solution(3872452470648923946)
XLA Ops:
  6.5 0.7 all-gather.2.cloned.1.call-update
  7.3 0.9 select_reduce_fusion.1
  8.2 0.2 reduce-window.14
  8.4 17.3 %copy.111 = bf16[512,8,2,1024]{3,1,2,0:T(8,128)(2,1)} copy(bf16[512,8,2,1024]{3,2,1,0:T(2,128)(2,1)} %bitcast.142) | data formatting | bytes 33554432
  25.8 0.2 compare_reduce_fusion
  26.0 0.2 fusion.46
  26.2 33.5 %all-gather.2.cloned.1.call-done = bf16[512,4096]{1,0:T(8,128)(2,1)} async-done(((bf16[512,1024]{1,0:T(8,128)(2,1)}), bf16[512,4096]{1,0:T(8,128)(2,1)}) %all-gather.2.cloned.1.call-update) | async-done | bytes 4194320 | tf_op jit(solution)/shard_map/all_gather | solution.py:57
  59.7 15.8 %convolution_convert_fusion = bf16[512,2048]{1,0:T(8,128)(2,1)S(1)} fusion(bf16[512,4096]{1,0:T(8,128)(2,1)} %all-gather.2.cloned.1.call-done, bf16[4096,2048]{1,0:T(8,128)(2,1)} %bitcast.143), kind=kOutput, calls=%fused_computation.8 | convolution fusion | flops 8590983168 | bytes 23068672 | tf_op jit(solution)/shard_map/dot_general | solution.py:58
  75.6 2.2 %copy-done.16 = bf16[4096,2,128]{2,1,0:T(2,128)(2,1)S(1)} copy-done((bf16[4096,2,128]{2,1,0:T(2,128)(2,1)S(1)}, bf16[4096,2,128]{2,1,0:T(2,128)(2,1)}, u32[]{:S(2)}) %copy-start.16) | copy-done | bytes 2097176
  77.9 1.3 fusion.20
  79.4 0.6 copy-done.8
  80.1 1.2 fusion.73
  81.3 0.1 copy_bitcast_fusion.1
  81.4 1.2 reduce-window.18
  82.5 0.2 slice_reduce_fusion
  82.8 0.2 slice_reduce_fusion.1
  83.0 0.1 fusion.62
  83.4 1.0 collective-permute-start.1
  84.5 0.7 collective-permute-done.1
  85.4 1.6 collective-permute-start.2
  87.1 1.3 collective-permute-start.11
  88.3 0.2 broadcast_select_fusion
  88.6 0.3 maximum_convert_fusion
  88.8 1.7 multiply_convert_fusion.2
  90.6 1.4 slice_convert_fusion
  92.0 2.3 %copy.84 = bf16[2,256,1024]{1,2,0:T(8,128)(2,1)} copy(bf16[2,256,1024]{2,1,0:T(8,128)(2,1)} %get-tuple-element.33) | data formatting | bytes 2097152 | tf_op jit(solution)/shard_map/slice | solution.py:95
  94.2 1.7 fusion.23
  95.9 4.6 %copy_add_fusion = (f32[2,16,64,128]{3,0,2,1:T(2,128)S(1)}, f32[2,16,64,128]{3,0,2,1:T(2,128)}) fusion(f32[2,16,64,128]{3,2,1,0:T(8,128)S(1)} %fusion.23, pred[2]{0:T(512)(128)(4,1)S(1)} %compare_reduce_fusion, f32[2,16]{0,1:T(8,128)S(1)} %copy.89, f32[2,16,64,128]{3,2,1,0:T(8,128)S(1)} %copy-done, s32[2]{0:T(128)S(1)} %fusion.46), kind=kOutput, calls=%fused_computation.42 | convolution fusion | flops 7077892 | bytes 4194442 | tf_op jit(solution)/shard_map/cr,rhpn->chpn/dot_general | solution.py:82
  100.9 2.8 %collective-permute-start.3 = (f32[8]{0:T(128)S(1)}, f32[8]{0:T(128)S(1)}, u32[]{:S(2)}, u32[]{:S(2)}) collective-permute-start(f32[8]{0:T(128)S(1)} %get-tuple-element.18), channel_id=1, source_target_pairs={{0,16},{4,20},{8,24},{12,28},{16,32},{20,36},{24,40},{28,44},{32,4... | collective-permute-start | bytes 104 | tf_op jit(solution)/shard_map/ppermute | solution.py:17
  103.8 1.7 collective-permute-start.12
  105.4 2.6 %collective-permute-done.3 = f32[8]{0:T(128)S(1)} collective-permute-done((f32[8]{0:T(128)S(1)}, f32[8]{0:T(128)S(1)}, u32[]{:S(2)}, u32[]{:S(2)}) %collective-permute-start.3) | collective-permute-done | bytes 64 | tf_op jit(solution)/shard_map/ppermute | solution.py:17
  108.1 0.3 collective-permute-start.4
  108.5 0.1 fusion.31
  108.6 1.3 collective-permute-start.6
  109.9 1.0 collective-permute-done.12
  111.0 0.3 collective-permute-start.13
  111.3 1.6 collective-permute-done.4
  113.0 1.5 collective-permute-start.10
  114.5 5.5 %collective-permute-done.6 = f32[8,64,128]{2,1,0:T(8,128)S(1)} collective-permute-done((f32[8,64,128]{2,1,0:T(8,128)S(1)}, f32[8,64,128]{2,1,0:T(8,128)S(1)}, u32[]{:S(2)}, u32[]{:S(2)}) %collective-permute-start.6) | collective-permute-done | bytes 262176 | tf_op jit(solution)/shard_map/ppermute | solution.py:17
  120.0 0.1 multiply_add_fusion.5
  120.3 2.4 %collective-permute-start.18 = (f32[8]{0:T(128)S(1)}, f32[8]{0:T(128)S(1)}, u32[]{:S(2)}, u32[]{:S(2)}) collective-permute-start(f32[8]{0:T(128)S(1)} %fusion.55), channel_id=1, source_target_pairs={{0,64},{4,68},{8,72},{12,76},{16,80},{20,84},{24,88},{28,92},{32,9... | collective-permute-start | bytes 104 | tf_op jit(solution)/shard_map/ppermute | solution.py:17
  122.7 5.4 %collective-permute-done.14 = f32[8,64,128]{2,1,0:T(8,128)S(1)} collective-permute-done((f32[8,64,128]{2,1,0:T(8,128)S(1)}, f32[8,64,128]{2,1,0:T(8,128)S(1)}, u32[]{:S(2)}, u32[]{:S(2)}) %collective-permute-start.14) | collective-permute-done | bytes 262176 | tf_op jit(solution)/shard_map/ppermute | solution.py:17
  128.2 0.1 multiply_add_fusion.2
  128.3 3.7 %collective-permute-done.7 = f32[8,64,128]{2,1,0:T(8,128)S(1)} collective-permute-done((f32[8,64,128]{2,1,0:T(8,128)S(1)}, f32[8,64,128]{2,1,0:T(8,128)S(1)}, u32[]{:S(2)}, u32[]{:S(2)}) %collective-permute-start.7) | collective-permute-done | bytes 262176 | tf_op jit(solution)/shard_map/ppermute | solution.py:17
  132.3 8.8 %collective-permute-done.15 = f32[8,64,128]{2,1,0:T(8,128)S(1)} collective-permute-done((f32[8,64,128]{2,1,0:T(8,128)S(1)}, f32[8,64,128]{2,1,0:T(8,128)S(1)}, u32[]{:S(2)}, u32[]{:S(2)}) %collective-permute-start.15) | collective-permute-done | bytes 262176 | tf_op jit(solution)/shard_map/ppermute | solution.py:17
  141.3 0.5 collective-permute-done.8
  141.9 1.2 collective-permute-start.9
  143.3 11.5 %collective-permute-done.16 = f32[8,64,128]{2,1,0:T(8,128)S(1)} collective-permute-done((f32[8,64,128]{2,1,0:T(8,128)S(1)}, f32[8,64,128]{2,1,0:T(8,128)S(1)}, u32[]{:S(2)}, u32[]{:S(2)}) %collective-permute-start.16) | collective-permute-done | bytes 262176 | tf_op jit(solution)/shard_map/ppermute | solution.py:17
  154.9 0.3 collective-permute-start.17
  155.3 0.2 add_add_fusion.1
  155.6 7.5 %collective-permute-done.17 = f32[8,64,128]{2,1,0:T(8,128)S(1)} collective-permute-done((f32[8,64,128]{2,1,0:T(8,128)S(1)}, f32[8,64,128]{2,1,0:T(8,128)S(1)}, u32[]{:S(2)}, u32[]{:S(2)}) %collective-permute-start.17) | collective-permute-done | bytes 262176 | tf_op jit(solution)/shard_map/ppermute | solution.py:17
  163.1 0.2 add_add_fusion
  163.5 1.1 bitcast_select_fusion.1
  164.7 1.8 copy.98
  166.5 1.3 fusion.37
  167.8 1.4 copy.93
  169.3 1.4 copy.94
  170.7 0.8 fusion.24
  171.6 2.1 %fusion.25 = f32[2,16,64,256]{3,2,1,0:T(8,128)S(1)} fusion(f32[2,16,64,128]{3,0,2,1:T(2,128)S(1)} %fusion.24, bf16[2,256,1280]{2,1,0:T(8,128)(2,1)} %copy-done.1), kind=kOutput, calls=%fused_computation.40 | convolution fusion | flops 805306368 | bytes 3276800 | tf_op jit(solution)/shard_map/cqgn,cgjpn->cqgjp/dot_general | solution.py:178
  173.7 2.6 %fusion.19 = f32[2,256,1,16,64]{1,4,3,0,2:T(8,128)S(1)} fusion(f32[2,16,64,256]{3,2,1,0:T(8,128)S(1)} %fusion.25, f32[2,256,1,16,64]{1,4,3,0,2:T(8,128)S(1)} %bitcast.149, bf16[2,256,16,64]{1,3,2,0:T(8,128)(2,1)S(1)} %bitcast.147, f32[2,16,256]{2,1,0:T(8,128)S(1)} %get-tuple-element.42, f32[2,16,256]{2,1,0:T(8,128)S(1)} %get-tuple-element.45, ...), kind=kOutput, calls=%fused_computation.30 | convolution fusion | flops 281018368 | bytes 8028224 | tf_op jit(solution)/shard_map/cgjqk,ckgjp->cqgjp/dot_general | solution.py:109
  176.3 3.8 %copy.105 = f32[2,256,1,16,64]{4,3,1,0,2:T(8,128)} copy(f32[2,256,1,16,64]{1,4,3,0,2:T(8,128)S(1)} %fusion.19) | data formatting | bytes 4194304 | tf_op jit(solution)/shard_map/reshape | solution.py:187
  180.1 3.5 %reshape.290 = f32[512,1024]{1,0:T(8,128)S(1)} reshape(f32[2,256,1,16,64]{4,3,1,0,2:T(8,128)} %copy.105) | data formatting | bytes 4194304 | tf_op jit(solution)/shard_map/reshape | solution.py:187
  183.6 2.1 %multiply_reduce_fusion = f32[512]{0:T(512)S(1)} fusion(f32[512,1024]{1,0:T(8,128)S(1)} %reshape.290, bf16[512,2048]{1,0:T(8,128)(2,1)} %copy-done.2), kind=kLoop, calls=%fused_computation.32 | loop fusion | flops 4193792 | bytes 3147776 | tf_op jit(solution)/shard_map/reduce_sum | solution.py:189
  185.7 1.7 multiply_convert_fusion.3
  (116 shorter events, 3.4 us)
Async XLA Ops:
  6.5 89.4 %copy-start = (f32[2,16,64,128]{3,2,1,0:T(8,128)S(1)}, f32[2,16,64,128]{3,2,1,0:T(8,128)}, u32[]{:S(2)}) copy-start(f32[2,16,64,128]{3,2,1,0:T(8,128)} %param.30) | copy-start | bytes 3145732
  6.5 53.2 %all-gather.2.cloned.1.call-start = ((), (), s32[]{:S(2)}) async-start(), calls=%async_computation | async-start | bytes 5242880 | tf_op jit(solution)/shard_map/all_gather | solution.py:57
  8.4 17.3 %copy-start.13 = (bf16[2,3,2,128]{3,2,1,0:T(2,128)(2,1)S(1)}, bf16[2,3,2,128]{3,2,1,0:T(2,128)(2,1)}, u32[]{:S(2)}) copy-start(bf16[2,3,2,128]{3,2,1,0:T(2,128)(2,1)} %param.32) | copy-start | bytes 9220
  8.4 17.3 %copy-start.11 = (f32[1024]{0:T(1024)S(1)}, f32[1024]{0:T(1024)}, u32[]{:S(2)}) copy-start(f32[1024]{0:T(1024)} %param.23) | copy-start | bytes 12292
  8.4 17.4 %copy-start.15 = (f32[2,128]{1,0:T(2,128)S(1)}, f32[2,128]{1,0:T(2,128)}, u32[]{:S(2)}) copy-start(f32[2,128]{1,0:T(2,128)} %param.25) | copy-start | bytes 3076
  8.4 17.4 %copy-start.9 = (f32[4,1024]{1,0:T(4,128)S(1)}, f32[4,1024]{1,0:T(4,128)}, u32[]{:S(2)}) copy-start(f32[4,1024]{1,0:T(4,128)} %param.22) | copy-start | bytes 49156
  8.4 17.8 %copy-start.12 = (f32[4,2,128]{2,1,0:T(2,128)S(1)}, f32[4,2,128]{2,1,0:T(2,128)}, u32[]{:S(2)}) copy-start(f32[4,2,128]{2,1,0:T(2,128)} %param.24) | copy-start | bytes 12292
  8.4 17.8 %copy-start.18 = (f32[16]{0:T(128)S(1)}, f32[16]{0:T(128)}, u32[]{:S(2)}) copy-start(f32[16]{0:T(128)} %param.26) | copy-start | bytes 196
  59.7 15.9 %copy-start.4 = (bf16[512,4096]{1,0:T(8,128)(2,1)S(1)}, bf16[512,4096]{1,0:T(8,128)(2,1)}, u32[]{:S(2)}) copy-start(bf16[512,4096]{1,0:T(8,128)(2,1)} %all-gather.2.cloned.1.call-done) | copy-start | bytes 12582916
  75.5 3.7 %copy-start.2 = (bf16[512,2048]{1,0:T(8,128)(2,1)}, bf16[512,2048]{1,0:T(8,128)(2,1)S(1)}, u32[]{:S(2)}) copy-start(bf16[512,2048]{1,0:T(8,128)(2,1)S(1)} %convolution_convert_fusion) | copy-start | bytes 6291460
  75.5 2.4 %copy-start.16 = (bf16[4096,2,128]{2,1,0:T(2,128)(2,1)S(1)}, bf16[4096,2,128]{2,1,0:T(2,128)(2,1)}, u32[]{:S(2)}) copy-start(bf16[4096,2,128]{2,1,0:T(2,128)(2,1)} %param.20) | copy-start | bytes 6291460
  79.2 0.9 copy-start.8
  79.3 1.9 copy-start.14
  79.3 9.0 %copy-start.17 = (bf16[2,3,1024]{2,0,1:T(2,128)(2,1)S(1)}, bf16[2,3,1024]{2,0,1:T(2,128)(2,1)}, u32[]{:S(2)}) copy-start(bf16[2,3,1024]{2,0,1:T(2,128)(2,1)} %param.31) | copy-start | bytes 36868
  79.3 9.0 %collective-permute-start = (bf16[2,3,1280]{2,0,1:T(2,128)(2,1)S(1)}, bf16[2,3,1280]{2,0,1:T(2,128)(2,1)S(1)}, u32[]{:S(2)}, u32[]{:S(2)}) collective-permute-start(bf16[2,3,1280]{2,0,1:T(2,128)(2,1)S(1)} %copy.107), channel_id=1, source_target_pairs={{0,4},{4,8},{8,12},{12,16},{16,20},{20,24},{24,28},{28,32},{32,36}... | collective-permute-start | bytes 46088 | tf_op jit(solution)/shard_map/ppermute | solution.py:17
  83.4 1.8 collective-permute-start.1
  85.4 15.3 %collective-permute-start.2 = (f32[8]{0:T(128)S(1)}, f32[8]{0:T(128)S(1)}, u32[]{:S(2)}, u32[]{:S(2)}) collective-permute-start(f32[8]{0:T(128)S(1)} %reshape_squeeze.12), channel_id=1, source_target_pairs={{0,8},{4,12},{8,16},{12,20},{16,24},{20,28},{24,32},{28,36},{32,40... | collective-permute-start | bytes 104 | tf_op jit(solution)/shard_map/ppermute | solution.py:17
  87.1 16.6 %collective-permute-start.11 = (f32[8]{0:T(128)S(1)}, f32[8]{0:T(128)S(1)}, u32[]{:S(2)}, u32[]{:S(2)}) collective-permute-start(f32[8]{0:T(128)S(1)} %reshape_squeeze.14), channel_id=1, source_target_pairs={{0,8},{4,12},{8,16},{12,20},{16,24},{20,28},{24,32},{28,36},{32,40... | collective-permute-start | bytes 104 | tf_op jit(solution)/shard_map/ppermute | solution.py:17
  90.6 1.4 copy-start.1
  100.7 7.8 %collective-permute-start.5 = (f32[16,64,128]{2,1,0:T(8,128)S(1)}, f32[16,64,128]{2,1,0:T(8,128)S(1)}, u32[]{:S(2)}, u32[]{:S(2)}) collective-permute-start(f32[16,64,128]{2,1,0:T(8,128)S(1)} %bitcast.155), channel_id=1, source_target_pairs={{0,4},{4,0},{8,12},{12,8},{16,20},{20,16},{24,28},{28,24},{32,36},... | collective-permute-start | bytes 1572872 | tf_op jit(solution)/shard_map/ppermute | solution.py:133
  100.9 7.2 %collective-permute-start.3 = (f32[8]{0:T(128)S(1)}, f32[8]{0:T(128)S(1)}, u32[]{:S(2)}, u32[]{:S(2)}) collective-permute-start(f32[8]{0:T(128)S(1)} %get-tuple-element.18), channel_id=1, source_target_pairs={{0,16},{4,20},{8,24},{12,28},{16,32},{20,36},{24,40},{28,44},{32,4... | collective-permute-start | bytes 104 | tf_op jit(solution)/shard_map/ppermute | solution.py:17
  103.8 7.2 %collective-permute-start.12 = (f32[8]{0:T(128)S(1)}, f32[8]{0:T(128)S(1)}, u32[]{:S(2)}, u32[]{:S(2)}) collective-permute-start(f32[8]{0:T(128)S(1)} %get-tuple-element.25), channel_id=1, source_target_pairs={{0,16},{4,20},{8,24},{12,28},{16,32},{20,36},{24,40},{28,44},{32,4... | collective-permute-start | bytes 104 | tf_op jit(solution)/shard_map/ppermute | solution.py:17
  108.1 4.8 %collective-permute-start.4 = (f32[8]{0:T(128)S(1)}, f32[8]{0:T(128)S(1)}, u32[]{:S(2)}, u32[]{:S(2)}) collective-permute-start(f32[8]{0:T(128)S(1)} %fusion.58), channel_id=1, source_target_pairs={{0,32},{4,36},{8,40},{12,44},{16,48},{20,52},{24,56},{28,60},{32,6... | collective-permute-start | bytes 104 | tf_op jit(solution)/shard_map/ppermute | solution.py:17
  108.6 11.4 %collective-permute-start.6 = (f32[8,64,128]{2,1,0:T(8,128)S(1)}, f32[8,64,128]{2,1,0:T(8,128)S(1)}, u32[]{:S(2)}, u32[]{:S(2)}) collective-permute-start(f32[8,64,128]{2,1,0:T(8,128)S(1)} %bitcast.154), channel_id=1, source_target_pairs={{0,8},{4,12},{8,16},{12,20},{16,24},{20,28},{24,32},{28,36},{32,40... | collective-permute-start | bytes 786440 | tf_op jit(solution)/shard_map/ppermute | solution.py:17
  111.0 9.2 %collective-permute-start.13 = (f32[8]{0:T(128)S(1)}, f32[8]{0:T(128)S(1)}, u32[]{:S(2)}, u32[]{:S(2)}) collective-permute-start(f32[8]{0:T(128)S(1)} %fusion.60), channel_id=1, source_target_pairs={{0,32},{4,36},{8,40},{12,44},{16,48},{20,52},{24,56},{28,60},{32,6... | collective-permute-start | bytes 104 | tf_op jit(solution)/shard_map/ppermute | solution.py:17
  113.0 19.2 %collective-permute-start.10 = (f32[8]{0:T(128)S(1)}, f32[8]{0:T(128)S(1)}, u32[]{:S(2)}, u32[]{:S(2)}) collective-permute-start(f32[8]{0:T(128)S(1)} %fusion.53), channel_id=1, source_target_pairs={{0,64},{4,68},{8,72},{12,76},{16,80},{20,84},{24,88},{28,92},{32,9... | collective-permute-start | bytes 104 | tf_op jit(solution)/shard_map/ppermute | solution.py:17
  114.5 13.6 %collective-permute-start.14 = (f32[8,64,128]{2,1,0:T(8,128)S(1)}, f32[8,64,128]{2,1,0:T(8,128)S(1)}, u32[]{:S(2)}, u32[]{:S(2)}) collective-permute-start(f32[8,64,128]{2,1,0:T(8,128)S(1)} %bitcast.153), channel_id=1, source_target_pairs={{0,8},{4,12},{8,16},{12,20},{16,24},{20,28},{24,32},{28,36},{32,40... | collective-permute-start | bytes 786440 | tf_op jit(solution)/shard_map/ppermute | solution.py:17
  120.1 11.9 %collective-permute-start.7 = (f32[8,64,128]{2,1,0:T(8,128)S(1)}, f32[8,64,128]{2,1,0:T(8,128)S(1)}, u32[]{:S(2)}, u32[]{:S(2)}) collective-permute-start(f32[8,64,128]{2,1,0:T(8,128)S(1)} %multiply_add_fusion.5), channel_id=1, source_target_pairs={{0,16},{4,20},{8,24},{12,28},{16,32},{20,36},{24,40},{28,44},{32,4... | collective-permute-start | bytes 786440 | tf_op jit(solution)/shard_map/ppermute | solution.py:17
  120.3 22.8 %collective-permute-start.18 = (f32[8]{0:T(128)S(1)}, f32[8]{0:T(128)S(1)}, u32[]{:S(2)}, u32[]{:S(2)}) collective-permute-start(f32[8]{0:T(128)S(1)} %fusion.55), channel_id=1, source_target_pairs={{0,64},{4,68},{8,72},{12,76},{16,80},{20,84},{24,88},{28,92},{32,9... | collective-permute-start | bytes 104 | tf_op jit(solution)/shard_map/ppermute | solution.py:17
  128.3 12.9 %collective-permute-start.15 = (f32[8,64,128]{2,1,0:T(8,128)S(1)}, f32[8,64,128]{2,1,0:T(8,128)S(1)}, u32[]{:S(2)}, u32[]{:S(2)}) collective-permute-start(f32[8,64,128]{2,1,0:T(8,128)S(1)} %multiply_add_fusion.2), channel_id=1, source_target_pairs={{0,16},{4,20},{8,24},{12,28},{16,32},{20,36},{24,40},{28,44},{32,4... | collective-permute-start | bytes 786440 | tf_op jit(solution)/shard_map/ppermute | solution.py:17
  132.1 9.7 %collective-permute-start.8 = (f32[8,64,128]{2,1,0:T(8,128)S(1)}, f32[8,64,128]{2,1,0:T(8,128)S(1)}, u32[]{:S(2)}, u32[]{:S(2)}) collective-permute-start(f32[8,64,128]{2,1,0:T(8,128)S(1)} %multiply_add_fusion.4), channel_id=1, source_target_pairs={{0,32},{4,36},{8,40},{12,44},{16,48},{20,52},{24,56},{28,60},{32,6... | collective-permute-start | bytes 786440 | tf_op jit(solution)/shard_map/ppermute | solution.py:17
  141.2 13.6 %collective-permute-start.16 = (f32[8,64,128]{2,1,0:T(8,128)S(1)}, f32[8,64,128]{2,1,0:T(8,128)S(1)}, u32[]{:S(2)}, u32[]{:S(2)}) collective-permute-start(f32[8,64,128]{2,1,0:T(8,128)S(1)} %multiply_add_fusion.1), channel_id=1, source_target_pairs={{0,32},{4,36},{8,40},{12,44},{16,48},{20,52},{24,56},{28,60},{32,6... | collective-permute-start | bytes 786440 | tf_op jit(solution)/shard_map/ppermute | solution.py:17
  141.9 13.3 %collective-permute-start.9 = (f32[8,64,128]{2,1,0:T(8,128)S(1)}, f32[8,64,128]{2,1,0:T(8,128)S(1)}, u32[]{:S(2)}, u32[]{:S(2)}) collective-permute-start(f32[8,64,128]{2,1,0:T(8,128)S(1)} %multiply_add_fusion.3), channel_id=1, source_target_pairs={{0,64},{4,68},{8,72},{12,76},{16,80},{20,84},{24,88},{28,92},{32,9... | collective-permute-start | bytes 786440 | tf_op jit(solution)/shard_map/ppermute | solution.py:17
  154.9 8.2 %collective-permute-start.17 = (f32[8,64,128]{2,1,0:T(8,128)S(1)}, f32[8,64,128]{2,1,0:T(8,128)S(1)}, u32[]{:S(2)}, u32[]{:S(2)}) collective-permute-start(f32[8,64,128]{2,1,0:T(8,128)S(1)} %multiply_add_fusion), channel_id=1, source_target_pairs={{0,64},{4,68},{8,72},{12,76},{16,80},{20,84},{24,88},{28,92},{32,9... | collective-permute-start | bytes 786440 | tf_op jit(solution)/shard_map/ppermute | solution.py:17
  164.6 4.6 %collective-permute-start.19 = (f32[16,64,128]{2,1,0:T(8,128)}, f32[16,64,128]{2,1,0:T(8,128)}, u32[]{:S(2)}, u32[]{:S(2)}) collective-permute-start(f32[16,64,128]{2,1,0:T(8,128)} %get-tuple-element.31), channel_id=1, source_target_pairs={{0,4},{4,0},{8,12},{12,8},{16,20},{20,16},{24,28},{28,24},{32,36},... | collective-permute-start | bytes 1572872 | tf_op jit(solution)/shard_map/ppermute | solution.py:169
  166.5 4.2 %copy-start.7 = (f32[2,16,64,128]{3,0,2,1:T(2,128)S(1)}, f32[2,16,64,128]{3,0,2,1:T(2,128)}, u32[]{:S(2)}) copy-start(f32[2,16,64,128]{3,0,2,1:T(2,128)} %get-tuple-element.52) | copy-start | bytes 3145732
  171.6 2.1 %copy-start.5 = (bf16[2,256,1024]{1,2,0:T(8,128)(2,1)S(1)}, bf16[2,256,1024]{1,2,0:T(8,128)(2,1)}, u32[]{:S(2)}) copy-start(bf16[2,256,1024]{1,2,0:T(8,128)(2,1)} %copy.84) | copy-start | bytes 3145732
  171.6 2.1 %copy-start.6 = (f32[2,256,1024]{1,2,0:T(8,128)S(1)}, f32[2,256,1024]{1,2,0:T(8,128)}, u32[]{:S(2)}) copy-start(f32[2,256,1024]{1,2,0:T(8,128)} %copy.98) | copy-start | bytes 6291460
  171.6 2.1 %copy-start.19 = (f32[16]{0:T(128)S(1)}, f32[16]{0:T(128)}, u32[]{:S(2)}) copy-start(f32[16]{0:T(128)} %param.28) | copy-start | bytes 196
  183.6 2.1 %copy-start.3 = (bf16[512,2048]{1,0:T(8,128)(2,1)S(1)}, bf16[512,2048]{1,0:T(8,128)(2,1)}, u32[]{:S(2)}) copy-start(bf16[512,2048]{1,0:T(8,128)(2,1)} %copy-done.2) | copy-start | bytes 6291460
  183.6 2.1 %copy-start.10 = (f32[1024]{0:T(1024)S(1)}, f32[1024]{0:T(1024)}, u32[]{:S(2)}) copy-start(f32[1024]{0:T(1024)} %param.29) | copy-start | bytes 12292
Sparse Core Ops, SparseCore 0:
  9.0 50.6 all-gather.1

commit v10 on v9

--- a/solution.py
+++ b/solution.py
@@ -167,13 +167,11 @@
     after_early = early[0][:, None, None] * before_chip + early[1]
     own_part = jnp.where(core == 0, before_chip, after_early)
     other_part = lax.ppermute(jnp.where(core == 0, after_early, before_chip), "seq", pair)
-    split_rows = lambda part: part.reshape((blocks, half) + part.shape[1:])
-    own_part, other_part = split_rows(own_part), split_rows(other_part)
-    previous = jnp.where(
-        core == 0,
-        jnp.concatenate([own_part, other_part], axis=1),
-        jnp.concatenate([other_part, own_part], axis=1),
-    )
+    previous = []
+    for r in range(blocks):
+        own_r, other_r = own_part[r * half : (r + 1) * half], other_part[r * half : (r + 1) * half]
+        previous.append(jnp.where(core == 0, jnp.concatenate([own_r, other_r]), jnp.concatenate([other_r, own_r])))
+    previous = jnp.stack(previous)
     state_in = jnp.where(first[:, None, None, None], bank_state, previous)
     read = jnp.einsum(
         "cqgn,cgjpn->cqgjp",

time: 196 us -> 196 us (level)
    reshape x2 -> x0, local copies, waits for them, and re-layouts: 2.9 us -> none  [per_device(): split_rows = lambda part: part.reshape((blocks, half) + part.shape[1:])]
    concatenate x0 -> x2, local copies, waits for them, and re-layouts: none -> 2.22 us  [per_device(): jnp.concatenate([own_r, other_r])]
where the time goes in v10:
time: 196 us; the launch traced here: 194 us
  waiting for transfers between devices  83.3 us (42%)
  local copies, waits for them, and re-layouts  35.4 us (18%)
  matrix products  30.6 us (16%)
  starting transfers between devices  15.9 us (8%)
  other arithmetic  15.2 us (8%)
  between operations  14.2 us (7%)
    ppermute x17, waiting for transfers between devices, from_behind(): return lax.ppermute(value, axis, pairs)  48.4 us
    all_gather x1, waiting for transfers between devices, per_device(): piece = lax.all_gather(hidden, 'mp', axis=1, tiled=True)  33.5 us
    unnamed x44, local copies, waits for them, and re-layouts  20.2 us
    dot_general x1, matrix products, per_device(): zx_sum = jnp.dot(piece, flat_zx, preferred_element_type=jnp.float32)  15.7 us
    ppermute x17, starting transfers between devices, from_behind(): return lax.ppermute(value, axis, pairs)  14.8 us
    reshape x2, local copies, waits for them, and re-layouts, per_device(): y_total.reshape(rows_dev, inner_dev) * jax.nn.silu(gate.astype(jnp.float32))  7.28 us
    dot_general x1, matrix products, per_device(): jnp.einsum('cr,rhpn->chpn', pick, state_bank, precision=lax.Precision.HIG...  4.63 us
  transfers between devices with their start and end apart: 21, of which 12 were waited for; matrix products, arithmetic and copies ran while one was open for 21% of the time, Pallas kernels for 0%

profile of v10, /device:TPU:0, one launch (start us, length us, event | category | flops | bytes accessed | tf_op | source)
XLA Modules:
  0.0 194.5 jit_solution(11082870028118530127)
XLA Ops:
  6.5 0.7 all-gather.2.cloned.1.call-update
  7.3 0.9 select_reduce_fusion.1
  8.2 0.2 reduce-window.14
  8.4 17.2 %copy.109 = bf16[512,8,2,1024]{3,1,2,0:T(8,128)(2,1)} copy(bf16[512,8,2,1024]{3,2,1,0:T(2,128)(2,1)} %bitcast.147) | data formatting | bytes 33554432
  25.8 0.2 compare_reduce_fusion
  25.9 0.2 fusion.45
  26.2 33.5 %all-gather.2.cloned.1.call-done = bf16[512,4096]{1,0:T(8,128)(2,1)} async-done(((bf16[512,1024]{1,0:T(8,128)(2,1)}), bf16[512,4096]{1,0:T(8,128)(2,1)}) %all-gather.2.cloned.1.call-update) | async-done | bytes 4194320 | tf_op jit(solution)/shard_map/all_gather | solution.py:57
  59.7 15.7 %convolution_convert_fusion = bf16[512,2048]{1,0:T(8,128)(2,1)S(1)} fusion(bf16[512,4096]{1,0:T(8,128)(2,1)} %all-gather.2.cloned.1.call-done, bf16[4096,2048]{1,0:T(8,128)(2,1)} %bitcast.148), kind=kOutput, calls=%fused_computation.8 | convolution fusion | flops 8590983168 | bytes 23068672 | tf_op jit(solution)/shard_map/dot_general | solution.py:58
  75.6 2.2 %copy-done.16 = bf16[4096,2,128]{2,1,0:T(2,128)(2,1)S(1)} copy-done((bf16[4096,2,128]{2,1,0:T(2,128)(2,1)S(1)}, bf16[4096,2,128]{2,1,0:T(2,128)(2,1)}, u32[]{:S(2)}) %copy-start.16) | copy-done | bytes 2097176
  77.8 1.3 fusion.20
  79.4 0.6 copy-done.8
  80.1 1.2 fusion.72
  81.2 0.1 copy_bitcast_fusion.1
  81.3 1.2 reduce-window.18
  82.5 0.2 slice_reduce_fusion
  82.8 0.2 slice_reduce_fusion.1
  83.0 0.1 fusion.61
  83.4 1.0 collective-permute-start.1
  84.5 0.7 collective-permute-done.1
  85.4 1.6 collective-permute-start.2
  87.1 1.3 collective-permute-start.11
  88.3 0.2 broadcast_select_fusion.1
  88.5 0.3 maximum_convert_fusion
  88.8 1.7 multiply_convert_fusion.2
  90.6 1.4 slice_convert_fusion
  92.0 2.3 %copy.84 = bf16[2,256,1024]{1,2,0:T(8,128)(2,1)} copy(bf16[2,256,1024]{2,1,0:T(8,128)(2,1)} %get-tuple-element.33) | data formatting | bytes 2097152 | tf_op jit(solution)/shard_map/slice | solution.py:95
  94.2 1.7 fusion.23
  95.9 4.6 %copy_add_fusion = (f32[2,16,64,128]{3,0,2,1:T(2,128)S(1)}, f32[2,16,64,128]{3,0,2,1:T(2,128)}) fusion(f32[2,16,64,128]{3,2,1,0:T(8,128)S(1)} %fusion.23, pred[2]{0:T(512)(128)(4,1)S(1)} %compare_reduce_fusion, f32[2,16]{0,1:T(8,128)S(1)} %copy.89, f32[2,16,64,128]{3,2,1,0:T(8,128)S(1)} %copy-done, s32[2]{0:T(128)S(1)} %fusion.45), kind=kOutput, calls=%fused_computation.41 | convolution fusion | flops 7077892 | bytes 4194442 | tf_op jit(solution)/shard_map/cr,rhpn->chpn/dot_general | solution.py:82
  100.9 2.8 %collective-permute-start.3 = (f32[8]{0:T(128)S(1)}, f32[8]{0:T(128)S(1)}, u32[]{:S(2)}, u32[]{:S(2)}) collective-permute-start(f32[8]{0:T(128)S(1)} %get-tuple-element.18), channel_id=1, source_target_pairs={{0,16},{4,20},{8,24},{12,28},{16,32},{20,36},{24,40},{28,44},{32,4... | collective-permute-start | bytes 104 | tf_op jit(solution)/shard_map/ppermute | solution.py:17
  103.7 1.7 collective-permute-start.12
  105.4 2.7 %collective-permute-done.3 = f32[8]{0:T(128)S(1)} collective-permute-done((f32[8]{0:T(128)S(1)}, f32[8]{0:T(128)S(1)}, u32[]{:S(2)}, u32[]{:S(2)}) %collective-permute-start.3) | collective-permute-done | bytes 64 | tf_op jit(solution)/shard_map/ppermute | solution.py:17
  108.1 0.2 collective-permute-start.4
  108.4 0.1 fusion.30
  108.6 1.3 collective-permute-start.6
  109.9 1.0 collective-permute-done.12
  111.0 0.3 collective-permute-start.13
  111.2 1.7 collective-permute-done.4
  113.0 1.5 collective-permute-start.10
  114.5 5.5 %collective-permute-done.6 = f32[8,64,128]{2,1,0:T(8,128)S(1)} collective-permute-done((f32[8,64,128]{2,1,0:T(8,128)S(1)}, f32[8,64,128]{2,1,0:T(8,128)S(1)}, u32[]{:S(2)}, u32[]{:S(2)}) %collective-permute-start.6) | collective-permute-done | bytes 262176 | tf_op jit(solution)/shard_map/ppermute | solution.py:17
  120.0 0.1 multiply_add_fusion.5
  120.3 2.3 %collective-permute-start.18 = (f32[8]{0:T(128)S(1)}, f32[8]{0:T(128)S(1)}, u32[]{:S(2)}, u32[]{:S(2)}) collective-permute-start(f32[8]{0:T(128)S(1)} %fusion.54), channel_id=1, source_target_pairs={{0,64},{4,68},{8,72},{12,76},{16,80},{20,84},{24,88},{28,92},{32,9... | collective-permute-start | bytes 104 | tf_op jit(solution)/shard_map/ppermute | solution.py:17
  122.7 5.4 %collective-permute-done.14 = f32[8,64,128]{2,1,0:T(8,128)S(1)} collective-permute-done((f32[8,64,128]{2,1,0:T(8,128)S(1)}, f32[8,64,128]{2,1,0:T(8,128)S(1)}, u32[]{:S(2)}, u32[]{:S(2)}) %collective-permute-start.14) | collective-permute-done | bytes 262176 | tf_op jit(solution)/shard_map/ppermute | solution.py:17
  128.3 3.7 %collective-permute-done.7 = f32[8,64,128]{2,1,0:T(8,128)S(1)} collective-permute-done((f32[8,64,128]{2,1,0:T(8,128)S(1)}, f32[8,64,128]{2,1,0:T(8,128)S(1)}, u32[]{:S(2)}, u32[]{:S(2)}) %collective-permute-start.7) | collective-permute-done | bytes 262176 | tf_op jit(solution)/shard_map/ppermute | solution.py:17
  132.3 8.8 %collective-permute-done.15 = f32[8,64,128]{2,1,0:T(8,128)S(1)} collective-permute-done((f32[8,64,128]{2,1,0:T(8,128)S(1)}, f32[8,64,128]{2,1,0:T(8,128)S(1)}, u32[]{:S(2)}, u32[]{:S(2)}) %collective-permute-start.15) | collective-permute-done | bytes 262176 | tf_op jit(solution)/shard_map/ppermute | solution.py:17
  141.3 0.6 collective-permute-done.8
  141.9 1.2 collective-permute-start.9
  143.3 11.5 %collective-permute-done.16 = f32[8,64,128]{2,1,0:T(8,128)S(1)} collective-permute-done((f32[8,64,128]{2,1,0:T(8,128)S(1)}, f32[8,64,128]{2,1,0:T(8,128)S(1)}, u32[]{:S(2)}, u32[]{:S(2)}) %collective-permute-start.16) | collective-permute-done | bytes 262176 | tf_op jit(solution)/shard_map/ppermute | solution.py:17
  154.9 0.3 collective-permute-start.17
  155.2 0.2 add_add_fusion.1
  155.6 7.5 %collective-permute-done.17 = f32[8,64,128]{2,1,0:T(8,128)S(1)} collective-permute-done((f32[8,64,128]{2,1,0:T(8,128)S(1)}, f32[8,64,128]{2,1,0:T(8,128)S(1)}, u32[]{:S(2)}, u32[]{:S(2)}) %collective-permute-start.17) | collective-permute-done | bytes 262176 | tf_op jit(solution)/shard_map/ppermute | solution.py:17
  163.1 0.2 add_add_fusion
  163.5 1.2 bitcast_select_fusion.1
  164.7 1.8 copy.96
  166.5 1.2 fusion.36
  167.7 1.2 slice_bitcast_fusion.1
  168.9 1.1 slice_bitcast_fusion
  170.0 0.6 broadcast_select_fusion
  170.6 1.1 maximum_select_fusion
  171.8 2.1 %fusion.24 = f32[2,16,64,256]{3,2,1,0:T(8,128)S(1)} fusion(f32[2,16,64,128]{3,0,2,1:T(2,128)S(1)} %maximum_select_fusion, bf16[2,256,1280]{2,1,0:T(8,128)(2,1)} %copy-done.1), kind=kOutput, calls=%fused_computation.39 | convolution fusion | flops 805306368 | bytes 3276800 | tf_op jit(solution)/shard_map/cqgn,cgjpn->cqgjp/dot_general | solution.py:176
  173.9 2.6 %fusion.19 = f32[2,256,1,16,64]{1,4,3,0,2:T(8,128)S(1)} fusion(f32[2,16,64,256]{3,2,1,0:T(8,128)S(1)} %fusion.24, f32[2,256,1,16,64]{1,4,3,0,2:T(8,128)S(1)} %bitcast.153, bf16[2,256,16,64]{1,3,2,0:T(8,128)(2,1)S(1)} %bitcast.152, f32[2,16,256]{2,1,0:T(8,128)S(1)} %get-tuple-element.46, f32[2,16,256]{2,1,0:T(8,128)S(1)} %get-tuple-element.49, ...), kind=kOutput, calls=%fused_computation.30 | convolution fusion | flops 281018368 | bytes 8028224 | tf_op jit(solution)/shard_map/cgjqk,ckgjp->cqgjp/dot_general | solution.py:109
  176.5 3.8 %copy.103 = f32[2,256,1,16,64]{4,3,1,0,2:T(8,128)} copy(f32[2,256,1,16,64]{1,4,3,0,2:T(8,128)S(1)} %fusion.19) | data formatting | bytes 4194304 | tf_op jit(solution)/shard_map/reshape | solution.py:185
  180.3 3.5 %reshape.392 = f32[512,1024]{1,0:T(8,128)S(1)} reshape(f32[2,256,1,16,64]{4,3,1,0,2:T(8,128)} %copy.103) | data formatting | bytes 4194304 | tf_op jit(solution)/shard_map/reshape | solution.py:185
  183.8 2.1 %multiply_reduce_fusion = f32[512]{0:T(512)S(1)} fusion(f32[512,1024]{1,0:T(8,128)S(1)} %reshape.392, bf16[512,2048]{1,0:T(8,128)(2,1)} %copy-done.2), kind=kLoop, calls=%fused_computation.32 | loop fusion | flops 4193792 | bytes 3147776 | tf_op jit(solution)/shard_map/reduce_sum | solution.py:187
  185.9 1.7 multiply_convert_fusion.3
  (118 shorter events, 3.6 us)
Async XLA Ops:
  6.5 89.4 %copy-start = (f32[2,16,64,128]{3,2,1,0:T(8,128)S(1)}, f32[2,16,64,128]{3,2,1,0:T(8,128)}, u32[]{:S(2)}) copy-start(f32[2,16,64,128]{3,2,1,0:T(8,128)} %param.30) | copy-start | bytes 3145732
  6.5 53.2 %all-gather.2.cloned.1.call-start = ((), (), s32[]{:S(2)}) async-start(), calls=%async_computation | async-start | bytes 5242880 | tf_op jit(solution)/shard_map/all_gather | solution.py:57
  8.4 17.3 %copy-start.13 = (bf16[2,3,2,128]{3,2,1,0:T(2,128)(2,1)S(1)}, bf16[2,3,2,128]{3,2,1,0:T(2,128)(2,1)}, u32[]{:S(2)}) copy-start(bf16[2,3,2,128]{3,2,1,0:T(2,128)(2,1)} %param.32) | copy-start | bytes 9220
  8.4 17.3 %copy-start.11 = (f32[1024]{0:T(1024)S(1)}, f32[1024]{0:T(1024)}, u32[]{:S(2)}) copy-start(f32[1024]{0:T(1024)} %param.23) | copy-start | bytes 12292
  8.4 17.3 %copy-start.15 = (f32[2,128]{1,0:T(2,128)S(1)}, f32[2,128]{1,0:T(2,128)}, u32[]{:S(2)}) copy-start(f32[2,128]{1,0:T(2,128)} %param.25) | copy-start | bytes 3076
  8.4 17.4 %copy-start.9 = (f32[4,1024]{1,0:T(4,128)S(1)}, f32[4,1024]{1,0:T(4,128)}, u32[]{:S(2)}) copy-start(f32[4,1024]{1,0:T(4,128)} %param.22) | copy-start | bytes 49156
  8.4 17.8 %copy-start.12 = (f32[4,2,128]{2,1,0:T(2,128)S(1)}, f32[4,2,128]{2,1,0:T(2,128)}, u32[]{:S(2)}) copy-start(f32[4,2,128]{2,1,0:T(2,128)} %param.24) | copy-start | bytes 12292
  8.4 17.8 %copy-start.18 = (f32[16]{0:T(128)S(1)}, f32[16]{0:T(128)}, u32[]{:S(2)}) copy-start(f32[16]{0:T(128)} %param.26) | copy-start | bytes 196
  59.7 15.9 %copy-start.4 = (bf16[512,4096]{1,0:T(8,128)(2,1)S(1)}, bf16[512,4096]{1,0:T(8,128)(2,1)}, u32[]{:S(2)}) copy-start(bf16[512,4096]{1,0:T(8,128)(2,1)} %all-gather.2.cloned.1.call-done) | copy-start | bytes 12582916
  75.5 3.6 %copy-start.2 = (bf16[512,2048]{1,0:T(8,128)(2,1)}, bf16[512,2048]{1,0:T(8,128)(2,1)S(1)}, u32[]{:S(2)}) copy-start(bf16[512,2048]{1,0:T(8,128)(2,1)S(1)} %convolution_convert_fusion) | copy-start | bytes 6291460
  75.5 2.4 %copy-start.16 = (bf16[4096,2,128]{2,1,0:T(2,128)(2,1)S(1)}, bf16[4096,2,128]{2,1,0:T(2,128)(2,1)}, u32[]{:S(2)}) copy-start(bf16[4096,2,128]{2,1,0:T(2,128)(2,1)} %param.20) | copy-start | bytes 6291460
  79.1 0.9 copy-start.8
  79.3 1.9 copy-start.14
  79.3 9.0 %copy-start.17 = (bf16[2,3,1024]{2,0,1:T(2,128)(2,1)S(1)}, bf16[2,3,1024]{2,0,1:T(2,128)(2,1)}, u32[]{:S(2)}) copy-start(bf16[2,3,1024]{2,0,1:T(2,128)(2,1)} %param.31) | copy-start | bytes 36868
  79.3 9.0 %collective-permute-start = (bf16[2,3,1280]{2,0,1:T(2,128)(2,1)S(1)}, bf16[2,3,1280]{2,0,1:T(2,128)(2,1)S(1)}, u32[]{:S(2)}, u32[]{:S(2)}) collective-permute-start(bf16[2,3,1280]{2,0,1:T(2,128)(2,1)S(1)} %copy.105), channel_id=1, source_target_pairs={{0,4},{4,8},{8,12},{12,16},{16,20},{20,24},{24,28},{28,32},{32,36}... | collective-permute-start | bytes 46088 | tf_op jit(solution)/shard_map/ppermute | solution.py:17
  83.4 1.8 collective-permute-start.1
  85.4 15.4 %collective-permute-start.2 = (f32[8]{0:T(128)S(1)}, f32[8]{0:T(128)S(1)}, u32[]{:S(2)}, u32[]{:S(2)}) collective-permute-start(f32[8]{0:T(128)S(1)} %reshape_squeeze.12), channel_id=1, source_target_pairs={{0,8},{4,12},{8,16},{12,20},{16,24},{20,28},{24,32},{28,36},{32,40... | collective-permute-start | bytes 104 | tf_op jit(solution)/shard_map/ppermute | solution.py:17
  87.1 16.6 %collective-permute-start.11 = (f32[8]{0:T(128)S(1)}, f32[8]{0:T(128)S(1)}, u32[]{:S(2)}, u32[]{:S(2)}) collective-permute-start(f32[8]{0:T(128)S(1)} %reshape_squeeze.14), channel_id=1, source_target_pairs={{0,8},{4,12},{8,16},{12,20},{16,24},{20,28},{24,32},{28,36},{32,40... | collective-permute-start | bytes 104 | tf_op jit(solution)/shard_map/ppermute | solution.py:17
  90.6 1.4 copy-start.1
  100.7 7.8 %collective-permute-start.5 = (f32[16,64,128]{2,1,0:T(8,128)S(1)}, f32[16,64,128]{2,1,0:T(8,128)S(1)}, u32[]{:S(2)}, u32[]{:S(2)}) collective-permute-start(f32[16,64,128]{2,1,0:T(8,128)S(1)} %bitcast.162), channel_id=1, source_target_pairs={{0,4},{4,0},{8,12},{12,8},{16,20},{20,16},{24,28},{28,24},{32,36},... | collective-permute-start | bytes 1572872 | tf_op jit(solution)/shard_map/ppermute | solution.py:133
  100.9 7.2 %collective-permute-start.3 = (f32[8]{0:T(128)S(1)}, f32[8]{0:T(128)S(1)}, u32[]{:S(2)}, u32[]{:S(2)}) collective-permute-start(f32[8]{0:T(128)S(1)} %get-tuple-element.18), channel_id=1, source_target_pairs={{0,16},{4,20},{8,24},{12,28},{16,32},{20,36},{24,40},{28,44},{32,4... | collective-permute-start | bytes 104 | tf_op jit(solution)/shard_map/ppermute | solution.py:17
  103.7 7.2 %collective-permute-start.12 = (f32[8]{0:T(128)S(1)}, f32[8]{0:T(128)S(1)}, u32[]{:S(2)}, u32[]{:S(2)}) collective-permute-start(f32[8]{0:T(128)S(1)} %get-tuple-element.25), channel_id=1, source_target_pairs={{0,16},{4,20},{8,24},{12,28},{16,32},{20,36},{24,40},{28,44},{32,4... | collective-permute-start | bytes 104 | tf_op jit(solution)/shard_map/ppermute | solution.py:17
  108.1 4.8 %collective-permute-start.4 = (f32[8]{0:T(128)S(1)}, f32[8]{0:T(128)S(1)}, u32[]{:S(2)}, u32[]{:S(2)}) collective-permute-start(f32[8]{0:T(128)S(1)} %fusion.57), channel_id=1, source_target_pairs={{0,32},{4,36},{8,40},{12,44},{16,48},{20,52},{24,56},{28,60},{32,6... | collective-permute-start | bytes 104 | tf_op jit(solution)/shard_map/ppermute | solution.py:17
  108.6 11.4 %collective-permute-start.6 = (f32[8,64,128]{2,1,0:T(8,128)S(1)}, f32[8,64,128]{2,1,0:T(8,128)S(1)}, u32[]{:S(2)}, u32[]{:S(2)}) collective-permute-start(f32[8,64,128]{2,1,0:T(8,128)S(1)} %bitcast.159), channel_id=1, source_target_pairs={{0,8},{4,12},{8,16},{12,20},{16,24},{20,28},{24,32},{28,36},{32,40... | collective-permute-start | bytes 786440 | tf_op jit(solution)/shard_map/ppermute | solution.py:17
  111.0 9.2 %collective-permute-start.13 = (f32[8]{0:T(128)S(1)}, f32[8]{0:T(128)S(1)}, u32[]{:S(2)}, u32[]{:S(2)}) collective-permute-start(f32[8]{0:T(128)S(1)} %fusion.59), channel_id=1, source_target_pairs={{0,32},{4,36},{8,40},{12,44},{16,48},{20,52},{24,56},{28,60},{32,6... | collective-permute-start | bytes 104 | tf_op jit(solution)/shard_map/ppermute | solution.py:17
  113.0 19.2 %collective-permute-start.10 = (f32[8]{0:T(128)S(1)}, f32[8]{0:T(128)S(1)}, u32[]{:S(2)}, u32[]{:S(2)}) collective-permute-start(f32[8]{0:T(128)S(1)} %fusion.52), channel_id=1, source_target_pairs={{0,64},{4,68},{8,72},{12,76},{16,80},{20,84},{24,88},{28,92},{32,9... | collective-permute-start | bytes 104 | tf_op jit(solution)/shard_map/ppermute | solution.py:17
  114.5 13.6 %collective-permute-start.14 = (f32[8,64,128]{2,1,0:T(8,128)S(1)}, f32[8,64,128]{2,1,0:T(8,128)S(1)}, u32[]{:S(2)}, u32[]{:S(2)}) collective-permute-start(f32[8,64,128]{2,1,0:T(8,128)S(1)} %bitcast.158), channel_id=1, source_target_pairs={{0,8},{4,12},{8,16},{12,20},{16,24},{20,28},{24,32},{28,36},{32,40... | collective-permute-start | bytes 786440 | tf_op jit(solution)/shard_map/ppermute | solution.py:17
  120.1 11.9 %collective-permute-start.7 = (f32[8,64,128]{2,1,0:T(8,128)S(1)}, f32[8,64,128]{2,1,0:T(8,128)S(1)}, u32[]{:S(2)}, u32[]{:S(2)}) collective-permute-start(f32[8,64,128]{2,1,0:T(8,128)S(1)} %multiply_add_fusion.5), channel_id=1, source_target_pairs={{0,16},{4,20},{8,24},{12,28},{16,32},{20,36},{24,40},{28,44},{32,4... | collective-permute-start | bytes 786440 | tf_op jit(solution)/shard_map/ppermute | solution.py:17
  120.3 22.8 %collective-permute-start.18 = (f32[8]{0:T(128)S(1)}, f32[8]{0:T(128)S(1)}, u32[]{:S(2)}, u32[]{:S(2)}) collective-permute-start(f32[8]{0:T(128)S(1)} %fusion.54), channel_id=1, source_target_pairs={{0,64},{4,68},{8,72},{12,76},{16,80},{20,84},{24,88},{28,92},{32,9... | collective-permute-start | bytes 104 | tf_op jit(solution)/shard_map/ppermute | solution.py:17
  128.2 12.9 %collective-permute-start.15 = (f32[8,64,128]{2,1,0:T(8,128)S(1)}, f32[8,64,128]{2,1,0:T(8,128)S(1)}, u32[]{:S(2)}, u32[]{:S(2)}) collective-permute-start(f32[8,64,128]{2,1,0:T(8,128)S(1)} %multiply_add_fusion.2), channel_id=1, source_target_pairs={{0,16},{4,20},{8,24},{12,28},{16,32},{20,36},{24,40},{28,44},{32,4... | collective-permute-start | bytes 786440 | tf_op jit(solution)/shard_map/ppermute | solution.py:17
  132.1 9.7 %collective-permute-start.8 = (f32[8,64,128]{2,1,0:T(8,128)S(1)}, f32[8,64,128]{2,1,0:T(8,128)S(1)}, u32[]{:S(2)}, u32[]{:S(2)}) collective-permute-start(f32[8,64,128]{2,1,0:T(8,128)S(1)} %multiply_add_fusion.4), channel_id=1, source_target_pairs={{0,32},{4,36},{8,40},{12,44},{16,48},{20,52},{24,56},{28,60},{32,6... | collective-permute-start | bytes 786440 | tf_op jit(solution)/shard_map/ppermute | solution.py:17
  141.2 13.6 %collective-permute-start.16 = (f32[8,64,128]{2,1,0:T(8,128)S(1)}, f32[8,64,128]{2,1,0:T(8,128)S(1)}, u32[]{:S(2)}, u32[]{:S(2)}) collective-permute-start(f32[8,64,128]{2,1,0:T(8,128)S(1)} %multiply_add_fusion.1), channel_id=1, source_target_pairs={{0,32},{4,36},{8,40},{12,44},{16,48},{20,52},{24,56},{28,60},{32,6... | collective-permute-start | bytes 786440 | tf_op jit(solution)/shard_map/ppermute | solution.py:17
  141.9 13.3 %collective-permute-start.9 = (f32[8,64,128]{2,1,0:T(8,128)S(1)}, f32[8,64,128]{2,1,0:T(8,128)S(1)}, u32[]{:S(2)}, u32[]{:S(2)}) collective-permute-start(f32[8,64,128]{2,1,0:T(8,128)S(1)} %multiply_add_fusion.3), channel_id=1, source_target_pairs={{0,64},{4,68},{8,72},{12,76},{16,80},{20,84},{24,88},{28,92},{32,9... | collective-permute-start | bytes 786440 | tf_op jit(solution)/shard_map/ppermute | solution.py:17
  154.9 8.2 %collective-permute-start.17 = (f32[8,64,128]{2,1,0:T(8,128)S(1)}, f32[8,64,128]{2,1,0:T(8,128)S(1)}, u32[]{:S(2)}, u32[]{:S(2)}) collective-permute-start(f32[8,64,128]{2,1,0:T(8,128)S(1)} %multiply_add_fusion), channel_id=1, source_target_pairs={{0,64},{4,68},{8,72},{12,76},{16,80},{20,84},{24,88},{28,92},{32,9... | collective-permute-start | bytes 786440 | tf_op jit(solution)/shard_map/ppermute | solution.py:17
  164.6 4.3 %collective-permute-start.19 = (f32[16,64,128]{2,1,0:T(8,128)}, f32[16,64,128]{2,1,0:T(8,128)}, u32[]{:S(2)}, u32[]{:S(2)}) collective-permute-start(f32[16,64,128]{2,1,0:T(8,128)} %get-tuple-element.31), channel_id=1, source_target_pairs={{0,4},{4,0},{8,12},{12,8},{16,20},{20,16},{24,28},{28,24},{32,36},... | collective-permute-start | bytes 1572872 | tf_op jit(solution)/shard_map/ppermute | solution.py:169
  167.7 2.9 %copy-start.7 = (f32[2,16,64,128]{3,0,2,1:T(2,128)S(1)}, f32[2,16,64,128]{3,0,2,1:T(2,128)}, u32[]{:S(2)}) copy-start(f32[2,16,64,128]{3,0,2,1:T(2,128)} %get-tuple-element.56) | copy-start | bytes 3145732
  171.8 2.1 %copy-start.5 = (bf16[2,256,1024]{1,2,0:T(8,128)(2,1)S(1)}, bf16[2,256,1024]{1,2,0:T(8,128)(2,1)}, u32[]{:S(2)}) copy-start(bf16[2,256,1024]{1,2,0:T(8,128)(2,1)} %copy.84) | copy-start | bytes 3145732
  171.8 2.1 %copy-start.6 = (f32[2,256,1024]{1,2,0:T(8,128)S(1)}, f32[2,256,1024]{1,2,0:T(8,128)}, u32[]{:S(2)}) copy-start(f32[2,256,1024]{1,2,0:T(8,128)} %copy.96) | copy-start | bytes 6291460
  171.8 2.1 %copy-start.19 = (f32[16]{0:T(128)S(1)}, f32[16]{0:T(128)}, u32[]{:S(2)}) copy-start(f32[16]{0:T(128)} %param.28) | copy-start | bytes 196
  183.8 2.1 %copy-start.3 = (bf16[512,2048]{1,0:T(8,128)(2,1)S(1)}, bf16[512,2048]{1,0:T(8,128)(2,1)}, u32[]{:S(2)}) copy-start(bf16[512,2048]{1,0:T(8,128)(2,1)} %copy-done.2) | copy-start | bytes 6291460
  183.8 2.1 %copy-start.10 = (f32[1024]{0:T(1024)S(1)}, f32[1024]{0:T(1024)}, u32[]{:S(2)}) copy-start(f32[1024]{0:T(1024)} %param.29) | copy-start | bytes 12292
Sparse Core Ops, SparseCore 0:
  9.0 50.6 all-gather.1
